TPU v7x, 128 devices: a whole 4x4x4 slice. The times are simulated.
128 devices in a mesh: region: 8 (over x, core), unit: 16 (over y, z).
Axes of the slice: x: 4, y: 4, z: 4, core: 2. Of those that a mesh axis runs over, the one named last changes fastest.
Arguments:
- noisy: bfloat16 [32768, 2048], P(('region', 'unit')), may hold values from -6 to 6
- strategy: bfloat16 [2048, 2048], replicated, may hold values from -0.125 to 0.125
- county_hist: float32 [1024, 2048], P(('region', 'unit')), may hold values from -24 to 24
- tract_county: int32 [32768], P(('region', 'unit')), may hold values from 0 to 1023, as said below
- tract_owner: int32 [32768, 1], P(('region', 'unit')), may hold values from 0 to 127; in each aligned block of 256 rows (0 to 255, 256 to 511, ...) at most 4 rows name the same one
Outputs:
- released: bfloat16 [32768, 2048], P(('region', 'unit'))
- relaid: float32 [65536, 2048], P(('region', 'unit'))
Inputs may be any that keep to these rules, and one draw needn't show every extreme that they name: `tract_county`: every county has at least one tract; the tracts of region r (rows r * 256 * 16 onward) lie in counties of region r (rows r * 8 * 16 onward of county_hist). `tract_owner`: among the 256 rows of one device no owner appears more than 4 times, and some owner appears exactly 4 times.
All inputs are finite; a program needn't handle non-finite values.
Results may differ from a plain program's by a relative error of at most 0.005.
Values sent between devices are 32-bit elements; how exact they have to be, the bound alone decides.
No kernel may reach another device: no remote copies, remote signals or barrier semaphores. Data moves between devices by JAX's collectives and lax.ppermute only.
A program may use at most 64 MiB of HBM per device.

v0:
```python
import jax
import jax.numpy as jnp
from jax import lax
from jax.sharding import PartitionSpec as P

ITERS = 2


step_size = 0.25


def local(noisy, strategy, county_hist, tract_county, tract_owner):
    unit_count = lax.axis_size("unit")
    region_count = lax.axis_size("region")
    devices = region_count * unit_count
    tract_rows = noisy.shape[0]
    width = strategy.shape[0]
    county_region = county_hist.shape[0] * unit_count
    first_county = lax.axis_index("region") * county_region
    local_id = tract_county - first_county
    member = (local_id[:, None] == jnp.arange(county_region, dtype=jnp.int32)[None, :]).astype(
        jnp.float32
    )
    county_tally = jnp.sum(member, axis=0)
    estimate = jnp.zeros((tract_rows, width), jnp.float32)
    for iteration in range(ITERS):
        if iteration == 0:
            misfit = -noisy
        else:
            answers = jnp.dot(
                estimate.astype(jnp.bfloat16), strategy, preferred_element_type=jnp.float32
            )
            misfit = (answers - noisy.astype(jnp.float32)).astype(jnp.bfloat16)
        gradient = lax.dot_general(
            misfit, strategy, (((1,), (1,)), ((), ())), preferred_element_type=jnp.float32
        )
        stepped = estimate - step_size * gradient
        partial_value = lax.dot_general(
            member,
            stepped,
            (((0,), (0,)), ((), ())),
            precision=lax.Precision.HIGHEST,
            preferred_element_type=jnp.float32,
        )
        child_total, tract_count = (
            lax.psum_scatter(partial_value, "unit", scatter_dimension=0, tiled=True),
            lax.psum_scatter(county_tally, "unit", scatter_dimension=0, tiled=True),
        )
        parent_gap = (county_hist - child_total) / tract_count[:, None]
        region_gap = lax.all_gather(parent_gap, "unit", axis=0, tiled=True)
        estimate = stepped + jnp.dot(
            member, region_gap, precision=lax.Precision.HIGHEST, preferred_element_type=jnp.float32
        )
    owners = tract_owner[:, 0]
    owner_hits = (owners[:, None] == jnp.arange(devices, dtype=jnp.int32)[None, :]).astype(
        jnp.int32
    )
    slot_index = jnp.sum((jnp.cumsum(owner_hits, axis=0) - owner_hits) * owner_hits, axis=1)
    capacity = 2 * tract_rows // devices
    target = owners * capacity + slot_index
    outgoing = jnp.zeros((devices * capacity, width), jnp.float32).at[target].set(estimate)
    released = jnp.dot(
        estimate.astype(jnp.bfloat16), strategy, preferred_element_type=jnp.float32
    ).astype(jnp.bfloat16)
    grouped = outgoing.reshape(devices, capacity, width)
    arrived = lax.all_to_all(grouped, ("region", "unit"), split_axis=0, concat_axis=0, tiled=True)
    relaid = arrived.reshape(devices * capacity, width)
    return (released, relaid)


def solution(mesh):
    in_specs = (
        P(("region", "unit"), None),
        P(),
        P(("region", "unit"), None),
        P(("region", "unit")),
        P(("region", "unit"), None),
    )
    out_specs = (P(("region", "unit"), None), P(("region", "unit"), None))
    return jax.shard_map(local, mesh=mesh, in_specs=in_specs, out_specs=out_specs, check_vma=False)
```

profile of v0, /device:TPU:6, one launch (start us, length us, event | category | flops | bytes accessed | tf_op | source)
XLA Modules:
  0.0 385.6 jit_solution(13782813712799772541)
XLA Ops:
  7.2 0.0 all-reduce.6.cloned.1.call-start
  7.2 0.7 broadcast_subtract_fusion
  7.9 6.1 %fusion = f32[256,2048]{1,0:T(8,128)S(1)} fusion(bf16[2048,2048]{1,0:T(8,128)(2,1)} %param.6, bf16[256,2048]{1,0:T(8,128)(2,1)} %param.5), kind=kOutput, calls=%fused_computation.5 | convolution fusion | flops 2149056512 | bytes 11534336 | tf_op jit(solution)/shard_map/dot_general | solution.py:34
  14.0 0.0 copy-start.4
  14.0 0.0 copy-start.1
  14.0 1.9 fusion.15
  15.9 0.0 all-reduce.6.cloned.1.call-update
  15.9 0.0 all-gather.3.cloned.1.call-start
  16.0 0.0 copy-done.4
  16.0 0.6 dynamic-slice
  17.2 0.1 convert_reduce_fusion
  17.4 42.1 %all-reduce.1 = f32[128]{0:T(128)S(1)} all-reduce(f32[128]{0:T(128)S(1)} %convert_reduce_fusion), channel_id=3, replica_groups=mesh['region'=8,'unit'=16] {'unit'}, use_global_device_ids=true, to_apply=%region_2.0.clone | all-reduce | flops 128 | bytes 1024
  59.4 0.1 dynamic-slice.3
  59.5 46.5 %all-reduce.6.cloned.1.call-done = f32[128,2048]{1,0:T(8,128)} async-done(((f32[128,2048]{1,0:T(8,128)}), f32[128,2048]{1,0:T(8,128)}) %all-reduce.6.cloned.1.call-update) | async-done | bytes 1048592
  106.0 0.0 copy-done.1
  106.0 1.5 fusion.17
  107.5 0.0 all-gather.3.cloned.1.call-update
  107.5 0.0 copy-start.3
  107.5 0.0 all-reduce.8.cloned.1.call-start
  107.6 42.9 %all-gather.3.cloned.1.call-done = f32[128,2048]{1,0:T(8,128)} async-done(((f32[8,2048]{1,0:T(8,128)}), f32[128,2048]{1,0:T(8,128)}) %all-gather.3.cloned.1.call-update) | async-done | bytes 1048592 | tf_op jit(solution)/shard_map/all_gather | solution.py:50
  150.5 3.6 convolution_add_fusion.1
  154.1 0.0 copy-done.3
  154.1 11.5 %fusion.1 = f32[256,2048]{1,0:T(8,128)S(1)} fusion(f32[256,2048]{1,0:T(8,128)} %convolution_add_fusion.1, bf16[2048,2048]{1,0:T(8,128)(2,1)} %param.6, bf16[256,2048]{1,0:T(8,128)(2,1)S(1)} %copy-done.3), kind=kOutput, calls=%fused_computation.6 | convolution fusion | flops 4298113024 | bytes 13631488 | tf_op jit(solution)/shard_map/dot_general | solution.py:34
  165.6 0.0 copy-start.2
  165.6 1.9 fusion.14
  167.5 0.0 all-reduce.8.cloned.1.call-update
  167.5 0.2 all-gather.5.cloned.1.call-start
  167.7 86.7 %all-reduce.8.cloned.1.call-done = f32[128,2048]{1,0:T(8,128)} async-done(((f32[128,2048]{1,0:T(8,128)}), f32[128,2048]{1,0:T(8,128)}) %all-reduce.8.cloned.1.call-update) | async-done | bytes 1048592
  254.4 1.5 fusion.16
  255.9 0.0 all-gather.5.cloned.1.call-update
  256.0 0.0 copy-done.2
  256.0 0.1 copy.12
  256.1 0.2 fusion.10
  256.4 0.2 fusion.12
  256.6 42.2 %all-gather.5.cloned.1.call-done = f32[128,2048]{1,0:T(8,128)} async-done(((f32[8,2048]{1,0:T(8,128)}), f32[128,2048]{1,0:T(8,128)}) %all-gather.5.cloned.1.call-update) | async-done | bytes 1048592 | tf_op jit(solution)/shard_map/all_gather | solution.py:50
  298.8 3.6 convolution_add_fusion
  302.4 5.1 %scatter_custom_fusion = f32[512,2048]{1,0:T(8,128)} fusion(s32[256]{0:T(256)S(1)} %bitcast.33, f32[256,2048]{1,0:T(8,128)} %convolution_add_fusion, f32[]{:T(128)} %constant.8.clone.1), kind=kCustom, calls=%fused_computation.10 | custom fusion | bytes 4194816 | tf_op jit(solution)/shard_map/scatter | solution.py:61
  307.6 5.2 %reshape.30 = f32[128,4,2048]{2,1,0:T(4,128)} reshape(f32[512,2048]{1,0:T(8,128)} %scatter_custom_fusion) | data formatting | bytes 8388608 | tf_op jit(solution)/shard_map/reshape | solution.py:65
  312.7 0.0 copy-start
  312.7 7.8 %all-to-all-start = ((f32[128,4,2048]{2,1,0:T(4,128)}), f32[128,4,2048]{2,1,0:T(4,128)}, u32[]{:S(2)}, u32[]{:S(2)}) async-start(f32[128,4,2048]{2,1,0:T(4,128)} %reshape.30), calls=%async_computation | async-start | bytes 8388608 | tf_op jit(solution)/shard_map/all_to_all | solution.py:66
  320.6 0.0 copy-done
  320.6 6.7 %convolution_convert_fusion = bf16[256,2048]{1,0:T(8,128)(2,1)} fusion(bf16[2048,2048]{1,0:T(8,128)(2,1)} %param.6, f32[256,2048]{1,0:T(8,128)S(1)} %copy-done), kind=kOutput, calls=%fused_computation.9 | convolution fusion | flops 2148532224 | bytes 11534336 | tf_op jit(solution)/shard_map/dot_general | solution.py:62
  327.3 46.5 %all-to-all-done = f32[128,4,2048]{2,1,0:T(4,128)} async-done(((f32[128,4,2048]{2,1,0:T(4,128)}), f32[128,4,2048]{2,1,0:T(4,128)}, u32[]{:S(2)}, u32[]{:S(2)}) %all-to-all-start) | async-done | bytes 4194336 | tf_op jit(solution)/shard_map/all_to_all | solution.py:66
  373.8 5.3 %reshape.31 = f32[512,2048]{1,0:T(8,128)} reshape(f32[128,4,2048]{2,1,0:T(4,128)} %all-to-all-done) | data formatting | bytes 8388608 | tf_op jit(solution)/shard_map/reshape | solution.py:67
  (7 shorter events, 0.1 us)
Async XLA Ops:
  7.2 98.8 %all-reduce.6.cloned.1.call-start = ((), (), s32[]{:S(2)}) async-start(), calls=%async_computation.3 | async-start | bytes 2097152
  14.0 2.0 copy-start.4
  14.0 92.0 %copy-start.1 = (f32[8,2048]{1,0:T(8,128)S(1)}, f32[8,2048]{1,0:T(8,128)}, u32[]{:S(2)}) copy-start(f32[8,2048]{1,0:T(8,128)} %param.7) | copy-start | bytes 196612
  15.9 134.5 %all-gather.3.cloned.1.call-start = ((), (), s32[]{:S(2)}) async-start(), calls=%async_computation.1 | async-start | bytes 1114112 | tf_op jit(solution)/shard_map/all_gather | solution.py:50
  107.5 46.5 %copy-start.3 = (bf16[256,2048]{1,0:T(8,128)(2,1)S(1)}, bf16[256,2048]{1,0:T(8,128)(2,1)}, u32[]{:S(2)}) copy-start(bf16[256,2048]{1,0:T(8,128)(2,1)} %param.5) | copy-start | bytes 3145732
  107.5 146.9 %all-reduce.8.cloned.1.call-start = ((), (), s32[]{:S(2)}) async-start(), calls=%async_computation.4 | async-start | bytes 2097152
  165.6 90.4 %copy-start.2 = (s32[256,1]{0,1:T(1,128)S(1)}, s32[256,1]{0,1:T(1,128)}, u32[]{:S(2)}) copy-start(s32[256,1]{0,1:T(1,128)} %param.9) | copy-start | bytes 3076
  167.5 131.3 %all-gather.5.cloned.1.call-start = ((), (), s32[]{:S(2)}) async-start(), calls=%async_computation.2 | async-start | bytes 1114112 | tf_op jit(solution)/shard_map/all_gather | solution.py:50
  312.7 7.9 %copy-start = (f32[256,2048]{1,0:T(8,128)S(1)}, f32[256,2048]{1,0:T(8,128)}, u32[]{:S(2)}) copy-start(f32[256,2048]{1,0:T(8,128)} %convolution_add_fusion) | copy-start | bytes 6291460
  312.7 61.1 %all-to-all-start = ((f32[128,4,2048]{2,1,0:T(4,128)}), f32[128,4,2048]{2,1,0:T(4,128)}, u32[]{:S(2)}, u32[]{:S(2)}) async-start(f32[128,4,2048]{2,1,0:T(4,128)} %reshape.30), calls=%async_computation | async-start | bytes 8388608 | tf_op jit(solution)/shard_map/all_to_all | solution.py:66
Sparse Core Ops, SparseCore 0:
  16.1 89.8 all-reduce.5
  108.7 41.7 all-gather.2
  167.6 86.7 all-reduce.7
  257.0 41.7 all-gather.4
where the time goes:
time: 386 us
  waiting for transfers between devices  265 us (69%)
  blocking collectives  42.1 us (11%)
  matrix products  35.3 us (9%)
  local copies, waits for them, and re-layouts  16.4 us (4%)
  between operations  14.5 us (4%)
  starting transfers between devices  8.19 us (2%)
  other arithmetic  4.33 us (1%)
    unnamed x6, waiting for transfers between devices  133 us
    all_gather x2, waiting for transfers between devices, local(): region_gap = lax.all_gather(parent_gap, 'unit', axis=0, tiled=True)  85.1 us
    all_to_all x1, waiting for transfers between devices, local(): lax.all_to_all(grouped, ('region', 'unit'), split_axis=0, concat_axis=0,...  46.5 us
    unnamed x1, blocking collectives  42.1 us
    dot_general x2, matrix products, local(): lax.dot_general(misfit, strategy, (((1,), (1,)), ((), ())), preferred_ele...  17.6 us
    all_to_all x1, starting transfers between devices, local(): lax.all_to_all(grouped, ('region', 'unit'), split_axis=0, concat_axis=0,...  7.85 us
  transfers between devices with their start and end apart: 5, of which 5 were waited for; matrix products, arithmetic and copies ran while one was open for 2% of the time, Pallas kernels for 0%

commit v1 on v0

--- a/solution.py
+++ b/solution.py
@@ -7,6 +7,19 @@
 
 
 step_size = 0.25
+
+
+def unit_sum(partial, unit_count):
+    rows, cols = partial.shape
+    grouped = partial.reshape(unit_count, rows // unit_count, cols)
+    arrived = lax.all_to_all(grouped, "unit", 0, 0, tiled=True)
+    return jnp.sum(arrived, axis=0)
+
+
+def unit_gather(block, unit_count):
+    spread = jnp.broadcast_to(block[None], (unit_count,) + block.shape)
+    arrived = lax.all_to_all(spread, "unit", 0, 0, tiled=True)
+    return arrived.reshape(unit_count * block.shape[0], block.shape[1])
 
 
 def local(noisy, strategy, county_hist, tract_county, tract_owner):
@@ -22,7 +35,9 @@
         jnp.float32
     )
     county_tally = jnp.sum(member, axis=0)
+    tally_lanes = 128
     estimate = jnp.zeros((tract_rows, width), jnp.float32)
+    tract_count = None
     for iteration in range(ITERS):
         if iteration == 0:
             misfit = -noisy
@@ -42,12 +57,15 @@
             precision=lax.Precision.HIGHEST,
             preferred_element_type=jnp.float32,
         )
-        child_total, tract_count = (
-            lax.psum_scatter(partial_value, "unit", scatter_dimension=0, tiled=True),
-            lax.psum_scatter(county_tally, "unit", scatter_dimension=0, tiled=True),
-        )
+        if tract_count is None:
+            tally = jnp.broadcast_to(county_tally[:, None], (county_region, tally_lanes))
+            summed = unit_sum(jnp.concatenate([partial_value, tally], axis=1), unit_count)
+            child_total = summed[:, :width]
+            tract_count = summed[:, width]
+        else:
+            child_total = unit_sum(partial_value, unit_count)
         parent_gap = (county_hist - child_total) / tract_count[:, None]
-        region_gap = lax.all_gather(parent_gap, "unit", axis=0, tiled=True)
+        region_gap = unit_gather(parent_gap, unit_count)
         estimate = stepped + jnp.dot(
             member, region_gap, precision=lax.Precision.HIGHEST, preferred_element_type=jnp.float32
         )

time: 386 us -> 188 us (0.49)
  waiting for transfers between devices: 265 us -> 76.5 us
  between operations: 14.5 us -> 0.77 us
  starting transfers between devices: 8.19 us -> 13.9 us
    unnamed x6 -> x0, waiting for transfers between devices: 133 us -> none
    all_gather x2 -> x0, waiting for transfers between devices: 85.1 us -> none  [local(): region_gap = lax.all_gather(parent_gap, 'unit', axis=0, tiled=True)]
    all_to_all x0 -> x2, blocking collectives: none -> 45.1 us  [the longest x1 25.9 us: unit_sum(): arrived = lax.all_to_all(grouped, 'unit', 0, 0, tiled=True)]
    unnamed x1 -> x0, blocking collectives: 42.1 us -> none
    all_to_all x0 -> x2, waiting for transfers between devices: none -> 30 us  [the longest x1 15.1 us: unit_gather(): arrived = lax.all_to_all(spread, 'unit', 0, 0, tiled=True)]
    all_to_all x0 -> x2, starting transfers between devices: none -> 7.49 us  [the longest x1 3.84 us: unit_gather(): arrived = lax.all_to_all(spread, 'unit', 0, 0, tiled=True)]
  transfers between devices with their start and end apart: 5 -> 3, of which waited for: 5 -> 3; matrix products, arithmetic and copies ran while one was open for 2% -> 4% of each run, Pallas kernels for 0% -> 0%
where the time goes in v1:
time: 188 us; the launch traced here: 187 us
  waiting for transfers between devices  76.5 us (41%)
  blocking collectives  45.1 us (24%)
  matrix products  31.9 us (17%)
  local copies, waits for them, and re-layouts  17.1 us (9%)
  starting transfers between devices  13.9 us (7%)
    all_to_all x1, waiting for transfers between devices, local(): lax.all_to_all(grouped, ('region', 'unit'), split_axis=0, concat_axis=0,...  46.5 us
    all_to_all x1, blocking collectives, unit_sum(): arrived = lax.all_to_all(grouped, 'unit', 0, 0, tiled=True)  25.9 us
    all_to_all x1, blocking collectives, unit_gather(): arrived = lax.all_to_all(spread, 'unit', 0, 0, tiled=True)  19.2 us
    dot_general x2, matrix products, local(): lax.dot_general(misfit, strategy, (((1,), (1,)), ((), ())), preferred_ele...  17.6 us
    all_to_all x1, waiting for transfers between devices, unit_gather(): arrived = lax.all_to_all(spread, 'unit', 0, 0, tiled=True)  15.1 us
    all_to_all x1, waiting for transfers between devices, unit_sum(): arrived = lax.all_to_all(grouped, 'unit', 0, 0, tiled=True)  14.9 us
    dot_general x1, matrix products, local(): jnp.dot(estimate.astype(jnp.bfloat16), strategy, preferred_element_type=j...  6.68 us
    all_to_all x1, starting transfers between devices, local(): lax.all_to_all(grouped, ('region', 'unit'), split_axis=0, concat_axis=0,...  6.44 us
  transfers between devices with their start and end apart: 3, of which 3 were waited for; matrix products, arithmetic and copies ran while one was open for 4% of the time, Pallas kernels for 0%

profile of v1, /device:TPU:6, one launch (start us, length us, event | category | flops | bytes accessed | tf_op | source)
XLA Modules:
  0.0 187.0 jit_solution(3604792390932002105)
XLA Ops:
  0.6 0.7 broadcast_subtract_fusion
  1.3 0.1 convert_reduce_fusion
  1.4 6.1 %fusion = f32[256,2048]{1,0:T(8,128)S(1)} fusion(bf16[2048,2048]{1,0:T(8,128)(2,1)} %param.6, bf16[256,2048]{1,0:T(8,128)(2,1)} %param.5), kind=kOutput, calls=%fused_computation.5 | convolution fusion | flops 2149056512 | bytes 11534336 | tf_op jit(solution)/shard_map/dot_general | solution.py:49
  7.5 0.9 fusion.16
  8.5 0.1 broadcast_in_dim.11
  8.5 0.1 maximum_bitcast_fusion
  8.6 0.0 copy-start.1
  8.7 25.9 %all_to_all.25 = f32[16,8,2176]{2,1,0:T(8,128)S(1)} all-to-all(f32[16,8,2176]{2,1,0:T(8,128)S(1)} %maximum_bitcast_fusion), channel_id=1, replica_groups=mesh['region'=8,'unit'=16] {'unit'}, dimensions={0} | all-to-all | bytes 2228224 | tf_op jit(solution)/shard_map/all_to_all | solution.py:15
  34.6 0.1 reduce_sum.39
  34.6 0.1 slice_reduce_fusion
  34.7 0.0 copy-done.1
  34.7 0.1 fusion.17
  34.8 0.1 broadcast_in_dim.12
  34.9 19.2 %all_to_all.26 = f32[16,8,2048]{2,1,0:T(8,128)S(1)} all-to-all(f32[16,8,2048]{2,1,0:T(8,128)S(1)} %broadcast_in_dim.12), channel_id=1, replica_groups=mesh['region'=8,'unit'=16] {'unit'}, dimensions={0} | all-to-all | bytes 2097152 | tf_op jit(solution)/shard_map/all_to_all | solution.py:21
  54.2 0.0 copy-start.3
  54.2 2.4 %convolution_add_fusion.1 = f32[256,2048]{1,0:T(8,128)} fusion(f32[256,2048]{1,0:T(8,128)S(1)} %fusion, f32[16,8,2048]{2,1,0:T(8,128)S(1)} %all_to_all.26, s32[256]{0:T(256)S(1)} %broadcast_subtract_fusion), kind=kOutput, calls=%fused_computation.4 | convolution fusion | flops 805863424 | bytes 5243904 | tf_op jit(solution)/shard_map/dot_general | solution.py:69
  56.5 0.0 copy-done.3
  56.5 11.5 %fusion.1 = f32[256,2048]{1,0:T(8,128)S(1)} fusion(f32[256,2048]{1,0:T(8,128)} %convolution_add_fusion.1, bf16[2048,2048]{1,0:T(8,128)(2,1)} %param.6, bf16[256,2048]{1,0:T(8,128)(2,1)S(1)} %copy-done.3), kind=kOutput, calls=%fused_computation.6 | convolution fusion | flops 4298113024 | bytes 13631488 | tf_op jit(solution)/shard_map/dot_general | solution.py:49
  68.0 0.0 copy-start.2
  68.0 1.9 %convolution_bitcast_fusion = f32[16,8,2048]{2,1,0:T(8,128)} fusion(f32[256,2048]{1,0:T(8,128)S(1)} %fusion.1, s32[256]{0:T(256)S(1)} %broadcast_subtract_fusion), kind=kOutput, calls=%fused_computation.10 | convolution fusion | flops 805339136 | bytes 3146752 | tf_op jit(solution)/shard_map/dot_general | solution.py:53
  69.9 3.7 %all-to-all-start.2 = ((f32[16,8,2048]{2,1,0:T(8,128)}), f32[16,8,2048]{2,1,0:T(8,128)S(1)}, u32[]{:S(2)}, u32[]{:S(2)}) async-start(f32[16,8,2048]{2,1,0:T(8,128)} %convolution_bitcast_fusion), calls=%async_computation.2 | async-start | bytes 2097152 | tf_op jit(solution)/shard_map/all_to_all | solution.py:15
  73.6 0.0 copy-done.2
  73.6 0.1 copy.10
  73.7 14.9 %all-to-all-done.2 = f32[16,8,2048]{2,1,0:T(8,128)S(1)} async-done(((f32[16,8,2048]{2,1,0:T(8,128)}), f32[16,8,2048]{2,1,0:T(8,128)S(1)}, u32[]{:S(2)}, u32[]{:S(2)}) %all-to-all-start.2) | async-done | bytes 1048608 | tf_op jit(solution)/shard_map/all_to_all | solution.py:15
  88.6 0.1 reduce_sum.40
  88.7 0.1 subtract_divide_fusion
  88.8 1.1 broadcast_in_dim.13
  89.9 3.8 %all-to-all-start.3 = ((f32[16,8,2048]{2,1,0:T(8,128)}), f32[16,8,2048]{2,1,0:T(8,128)S(1)}, u32[]{:S(2)}, u32[]{:S(2)}) async-start(f32[16,8,2048]{2,1,0:T(8,128)} %broadcast_in_dim.13), calls=%async_computation.3 | async-start | bytes 2097152 | tf_op jit(solution)/shard_map/all_to_all | solution.py:21
  93.7 0.2 fusion.12
  94.0 0.2 fusion.14
  94.2 15.1 %all-to-all-done.3 = f32[16,8,2048]{2,1,0:T(8,128)S(1)} async-done(((f32[16,8,2048]{2,1,0:T(8,128)}), f32[16,8,2048]{2,1,0:T(8,128)S(1)}, u32[]{:S(2)}, u32[]{:S(2)}) %all-to-all-start.3) | async-done | bytes 1048608 | tf_op jit(solution)/shard_map/all_to_all | solution.py:21
  109.3 2.4 %convolution_add_fusion = f32[256,2048]{1,0:T(8,128)} fusion(f32[256,2048]{1,0:T(8,128)S(1)} %fusion.1, f32[16,8,2048]{2,1,0:T(8,128)S(1)} %all-to-all-done.3, s32[256]{0:T(256)S(1)} %broadcast_subtract_fusion), kind=kOutput, calls=%fused_computation.3 | convolution fusion | flops 805863424 | bytes 5243904 | tf_op jit(solution)/shard_map/dot_general | solution.py:69
  111.7 5.1 %scatter_custom_fusion = f32[512,2048]{1,0:T(8,128)} fusion(s32[256]{0:T(256)S(1)} %bitcast.40, f32[256,2048]{1,0:T(8,128)} %convolution_add_fusion, f32[]{:T(128)} %constant.8.clone.1), kind=kCustom, calls=%fused_computation.11 | custom fusion | bytes 4194816 | tf_op jit(solution)/shard_map/scatter | solution.py:79
  116.8 5.2 %reshape.48 = f32[128,4,2048]{2,1,0:T(4,128)} reshape(f32[512,2048]{1,0:T(8,128)} %scatter_custom_fusion) | data formatting | bytes 8388608 | tf_op jit(solution)/shard_map/reshape | solution.py:83
  122.0 0.0 copy-start
  122.0 6.4 %all-to-all-start.4 = ((f32[128,4,2048]{2,1,0:T(4,128)}), f32[128,4,2048]{2,1,0:T(4,128)}, u32[]{:S(2)}, u32[]{:S(2)}) async-start(f32[128,4,2048]{2,1,0:T(4,128)} %reshape.48), calls=%async_computation.4 | async-start | bytes 8388608 | tf_op jit(solution)/shard_map/all_to_all | solution.py:84
  128.4 0.0 copy-done
  128.5 6.7 %convolution_convert_fusion = bf16[256,2048]{1,0:T(8,128)(2,1)} fusion(bf16[2048,2048]{1,0:T(8,128)(2,1)} %param.6, f32[256,2048]{1,0:T(8,128)S(1)} %copy-done), kind=kOutput, calls=%fused_computation.9 | convolution fusion | flops 2148532224 | bytes 11534336 | tf_op jit(solution)/shard_map/dot_general | solution.py:80
  135.1 46.5 %all-to-all-done.4 = f32[128,4,2048]{2,1,0:T(4,128)} async-done(((f32[128,4,2048]{2,1,0:T(4,128)}), f32[128,4,2048]{2,1,0:T(4,128)}, u32[]{:S(2)}, u32[]{:S(2)}) %all-to-all-start.4) | async-done | bytes 4194336 | tf_op jit(solution)/shard_map/all_to_all | solution.py:84
  181.7 5.3 %reshape.49 = f32[512,2048]{1,0:T(8,128)} reshape(f32[128,4,2048]{2,1,0:T(4,128)} %all-to-all-done.4) | data formatting | bytes 8388608 | tf_op jit(solution)/shard_map/reshape | solution.py:85
  (7 shorter events, 0.1 us)
Async XLA Ops:
  8.6 26.1 %copy-start.1 = (f32[8,2048]{1,0:T(8,128)S(1)}, f32[8,2048]{1,0:T(8,128)}, u32[]{:S(2)}) copy-start(f32[8,2048]{1,0:T(8,128)} %param.7) | copy-start | bytes 196612
  54.2 2.4 %copy-start.3 = (bf16[256,2048]{1,0:T(8,128)(2,1)S(1)}, bf16[256,2048]{1,0:T(8,128)(2,1)}, u32[]{:S(2)}) copy-start(bf16[256,2048]{1,0:T(8,128)(2,1)} %param.5) | copy-start | bytes 3145732
  68.0 5.6 %copy-start.2 = (s32[256,1]{0,1:T(1,128)S(1)}, s32[256,1]{0,1:T(1,128)}, u32[]{:S(2)}) copy-start(s32[256,1]{0,1:T(1,128)} %param.9) | copy-start | bytes 3076
  69.9 18.7 %all-to-all-start.2 = ((f32[16,8,2048]{2,1,0:T(8,128)}), f32[16,8,2048]{2,1,0:T(8,128)S(1)}, u32[]{:S(2)}, u32[]{:S(2)}) async-start(f32[16,8,2048]{2,1,0:T(8,128)} %convolution_bitcast_fusion), calls=%async_computation.2 | async-start | bytes 2097152 | tf_op jit(solution)/shard_map/all_to_all | solution.py:15
  89.9 19.4 %all-to-all-start.3 = ((f32[16,8,2048]{2,1,0:T(8,128)}), f32[16,8,2048]{2,1,0:T(8,128)S(1)}, u32[]{:S(2)}, u32[]{:S(2)}) async-start(f32[16,8,2048]{2,1,0:T(8,128)} %broadcast_in_dim.13), calls=%async_computation.3 | async-start | bytes 2097152 | tf_op jit(solution)/shard_map/all_to_all | solution.py:21
  122.0 6.4 %copy-start = (f32[256,2048]{1,0:T(8,128)S(1)}, f32[256,2048]{1,0:T(8,128)}, u32[]{:S(2)}) copy-start(f32[256,2048]{1,0:T(8,128)} %convolution_add_fusion) | copy-start | bytes 6291460
  122.0 59.7 %all-to-all-start.4 = ((f32[128,4,2048]{2,1,0:T(4,128)}), f32[128,4,2048]{2,1,0:T(4,128)}, u32[]{:S(2)}, u32[]{:S(2)}) async-start(f32[128,4,2048]{2,1,0:T(4,128)} %reshape.48), calls=%async_computation.4 | async-start | bytes 8388608 | tf_op jit(solution)/shard_map/all_to_all | solution.py:84

commit v2 on v1

--- a/solution.py
+++ b/solution.py
@@ -66,22 +66,20 @@
             child_total = unit_sum(partial_value, unit_count)
         parent_gap = (county_hist - child_total) / tract_count[:, None]
         region_gap = unit_gather(parent_gap, unit_count)
-        estimate = stepped + jnp.dot(
-            member, region_gap, precision=lax.Precision.HIGHEST, preferred_element_type=jnp.float32
-        )
+        estimate = stepped + jnp.take(region_gap, local_id, axis=0)
     owners = tract_owner[:, 0]
     owner_hits = (owners[:, None] == jnp.arange(devices, dtype=jnp.int32)[None, :]).astype(
         jnp.int32
     )
     slot_index = jnp.sum((jnp.cumsum(owner_hits, axis=0) - owner_hits) * owner_hits, axis=1)
     capacity = 2 * tract_rows // devices
-    target = owners * capacity + slot_index
-    outgoing = jnp.zeros((devices * capacity, width), jnp.float32).at[target].set(estimate)
+    outgoing = jnp.zeros((devices, capacity, width), jnp.float32).at[owners, slot_index].set(
+        estimate
+    )
     released = jnp.dot(
         estimate.astype(jnp.bfloat16), strategy, preferred_element_type=jnp.float32
     ).astype(jnp.bfloat16)
-    grouped = outgoing.reshape(devices, capacity, width)
-    arrived = lax.all_to_all(grouped, ("region", "unit"), split_axis=0, concat_axis=0, tiled=True)
+    arrived = lax.all_to_all(outgoing, ("region", "unit"), split_axis=0, concat_axis=0, tiled=True)
     relaid = arrived.reshape(devices * capacity, width)
     return (released, relaid)
 

time: 188 us -> 229 us (1.22)
  local copies, waits for them, and re-layouts: 17.1 us -> 56.8 us
  blocking collectives: 45.1 us -> 25.9 us
  waiting for transfers between devices: 76.5 us -> 93 us
  starting transfers between devices: 13.9 us -> 17.6 us
  matrix products: 31.9 us -> 28.8 us
  other arithmetic: 1.6 us -> 4.1 us
    scatter x1, local copies, waits for them, and re-layouts: 5.12 us -> 40.3 us  [local(): jnp.zeros((devices, capacity, width), jnp.float32).at[owners, slot_index]]
    all_to_all x1 -> x0, blocking collectives: 19.2 us -> none  [unit_gather(): arrived = lax.all_to_all(spread, 'unit', 0, 0, tiled=True)]
    all_to_all x1 -> x2, waiting for transfers between devices: 15.1 us -> 31 us  [unit_gather(): arrived = lax.all_to_all(spread, 'unit', 0, 0, tiled=True)]
    gather x0 -> x2, local copies, waits for them, and re-layouts: none -> 5.42 us  [local(): estimate = stepped + jnp.take(region_gap, local_id, axis=0)]
    reshape x1 -> x0, local copies, waits for them, and re-layouts: 5.16 us -> none  [local(): grouped = outgoing.reshape(devices, capacity, width)]
    dot_general x2 -> x0, matrix products: 4.79 us -> none  [local(): jnp.dot(member, region_gap, precision=lax.Precision.HIGHEST, preferred_el...]
    all_to_all x1 -> x2, starting transfers between devices: 3.84 us -> 7.49 us  [unit_gather(): arrived = lax.all_to_all(spread, 'unit', 0, 0, tiled=True)]
    broadcast_in_dim x0 -> x1, local copies, waits for them, and re-layouts: none -> 3.07 us  [local(): jnp.zeros((devices, capacity, width), jnp.float32).at[owners, slot_index]]
  transfers between devices with their start and end apart: 3 -> 4, of which waited for: 3 -> 4; matrix products, arithmetic and copies ran while one was open for 4% -> 3% of each run, Pallas kernels for 0% -> 0%
where the time goes in v2:
time: 229 us; the launch traced here: 227 us
  waiting for transfers between devices  93 us (41%)
  local copies, waits for them, and re-layouts  56.8 us (25%)
  matrix products  28.8 us (13%)
  blocking collectives  25.9 us (11%)
  starting transfers between devices  17.6 us (8%)
  other arithmetic  4.1 us (2%)
    all_to_all x1, waiting for transfers between devices, local(): lax.all_to_all(outgoing, ('region', 'unit'), split_axis=0, concat_axis=0,...  46.5 us
    scatter x1, local copies, waits for them, and re-layouts, local(): jnp.zeros((devices, capacity, width), jnp.float32).at[owners, slot_index]  40.3 us
    all_to_all x2, waiting for transfers between devices, unit_gather(): arrived = lax.all_to_all(spread, 'unit', 0, 0, tiled=True)  31 us
    all_to_all x1, blocking collectives, unit_sum(): arrived = lax.all_to_all(grouped, 'unit', 0, 0, tiled=True)  25.9 us
    dot_general x2, matrix products, local(): lax.dot_general(misfit, strategy, (((1,), (1,)), ((), ())), preferred_ele...  19.3 us
    all_to_all x1, waiting for transfers between devices, unit_sum(): arrived = lax.all_to_all(grouped, 'unit', 0, 0, tiled=True)  15.5 us
    all_to_all x2, starting transfers between devices, unit_gather(): arrived = lax.all_to_all(spread, 'unit', 0, 0, tiled=True)  7.49 us
    dot_general x1, matrix products, local(): jnp.dot(estimate.astype(jnp.bfloat16), strategy, preferred_element_type=j...  6.68 us
  transfers between devices with their start and end apart: 4, of which 4 were waited for; matrix products, arithmetic and copies ran while one was open for 3% of the time, Pallas kernels for 0%

profile of v2, /device:TPU:6, one launch (start us, length us, event | category | flops | bytes accessed | tf_op | source)
XLA Modules:
  0.0 227.0 jit_solution(16957211454359822149)
XLA Ops:
  0.6 0.7 compare_and_fusion
  1.3 0.1 convert_reduce_fusion
  1.4 6.1 %fusion = f32[256,2048]{1,0:T(8,128)S(1)} fusion(bf16[2048,2048]{1,0:T(8,128)(2,1)} %param.8, bf16[256,2048]{1,0:T(8,128)(2,1)} %param.7), kind=kOutput, calls=%fused_computation.5 | convolution fusion | flops 2149056512 | bytes 11534336 | tf_op jit(solution)/shard_map/dot_general | solution.py:49
  7.5 0.0 copy-start.1
  7.5 0.9 fusion.12
  8.5 0.1 broadcast_in_dim.20
  8.6 0.1 maximum_bitcast_fusion
  8.6 0.2 copy-done.1
  8.8 0.0 copy-start.2
  8.8 25.9 %all_to_all.25 = f32[16,8,2176]{2,1,0:T(8,128)S(1)} all-to-all(f32[16,8,2176]{2,1,0:T(8,128)S(1)} %maximum_bitcast_fusion), channel_id=1, replica_groups=mesh['region'=8,'unit'=16] {'unit'}, dimensions={0} | all-to-all | bytes 2228224 | tf_op jit(solution)/shard_map/all_to_all | solution.py:15
  34.8 0.1 reduce_sum.39
  34.8 0.1 slice_reduce_fusion
  34.9 0.0 copy-done.2
  34.9 0.1 fusion.13
  35.0 1.1 broadcast_in_dim.21
  36.1 3.7 %all-to-all-start.1 = ((f32[16,8,2048]{2,1,0:T(8,128)}), f32[16,8,2048]{2,1,0:T(8,128)S(1)}, u32[]{:S(2)}, u32[]{:S(2)}) async-start(f32[16,8,2048]{2,1,0:T(8,128)} %broadcast_in_dim.21), calls=%async_computation.1 | async-start | bytes 2097152 | tf_op jit(solution)/shard_map/all_to_all | solution.py:21
  39.8 16.0 %all-to-all-done.1 = f32[16,8,2048]{2,1,0:T(8,128)S(1)} async-done(((f32[16,8,2048]{2,1,0:T(8,128)}), f32[16,8,2048]{2,1,0:T(8,128)S(1)}, u32[]{:S(2)}, u32[]{:S(2)}) %all-to-all-start.1) | async-done | bytes 1048608 | tf_op jit(solution)/shard_map/all_to_all | solution.py:21
  55.8 2.7 %gather_fusion = f32[256,2048]{1,0:T(8,128)} fusion(f32[128,2048]{1,0:T(8,128)S(1)} %bitcast.30, s32[1024]{0:T(1024)S(1)} %pad_clamp_fusion), kind=kCustom, calls=%fused_computation.clone | custom fusion | bytes 4195328 | tf_op jit(solution)/shard_map/jit(_take)/gather | solution.py:69
  58.5 13.2 %fusion.1 = f32[256,2048]{1,0:T(8,128)S(1)} fusion(bf16[2048,2048]{1,0:T(8,128)(2,1)} %param.8, bf16[256,2048]{1,0:T(8,128)(2,1)} %param.7, f32[256,2048]{1,0:T(8,128)} %copy-done.1, f32[256,2048]{1,0:T(8,128)} %gather_fusion, pred[256]{0:T(512)(128)(4,1)S(1)} %get-tuple-element.3), kind=kOutput, calls=%fused_computation.6 | convolution fusion | flops 4300210176 | bytes 15728896 | tf_op jit(solution)/shard_map/dot_general | solution.py:49
  71.7 0.0 copy-start
  71.7 0.0 copy-start.3
  71.7 1.9 convolution_bitcast_fusion
  73.6 0.0 copy-done
  73.6 3.7 %all-to-all-start.2 = ((f32[16,8,2048]{2,1,0:T(8,128)}), f32[16,8,2048]{2,1,0:T(8,128)S(1)}, u32[]{:S(2)}, u32[]{:S(2)}) async-start(f32[16,8,2048]{2,1,0:T(8,128)} %convolution_bitcast_fusion), calls=%async_computation.2 | async-start | bytes 2097152 | tf_op jit(solution)/shard_map/all_to_all | solution.py:15
  77.3 0.0 copy-done.3
  77.3 0.1 copy.10
  77.4 15.5 %all-to-all-done.2 = f32[16,8,2048]{2,1,0:T(8,128)S(1)} async-done(((f32[16,8,2048]{2,1,0:T(8,128)}), f32[16,8,2048]{2,1,0:T(8,128)S(1)}, u32[]{:S(2)}, u32[]{:S(2)}) %all-to-all-start.2) | async-done | bytes 1048608 | tf_op jit(solution)/shard_map/all_to_all | solution.py:15
  92.9 0.1 reduce_sum.40
  92.9 0.1 subtract_divide_fusion
  93.0 1.1 broadcast_in_dim.22
  94.1 3.8 %all-to-all-start.3 = ((f32[16,8,2048]{2,1,0:T(8,128)}), f32[16,8,2048]{2,1,0:T(8,128)S(1)}, u32[]{:S(2)}, u32[]{:S(2)}) async-start(f32[16,8,2048]{2,1,0:T(8,128)} %broadcast_in_dim.22), calls=%async_computation.3 | async-start | bytes 2097152 | tf_op jit(solution)/shard_map/all_to_all | solution.py:21
  97.9 0.2 fusion.8
  98.2 0.2 fusion.10
  98.4 15.0 %all-to-all-done.3 = f32[16,8,2048]{2,1,0:T(8,128)S(1)} async-done(((f32[16,8,2048]{2,1,0:T(8,128)}), f32[16,8,2048]{2,1,0:T(8,128)S(1)}, u32[]{:S(2)}, u32[]{:S(2)}) %all-to-all-start.3) | async-done | bytes 1048608 | tf_op jit(solution)/shard_map/all_to_all | solution.py:21
  113.5 2.7 %gather_fusion.1 = f32[256,2048]{1,0:T(8,128)} fusion(f32[128,2048]{1,0:T(8,128)S(1)} %bitcast.29, s32[1024]{0:T(1024)S(1)} %pad_clamp_fusion), kind=kCustom, calls=%fused_computation.1.clone | custom fusion | bytes 4195328 | tf_op jit(solution)/shard_map/jit(_take)/gather | solution.py:69
  116.2 2.5 %select_add_fusion = f32[256,2048]{1,0:T(8,128)S(1)} fusion(f32[256,2048]{1,0:T(8,128)} %copy-done, f32[256,2048]{1,0:T(8,128)} %gather_fusion.1, pred[256]{0:T(512)(128)(4,1)S(1)} %get-tuple-element.3), kind=kLoop, calls=%fused_computation.11 | loop fusion | flops 1048576 | bytes 6291712 | tf_op jit(solution)/shard_map/add | solution.py:69
  118.7 3.1 %broadcast_in_dim.23 = f32[128,4,2048]{2,1,0:T(4,128)} broadcast(f32[]{:T(128)} %constant.15.clone.1), dimensions={} | broadcast | bytes 4194308 | tf_op jit(solution)/shard_map/broadcast_in_dim | solution.py:76
  121.7 40.3 %scatter_fusion = f32[128,4,2048]{2,1,0:T(4,128)} fusion(f32[128,4,2048]{2,1,0:T(4,128)} %broadcast_in_dim.23, s32[256]{0:T(256)S(1)} %bitcast.31, f32[256,2048]{1,0:T(8,128)S(1)} %select_add_fusion), kind=kCustom, calls=%fused_computation.2 | custom fusion | bytes 6293504 | tf_op jit(solution)/shard_map/scatter | solution.py:76
  162.0 6.4 %all-to-all-start.4 = ((f32[128,4,2048]{2,1,0:T(4,128)}), f32[128,4,2048]{2,1,0:T(4,128)}, u32[]{:S(2)}, u32[]{:S(2)}) async-start(f32[128,4,2048]{2,1,0:T(4,128)} %scatter_fusion), calls=%async_computation.4 | async-start | bytes 8388608 | tf_op jit(solution)/shard_map/all_to_all | solution.py:82
  168.5 6.7 %convolution_convert_fusion = bf16[256,2048]{1,0:T(8,128)(2,1)} fusion(bf16[2048,2048]{1,0:T(8,128)(2,1)} %param.8, f32[256,2048]{1,0:T(8,128)S(1)} %select_add_fusion), kind=kOutput, calls=%fused_computation.9 | convolution fusion | flops 2148532224 | bytes 11534336 | tf_op jit(solution)/shard_map/dot_general | solution.py:79
  175.2 46.5 %all-to-all-done.4 = f32[128,4,2048]{2,1,0:T(4,128)} async-done(((f32[128,4,2048]{2,1,0:T(4,128)}), f32[128,4,2048]{2,1,0:T(4,128)}, u32[]{:S(2)}, u32[]{:S(2)}) %all-to-all-start.4) | async-done | bytes 4194336 | tf_op jit(solution)/shard_map/all_to_all | solution.py:82
  221.7 5.3 %reshape.62 = f32[512,2048]{1,0:T(8,128)} reshape(f32[128,4,2048]{2,1,0:T(4,128)} %all-to-all-done.4) | data formatting | bytes 8388608 | tf_op jit(solution)/shard_map/reshape | solution.py:83
  (9 shorter events, 0.1 us)
Async XLA Ops:
  7.5 1.3 copy-start.1
  8.8 26.1 %copy-start.2 = (f32[8,2048]{1,0:T(8,128)S(1)}, f32[8,2048]{1,0:T(8,128)}, u32[]{:S(2)}) copy-start(f32[8,2048]{1,0:T(8,128)} %param.9) | copy-start | bytes 196612
  36.1 19.7 %all-to-all-start.1 = ((f32[16,8,2048]{2,1,0:T(8,128)}), f32[16,8,2048]{2,1,0:T(8,128)S(1)}, u32[]{:S(2)}, u32[]{:S(2)}) async-start(f32[16,8,2048]{2,1,0:T(8,128)} %broadcast_in_dim.21), calls=%async_computation.1 | async-start | bytes 2097152 | tf_op jit(solution)/shard_map/all_to_all | solution.py:21
  71.7 1.9 copy-start
  71.7 5.6 %copy-start.3 = (s32[256,1]{0,1:T(1,128)S(1)}, s32[256,1]{0,1:T(1,128)}, u32[]{:S(2)}) copy-start(s32[256,1]{0,1:T(1,128)} %param.11) | copy-start | bytes 3076
  73.6 19.2 %all-to-all-start.2 = ((f32[16,8,2048]{2,1,0:T(8,128)}), f32[16,8,2048]{2,1,0:T(8,128)S(1)}, u32[]{:S(2)}, u32[]{:S(2)}) async-start(f32[16,8,2048]{2,1,0:T(8,128)} %convolution_bitcast_fusion), calls=%async_computation.2 | async-start | bytes 2097152 | tf_op jit(solution)/shard_map/all_to_all | solution.py:15
  94.1 19.4 %all-to-all-start.3 = ((f32[16,8,2048]{2,1,0:T(8,128)}), f32[16,8,2048]{2,1,0:T(8,128)S(1)}, u32[]{:S(2)}, u32[]{:S(2)}) async-start(f32[16,8,2048]{2,1,0:T(8,128)} %broadcast_in_dim.22), calls=%async_computation.3 | async-start | bytes 2097152 | tf_op jit(solution)/shard_map/all_to_all | solution.py:21
  162.0 59.7 %all-to-all-start.4 = ((f32[128,4,2048]{2,1,0:T(4,128)}), f32[128,4,2048]{2,1,0:T(4,128)}, u32[]{:S(2)}, u32[]{:S(2)}) async-start(f32[128,4,2048]{2,1,0:T(4,128)} %scatter_fusion), calls=%async_computation.4 | async-start | bytes 8388608 | tf_op jit(solution)/shard_map/all_to_all | solution.py:82

commit v3 on v1

--- a/solution.py
+++ b/solution.py
@@ -1,12 +1,85 @@
 import jax
 import jax.numpy as jnp
 from jax import lax
+from jax.experimental import pallas as pl
 from jax.sharding import PartitionSpec as P
 
 ITERS = 2
 
 
 step_size = 0.25
+
+
+COLUMN_BLOCK = 1024
+
+
+def _answer_kernel(e_ref, s_ref, n_ref, o_ref):
+    answers = jnp.dot(e_ref[...], s_ref[...], preferred_element_type=jnp.float32)
+    o_ref[...] = (answers - n_ref[...].astype(jnp.float32)).astype(o_ref.dtype)
+
+
+def misfit_of(estimate_bf16, strategy, noisy):
+    rows, inner = estimate_bf16.shape
+    cols = strategy.shape[1]
+    block = min(COLUMN_BLOCK, cols)
+    return pl.pallas_call(
+        _answer_kernel,
+        grid=(cols // block,),
+        in_specs=[
+            pl.BlockSpec((rows, inner), lambda j: (0, 0)),
+            pl.BlockSpec((inner, block), lambda j: (0, j)),
+            pl.BlockSpec((rows, block), lambda j: (0, j)),
+        ],
+        out_specs=pl.BlockSpec((rows, block), lambda j: (0, j)),
+        out_shape=jax.ShapeDtypeStruct((rows, cols), jnp.bfloat16),
+        cost_estimate=pl.CostEstimate(
+            flops=2 * rows * inner * cols,
+            transcendentals=0,
+            bytes_accessed=2 * (rows * inner + inner * cols + 2 * rows * cols),
+        ),
+    )(estimate_bf16, strategy, noisy)
+
+
+def _step_kernel(m_ref, s_ref, e_ref, o_ref):
+    gradient = lax.dot_general(
+        m_ref[...], s_ref[...], (((1,), (1,)), ((), ())), preferred_element_type=jnp.float32
+    )
+    o_ref[...] = e_ref[...] - step_size * gradient
+
+
+def _first_step_kernel(m_ref, s_ref, o_ref):
+    gradient = lax.dot_general(
+        m_ref[...], s_ref[...], (((1,), (1,)), ((), ())), preferred_element_type=jnp.float32
+    )
+    o_ref[...] = 0.0 - step_size * gradient
+
+
+def stepped_of(misfit, strategy, estimate):
+    rows, inner = misfit.shape
+    cols = strategy.shape[0]
+    block = min(COLUMN_BLOCK, cols)
+    in_specs = [
+        pl.BlockSpec((rows, inner), lambda j: (0, 0)),
+        pl.BlockSpec((block, inner), lambda j: (j, 0)),
+    ]
+    operands = [misfit, strategy]
+    kernel = _first_step_kernel
+    if estimate is not None:
+        in_specs.append(pl.BlockSpec((rows, block), lambda j: (0, j)))
+        operands.append(estimate)
+        kernel = _step_kernel
+    return pl.pallas_call(
+        kernel,
+        grid=(cols // block,),
+        in_specs=in_specs,
+        out_specs=pl.BlockSpec((rows, block), lambda j: (0, j)),
+        out_shape=jax.ShapeDtypeStruct((rows, cols), jnp.float32),
+        cost_estimate=pl.CostEstimate(
+            flops=2 * rows * inner * cols,
+            transcendentals=0,
+            bytes_accessed=2 * (rows * inner + inner * cols) + 8 * rows * cols,
+        ),
+    )(*operands)
 
 
 def unit_sum(partial, unit_count):
@@ -40,21 +113,15 @@
     tract_count = None
     for iteration in range(ITERS):
         if iteration == 0:
-            misfit = -noisy
+            stepped = stepped_of(-noisy, strategy, None)
         else:
-            answers = jnp.dot(
-                estimate.astype(jnp.bfloat16), strategy, preferred_element_type=jnp.float32
-            )
-            misfit = (answers - noisy.astype(jnp.float32)).astype(jnp.bfloat16)
-        gradient = lax.dot_general(
-            misfit, strategy, (((1,), (1,)), ((), ())), preferred_element_type=jnp.float32
-        )
-        stepped = estimate - step_size * gradient
+            misfit = misfit_of(estimate.astype(jnp.bfloat16), strategy, noisy)
+            stepped = stepped_of(misfit, strategy, estimate)
         partial_value = lax.dot_general(
             member,
             stepped,
             (((0,), (0,)), ((), ())),
-            precision=lax.Precision.HIGHEST,
+            precision=lax.Precision.HIGH,
             preferred_element_type=jnp.float32,
         )
         if tract_count is None:
@@ -67,7 +134,7 @@
         parent_gap = (county_hist - child_total) / tract_count[:, None]
         region_gap = unit_gather(parent_gap, unit_count)
         estimate = stepped + jnp.dot(
-            member, region_gap, precision=lax.Precision.HIGHEST, preferred_element_type=jnp.float32
+            member, region_gap, precision=lax.Precision.HIGH, preferred_element_type=jnp.float32
         )
     owners = tract_owner[:, 0]
     owner_hits = (owners[:, None] == jnp.arange(devices, dtype=jnp.int32)[None, :]).astype(

time: 188 us -> 196 us (1.043)
  Pallas kernels: 0 us -> 20.9 us
  matrix products: 31.9 us -> 16.6 us
  other arithmetic: 1.6 us -> 4.01 us
    pallas_call x0 -> x3, Pallas kernels: none -> 20.9 us  [the longest x2 13.6 us: stepped_of(): pl.pallas_call(kernel, grid=(cols // block,), in_specs=in_specs, out_spec...]
    dot_general x4 -> x2, matrix products: 22.3 us -> 4.63 us  [local(): jnp.dot(member, region_gap, precision=lax.Precision.HIGH, preferred_eleme...]
    dot_general x2, matrix products: 2.84 us -> 5.32 us  [local(): lax.dot_general(member, stepped, (((0,), (0,)), ((), ())), precision=lax....]
    neg x0 -> x1, other arithmetic: none -> 2.41 us  [local(): stepped = stepped_of(-noisy, strategy, None)]
where the time goes in v3:
time: 196 us; the launch traced here: 195 us
  waiting for transfers between devices  76.7 us (39%)
  blocking collectives  45.3 us (23%)
  Pallas kernels  20.9 us (11%)
  local copies, waits for them, and re-layouts  17.1 us (9%)
  matrix products  16.6 us (8%)
  starting transfers between devices  13.8 us (7%)
  other arithmetic  4.01 us (2%)
    all_to_all x1, waiting for transfers between devices, local(): lax.all_to_all(grouped, ('region', 'unit'), split_axis=0, concat_axis=0,...  46.5 us
    all_to_all x1, blocking collectives, unit_sum(): arrived = lax.all_to_all(grouped, 'unit', 0, 0, tiled=True)  25.9 us
    all_to_all x1, blocking collectives, unit_gather(): arrived = lax.all_to_all(spread, 'unit', 0, 0, tiled=True)  19.4 us
    all_to_all x1, waiting for transfers between devices, unit_gather(): arrived = lax.all_to_all(spread, 'unit', 0, 0, tiled=True)  15.2 us
    all_to_all x1, waiting for transfers between devices, unit_sum(): arrived = lax.all_to_all(grouped, 'unit', 0, 0, tiled=True)  14.9 us
    pallas_call x2, Pallas kernels, stepped_of(): pl.pallas_call(kernel, grid=(cols // block,), in_specs=in_specs, out_spec...  13.6 us
    pallas_call x1, Pallas kernels, misfit_of(): pl.pallas_call(_answer_kernel, grid=(cols // block,), in_specs=[pl.BlockS...  7.24 us
    dot_general x1, matrix products, local(): jnp.dot(estimate.astype(jnp.bfloat16), strategy, preferred_element_type=j...  6.68 us
  transfers between devices with their start and end apart: 3, of which 3 were waited for; matrix products, arithmetic and copies ran while one was open for 4% of the time, Pallas kernels for 0%

profile of v3, /device:TPU:6, one launch (start us, length us, event | category | flops | bytes accessed | tf_op | source)
XLA Modules:
  0.0 195.1 jit_solution(7674917901574874529)
XLA Ops:
  0.6 0.7 broadcast_subtract_fusion
  1.3 0.1 convert_reduce_fusion
  1.4 2.4 %neg.3.m_ref = bf16[256,2048]{1,0:T(8,128)(2,1)} negate(bf16[256,2048]{1,0:T(8,128)(2,1)} %n_ref.1) | non-fusion elementwise | flops 524288 | bytes 2097152 | tf_op jit(solution)/shard_map/neg | solution.py:116
  3.8 6.0 %shard_map.68 = f32[256,2048]{1,0:T(8,128)} custom-call(bf16[256,2048]{1,0:T(8,128)(2,1)} %neg.3.m_ref, bf16[2048,2048]{1,0:T(8,128)(2,1)} %s_ref.5), custom_call_target="tpu_custom_call" | custom-call | flops 2147483648 | bytes 13631488 | tf_op jit(solution)/shard_map/pallas_call | solution.py:71
  9.9 2.2 %fusion.9 = f32[128,2048]{1,0:T(8,128)S(1)} fusion(f32[256,2048]{1,0:T(8,128)} %shard_map.68, s32[256]{0:T(256)S(1)} %broadcast_subtract_fusion), kind=kOutput, calls=%fused_computation.20 | convolution fusion | flops 402685952 | bytes 3146752 | tf_op jit(solution)/shard_map/dot_general | solution.py:120
  12.1 0.1 broadcast_in_dim.8
  12.1 0.1 maximum_bitcast_fusion
  12.2 0.0 copy-start.3
  12.2 25.9 %all_to_all.25 = f32[16,8,2176]{2,1,0:T(8,128)S(1)} all-to-all(f32[16,8,2176]{2,1,0:T(8,128)S(1)} %maximum_bitcast_fusion), channel_id=1, replica_groups=mesh['region'=8,'unit'=16] {'unit'}, dimensions={0} | all-to-all | bytes 2228224 | tf_op jit(solution)/shard_map/all_to_all | solution.py:88
  38.2 0.0 copy-start.1
  38.2 0.1 reduce_sum.39
  38.2 0.1 slice_reduce_fusion
  38.3 0.0 copy-done.3
  38.3 0.1 fusion.10
  38.4 0.1 broadcast_in_dim.9
  38.5 19.4 %all_to_all.26 = f32[16,8,2048]{2,1,0:T(8,128)S(1)} all-to-all(f32[16,8,2048]{2,1,0:T(8,128)S(1)} %broadcast_in_dim.9), channel_id=1, replica_groups=mesh['region'=8,'unit'=16] {'unit'}, dimensions={0} | all-to-all | bytes 2097152 | tf_op jit(solution)/shard_map/all_to_all | solution.py:94
  57.9 0.0 copy-done.1
  57.9 2.5 %fusion.16 = (bf16[256,2048]{1,0:T(8,128)(2,1)}, f32[256,2048]{1,0:T(8,128)}) fusion(f32[256,2048]{1,0:T(8,128)S(1)} %copy-done.1, f32[16,8,2048]{2,1,0:T(8,128)S(1)} %all_to_all.26, s32[256]{0:T(256)S(1)} %broadcast_subtract_fusion), kind=kOutput, calls=%fused_computation.34 | convolution fusion | flops 403734528 | bytes 6292480 | tf_op jit(solution)/shard_map/dot_general | solution.py:136
  60.4 7.2 %shard_map.69.m_ref = bf16[256,2048]{1,0:T(8,128)(2,1)} custom-call(bf16[256,2048]{1,0:T(8,128)(2,1)} %get-tuple-element.2.e_ref, bf16[2048,2048]{1,0:T(8,128)(2,1)} %s_ref.5, bf16[256,2048]{1,0:T(8,128)(2,1)} %n_ref.1), custom_call_target="tpu_custom_call" | custom-call | flops 2147483648 | bytes 11534336 | tf_op jit(solution)/shard_map/pallas_call | solution.py:25
  67.6 7.6 %shard_map.70 = f32[256,2048]{1,0:T(8,128)} custom-call(bf16[256,2048]{1,0:T(8,128)(2,1)} %shard_map.69.m_ref, bf16[2048,2048]{1,0:T(8,128)(2,1)} %s_ref.5, f32[256,2048]{1,0:T(8,128)} %get-tuple-element.3.e_ref), custom_call_target="tpu_custom_call" | custom-call | flops 2147483648 | bytes 13631488 | tf_op jit(solution)/shard_map/pallas_call | solution.py:71
  75.2 0.0 copy-start.4
  75.2 3.2 %convolution_bitcast_fusion = f32[16,8,2048]{2,1,0:T(8,128)} fusion(f32[256,2048]{1,0:T(8,128)} %shard_map.70, s32[256]{0:T(256)S(1)} %broadcast_subtract_fusion), kind=kOutput, calls=%fused_computation.4 | convolution fusion | flops 402685952 | bytes 3146752 | tf_op jit(solution)/shard_map/dot_general | solution.py:120
  78.4 3.7 %all-to-all-start.2 = ((f32[16,8,2048]{2,1,0:T(8,128)}), f32[16,8,2048]{2,1,0:T(8,128)S(1)}, u32[]{:S(2)}, u32[]{:S(2)}) async-start(f32[16,8,2048]{2,1,0:T(8,128)} %convolution_bitcast_fusion), calls=%async_computation.2 | async-start | bytes 2097152 | tf_op jit(solution)/shard_map/all_to_all | solution.py:88
  82.0 0.0 copy-done.4
  82.0 0.1 copy.10
  82.2 14.9 %all-to-all-done.2 = f32[16,8,2048]{2,1,0:T(8,128)S(1)} async-done(((f32[16,8,2048]{2,1,0:T(8,128)}), f32[16,8,2048]{2,1,0:T(8,128)S(1)}, u32[]{:S(2)}, u32[]{:S(2)}) %all-to-all-start.2) | async-done | bytes 1048608 | tf_op jit(solution)/shard_map/all_to_all | solution.py:88
  97.1 0.1 reduce_sum.40
  97.1 0.0 copy-start
  97.2 0.1 subtract_divide_fusion
  97.2 1.1 broadcast_in_dim.10
  98.3 3.7 %all-to-all-start.3 = ((f32[16,8,2048]{2,1,0:T(8,128)}), f32[16,8,2048]{2,1,0:T(8,128)S(1)}, u32[]{:S(2)}, u32[]{:S(2)}) async-start(f32[16,8,2048]{2,1,0:T(8,128)} %broadcast_in_dim.10), calls=%async_computation.3 | async-start | bytes 2097152 | tf_op jit(solution)/shard_map/all_to_all | solution.py:94
  102.0 0.2 fusion.5
  102.3 0.2 fusion.7
  102.5 15.2 %all-to-all-done.3 = f32[16,8,2048]{2,1,0:T(8,128)S(1)} async-done(((f32[16,8,2048]{2,1,0:T(8,128)}), f32[16,8,2048]{2,1,0:T(8,128)S(1)}, u32[]{:S(2)}, u32[]{:S(2)}) %all-to-all-start.3) | async-done | bytes 1048608 | tf_op jit(solution)/shard_map/all_to_all | solution.py:94
  117.7 0.0 copy-done
  117.7 2.2 %convolution_add_fusion = f32[256,2048]{1,0:T(8,128)} fusion(f32[256,2048]{1,0:T(8,128)S(1)} %copy-done, f32[16,8,2048]{2,1,0:T(8,128)S(1)} %all-to-all-done.3, s32[256]{0:T(256)S(1)} %broadcast_subtract_fusion), kind=kOutput, calls=%fused_computation.1 | convolution fusion | flops 403210240 | bytes 5243904 | tf_op jit(solution)/shard_map/dot_general | solution.py:136
  119.9 5.1 %scatter_custom_fusion = f32[512,2048]{1,0:T(8,128)} fusion(s32[256]{0:T(256)S(1)} %bitcast.39, f32[256,2048]{1,0:T(8,128)} %convolution_add_fusion, f32[]{:T(128)} %constant.5.clone.1), kind=kCustom, calls=%fused_computation.5 | custom fusion | bytes 4194816 | tf_op jit(solution)/shard_map/scatter | solution.py:146
  125.0 5.2 %reshape.48 = f32[128,4,2048]{2,1,0:T(4,128)} reshape(f32[512,2048]{1,0:T(8,128)} %scatter_custom_fusion) | data formatting | bytes 8388608 | tf_op jit(solution)/shard_map/reshape | solution.py:150
  130.2 0.0 copy-start.2
  130.2 6.5 %all-to-all-start.4 = ((f32[128,4,2048]{2,1,0:T(4,128)}), f32[128,4,2048]{2,1,0:T(4,128)}, u32[]{:S(2)}, u32[]{:S(2)}) async-start(f32[128,4,2048]{2,1,0:T(4,128)} %reshape.48), calls=%async_computation.4 | async-start | bytes 8388608 | tf_op jit(solution)/shard_map/all_to_all | solution.py:151
  136.6 0.0 copy-done.2
  136.6 6.7 %convolution_convert_fusion = bf16[256,2048]{1,0:T(8,128)(2,1)} fusion(bf16[2048,2048]{1,0:T(8,128)(2,1)} %s_ref.5, f32[256,2048]{1,0:T(8,128)S(1)} %copy-done.2), kind=kOutput, calls=%fused_computation.3 | convolution fusion | flops 2148532224 | bytes 11534336 | tf_op jit(solution)/shard_map/dot_general | solution.py:147
  143.3 46.5 %all-to-all-done.4 = f32[128,4,2048]{2,1,0:T(4,128)} async-done(((f32[128,4,2048]{2,1,0:T(4,128)}), f32[128,4,2048]{2,1,0:T(4,128)}, u32[]{:S(2)}, u32[]{:S(2)}) %all-to-all-start.4) | async-done | bytes 4194336 | tf_op jit(solution)/shard_map/all_to_all | solution.py:151
  189.9 5.3 %reshape.49 = f32[512,2048]{1,0:T(8,128)} reshape(f32[128,4,2048]{2,1,0:T(4,128)} %all-to-all-done.4) | data formatting | bytes 8388608 | tf_op jit(solution)/shard_map/reshape | solution.py:152
  (7 shorter events, 0.1 us)
Async XLA Ops:
  12.2 26.1 %copy-start.3 = (f32[8,2048]{1,0:T(8,128)S(1)}, f32[8,2048]{1,0:T(8,128)}, u32[]{:S(2)}) copy-start(f32[8,2048]{1,0:T(8,128)} %param.7) | copy-start | bytes 196612
  38.2 19.7 %copy-start.1 = (f32[256,2048]{1,0:T(8,128)S(1)}, f32[256,2048]{1,0:T(8,128)}, u32[]{:S(2)}) copy-start(f32[256,2048]{1,0:T(8,128)} %shard_map.68) | copy-start | bytes 6291460
  75.2 6.8 %copy-start.4 = (s32[256,1]{0,1:T(1,128)S(1)}, s32[256,1]{0,1:T(1,128)}, u32[]{:S(2)}) copy-start(s32[256,1]{0,1:T(1,128)} %param.9) | copy-start | bytes 3076
  78.4 18.7 %all-to-all-start.2 = ((f32[16,8,2048]{2,1,0:T(8,128)}), f32[16,8,2048]{2,1,0:T(8,128)S(1)}, u32[]{:S(2)}, u32[]{:S(2)}) async-start(f32[16,8,2048]{2,1,0:T(8,128)} %convolution_bitcast_fusion), calls=%async_computation.2 | async-start | bytes 2097152 | tf_op jit(solution)/shard_map/all_to_all | solution.py:88
  97.1 20.6 %copy-start = (f32[256,2048]{1,0:T(8,128)S(1)}, f32[256,2048]{1,0:T(8,128)}, u32[]{:S(2)}) copy-start(f32[256,2048]{1,0:T(8,128)} %shard_map.70) | copy-start | bytes 6291460
  98.3 19.4 %all-to-all-start.3 = ((f32[16,8,2048]{2,1,0:T(8,128)}), f32[16,8,2048]{2,1,0:T(8,128)S(1)}, u32[]{:S(2)}, u32[]{:S(2)}) async-start(f32[16,8,2048]{2,1,0:T(8,128)} %broadcast_in_dim.10), calls=%async_computation.3 | async-start | bytes 2097152 | tf_op jit(solution)/shard_map/all_to_all | solution.py:94
  130.2 6.5 %copy-start.2 = (f32[256,2048]{1,0:T(8,128)S(1)}, f32[256,2048]{1,0:T(8,128)}, u32[]{:S(2)}) copy-start(f32[256,2048]{1,0:T(8,128)} %convolution_add_fusion) | copy-start | bytes 6291460
  130.2 59.7 %all-to-all-start.4 = ((f32[128,4,2048]{2,1,0:T(4,128)}), f32[128,4,2048]{2,1,0:T(4,128)}, u32[]{:S(2)}, u32[]{:S(2)}) async-start(f32[128,4,2048]{2,1,0:T(4,128)} %reshape.48), calls=%async_computation.4 | async-start | bytes 8388608 | tf_op jit(solution)/shard_map/all_to_all | solution.py:151

commit v4 on v1

--- a/solution.py
+++ b/solution.py
@@ -36,6 +36,18 @@
     )
     county_tally = jnp.sum(member, axis=0)
     tally_lanes = 128
+    owners = tract_owner[:, 0]
+    owner_hits = (owners[:, None] == jnp.arange(devices, dtype=jnp.int32)[None, :]).astype(
+        jnp.int32
+    )
+    slot_index = jnp.sum((jnp.cumsum(owner_hits, axis=0) - owner_hits) * owner_hits, axis=1)
+    capacity = 2 * tract_rows // devices
+    target = owners * capacity + slot_index
+    slot_hits = target[None, :] == jnp.arange(devices * capacity, dtype=jnp.int32)[:, None]
+    slot_county = jnp.sum(jnp.where(slot_hits, local_id[None, :] + 1, 0), axis=1) - 1
+    slot_member = (
+        slot_county[:, None] == jnp.arange(county_region, dtype=jnp.int32)[None, :]
+    ).astype(jnp.float32).reshape(devices, capacity, county_region)
     estimate = jnp.zeros((tract_rows, width), jnp.float32)
     tract_count = None
     for iteration in range(ITERS):
@@ -64,23 +76,28 @@
             tract_count = summed[:, width]
         else:
             child_total = unit_sum(partial_value, unit_count)
+        if iteration == ITERS - 1:
+            slot_stepped = (
+                jnp.zeros((devices * capacity, width), jnp.float32)
+                .at[target]
+                .set(stepped)
+                .reshape(devices, capacity, width)
+            )
         parent_gap = (county_hist - child_total) / tract_count[:, None]
         region_gap = unit_gather(parent_gap, unit_count)
         estimate = stepped + jnp.dot(
             member, region_gap, precision=lax.Precision.HIGHEST, preferred_element_type=jnp.float32
         )
-    owners = tract_owner[:, 0]
-    owner_hits = (owners[:, None] == jnp.arange(devices, dtype=jnp.int32)[None, :]).astype(
-        jnp.int32
+    grouped = slot_stepped + jnp.einsum(
+        "osc,ch->osh",
+        slot_member,
+        region_gap,
+        precision=lax.Precision.HIGHEST,
+        preferred_element_type=jnp.float32,
     )
-    slot_index = jnp.sum((jnp.cumsum(owner_hits, axis=0) - owner_hits) * owner_hits, axis=1)
-    capacity = 2 * tract_rows // devices
-    target = owners * capacity + slot_index
-    outgoing = jnp.zeros((devices * capacity, width), jnp.float32).at[target].set(estimate)
     released = jnp.dot(
         estimate.astype(jnp.bfloat16), strategy, preferred_element_type=jnp.float32
     ).astype(jnp.bfloat16)
-    grouped = outgoing.reshape(devices, capacity, width)
     arrived = lax.all_to_all(grouped, ("region", "unit"), split_axis=0, concat_axis=0, tiled=True)
     relaid = arrived.reshape(devices * capacity, width)
     return (released, relaid)

time: 188 us -> 184 us (0.979)
  waiting for transfers between devices: 76.5 us -> 49.1 us
  blocking collectives: 45.1 us -> 63.2 us
  local copies, waits for them, and re-layouts: 17.1 us -> 21.6 us
  matrix products: 31.9 us -> 35.8 us
  starting transfers between devices: 13.9 us -> 10.2 us
    all_to_all x1 -> x2, blocking collectives: 25.9 us -> 43.9 us  [unit_sum(): arrived = lax.all_to_all(grouped, 'unit', 0, 0, tiled=True)]
    all_to_all x1 -> x0, waiting for transfers between devices: 14.9 us -> none  [unit_sum(): arrived = lax.all_to_all(grouped, 'unit', 0, 0, tiled=True)]
    all_to_all x1, waiting for transfers between devices: 15.1 us -> 3.74 us  [unit_gather(): arrived = lax.all_to_all(spread, 'unit', 0, 0, tiled=True)]
    dot_general x0 -> x1, matrix products: none -> 6.26 us  [local(): jnp.einsum('osc,ch->osh', slot_member, region_gap, precision=lax.Precisio...]
    add x0 -> x1, local copies, waits for them, and re-layouts: none -> 4.71 us  [local(): slot_stepped + jnp.einsum('osc,ch->osh', slot_member, region_gap, precisi...]
    all_to_all x1 -> x0, starting transfers between devices: 3.66 us -> none  [unit_sum(): arrived = lax.all_to_all(grouped, 'unit', 0, 0, tiled=True)]
  transfers between devices with their start and end apart: 3 -> 2, of which waited for: 3 -> 2; matrix products, arithmetic and copies ran while one was open for 4% -> 9% of each run, Pallas kernels for 0% -> 0%
where the time goes in v4:
time: 184 us; the launch traced here: 183 us
  blocking collectives  63.2 us (34%)
  waiting for transfers between devices  49.1 us (27%)
  matrix products  35.8 us (19%)
  local copies, waits for them, and re-layouts  21.6 us (12%)
  starting transfers between devices  10.2 us (6%)
  other arithmetic  2.46 us (1%)
    all_to_all x1, waiting for transfers between devices, local(): lax.all_to_all(grouped, ('region', 'unit'), split_axis=0, concat_axis=0,...  45.4 us
    all_to_all x2, blocking collectives, unit_sum(): arrived = lax.all_to_all(grouped, 'unit', 0, 0, tiled=True)  43.9 us
    all_to_all x1, blocking collectives, unit_gather(): arrived = lax.all_to_all(spread, 'unit', 0, 0, tiled=True)  19.2 us
    dot_general x2, matrix products, local(): lax.dot_general(misfit, strategy, (((1,), (1,)), ((), ())), preferred_ele...  17.6 us
    dot_general x1, matrix products, local(): jnp.dot(estimate.astype(jnp.bfloat16), strategy, preferred_element_type=j...  6.72 us
    all_to_all x1, starting transfers between devices, local(): lax.all_to_all(grouped, ('region', 'unit'), split_axis=0, concat_axis=0,...  6.37 us
    dot_general x1, matrix products, local(): jnp.einsum('osc,ch->osh', slot_member, region_gap, precision=lax.Precisio...  6.26 us
    reshape x1, local copies, waits for them, and re-layouts, local(): relaid = arrived.reshape(devices * capacity, width)  5.27 us
  transfers between devices with their start and end apart: 2, of which 2 were waited for; matrix products, arithmetic and copies ran while one was open for 9% of the time, Pallas kernels for 0%

profile of v4, /device:TPU:6, one launch (start us, length us, event | category | flops | bytes accessed | tf_op | source)
XLA Modules:
  0.0 183.2 jit_solution(7665692103174659980)
XLA Ops:
  0.6 0.8 copy.18
  1.4 0.2 fusion.15
  1.7 0.9 fusion.17
  2.6 0.7 broadcast_add_fusion.2
  3.3 0.1 convert_reduce_fusion
  3.4 6.1 %fusion = f32[256,2048]{1,0:T(8,128)S(1)} fusion(bf16[2048,2048]{1,0:T(8,128)(2,1)} %param.6, bf16[256,2048]{1,0:T(8,128)(2,1)} %param.5), kind=kOutput, calls=%fused_computation.6 | convolution fusion | flops 2149056512 | bytes 11534336 | tf_op jit(solution)/shard_map/dot_general | solution.py:61
  9.5 0.9 fusion.20
  10.4 0.1 broadcast_in_dim.23
  10.5 0.1 maximum_bitcast_fusion
  10.6 0.0 copy-start
  10.6 25.9 %all_to_all.25 = f32[16,8,2176]{2,1,0:T(8,128)S(1)} all-to-all(f32[16,8,2176]{2,1,0:T(8,128)S(1)} %maximum_bitcast_fusion), channel_id=1, replica_groups=mesh['region'=8,'unit'=16] {'unit'}, dimensions={0} | all-to-all | bytes 2228224 | tf_op jit(solution)/shard_map/all_to_all | solution.py:15
  36.5 0.1 reduce_sum.48
  36.6 0.1 slice_reduce_fusion
  36.7 0.0 copy-done
  36.7 0.1 fusion.21
  36.8 0.1 broadcast_in_dim.24
  36.9 19.2 %all_to_all.26 = f32[16,8,2048]{2,1,0:T(8,128)S(1)} all-to-all(f32[16,8,2048]{2,1,0:T(8,128)S(1)} %broadcast_in_dim.24), channel_id=1, replica_groups=mesh['region'=8,'unit'=16] {'unit'}, dimensions={0} | all-to-all | bytes 2097152 | tf_op jit(solution)/shard_map/all_to_all | solution.py:21
  56.1 0.0 copy-start.2
  56.1 2.4 %convolution_add_fusion.1 = f32[256,2048]{1,0:T(8,128)} fusion(f32[256,2048]{1,0:T(8,128)S(1)} %fusion, f32[16,8,2048]{2,1,0:T(8,128)S(1)} %all_to_all.26, s32[256]{0:T(256)S(1)} %get-tuple-element.3), kind=kOutput, calls=%fused_computation.5 | convolution fusion | flops 805863424 | bytes 5243904 | tf_op jit(solution)/shard_map/dot_general | solution.py:88
  58.5 0.0 copy-done.2
  58.5 11.5 %fusion.1 = f32[256,2048]{1,0:T(8,128)S(1)} fusion(f32[256,2048]{1,0:T(8,128)} %convolution_add_fusion.1, bf16[2048,2048]{1,0:T(8,128)(2,1)} %param.6, bf16[256,2048]{1,0:T(8,128)(2,1)S(1)} %copy-done.2), kind=kOutput, calls=%fused_computation.7 | convolution fusion | flops 4298113024 | bytes 13631488 | tf_op jit(solution)/shard_map/dot_general | solution.py:61
  70.0 0.9 convolution_bitcast_fusion
  70.9 18.0 %all_to_all.27 = f32[16,8,2048]{2,1,0:T(8,128)S(1)} all-to-all(f32[16,8,2048]{2,1,0:T(8,128)S(1)} %convolution_bitcast_fusion), channel_id=1, replica_groups=mesh['region'=8,'unit'=16] {'unit'}, dimensions={0} | all-to-all | bytes 2097152 | tf_op jit(solution)/shard_map/all_to_all | solution.py:15
  89.0 0.0 copy-start.1
  89.0 0.1 reduce_sum.49
  89.0 0.1 subtract_divide_fusion
  89.1 1.1 broadcast_in_dim.25
  90.2 3.8 %all-to-all-start.3 = ((f32[16,8,2048]{2,1,0:T(8,128)}), f32[16,8,2048]{2,1,0:T(8,128)S(1)}, u32[]{:S(2)}, u32[]{:S(2)}) async-start(f32[16,8,2048]{2,1,0:T(8,128)} %broadcast_in_dim.25), calls=%async_computation.3 | async-start | bytes 2097152 | tf_op jit(solution)/shard_map/all_to_all | solution.py:21
  94.0 0.1 select_reduce_fusion
  94.2 0.1 sub.39
  94.3 0.1 copy.20
  94.3 0.0 copy-done.1
  94.4 4.1 %scatter_custom_fusion = f32[512,2048]{1,0:T(8,128)} fusion(s32[256]{0:T(256)S(1)} %bitcast.49, f32[256,2048]{1,0:T(8,128)S(1)} %fusion.1, f32[]{:T(128)} %constant.10.clone.1), kind=kCustom, calls=%fused_computation.13 | custom fusion | bytes 4194308 | tf_op jit(solution)/shard_map/scatter | solution.py:83
  98.4 5.2 %reshape.87 = f32[128,4,2048]{2,1,0:T(4,128)} reshape(f32[512,2048]{1,0:T(8,128)} %scatter_custom_fusion) | data formatting | bytes 8388608 | tf_op jit(solution)/shard_map/reshape | solution.py:84
  103.6 3.7 %all-to-all-done.3 = f32[16,8,2048]{2,1,0:T(8,128)S(1)} async-done(((f32[16,8,2048]{2,1,0:T(8,128)}), f32[16,8,2048]{2,1,0:T(8,128)S(1)}, u32[]{:S(2)}, u32[]{:S(2)}) %all-to-all-start.3) | async-done | bytes 1048608 | tf_op jit(solution)/shard_map/all_to_all | solution.py:21
  107.4 6.3 %copy_add_fusion = f32[128,4,2048]{2,0,1:T(8,128)S(1)} fusion(f32[128,4,2048]{2,1,0:T(4,128)} %reshape.87, f32[16,8,2048]{2,1,0:T(8,128)S(1)} %all-to-all-done.3, s32[128,4]{0,1:T(4,128)S(1)} %copy.20), kind=kOutput, calls=%fused_computation.1 | convolution fusion | flops 1611726848 | bytes 9439232 | tf_op jit(solution)/shard_map/osc,ch->osh/dot_general | solution.py:91
  113.6 4.7 %copy.22 = f32[128,4,2048]{2,1,0:T(4,128)} copy(f32[128,4,2048]{2,0,1:T(8,128)S(1)} %copy_add_fusion) | data formatting | bytes 8388608 | tf_op jit(solution)/shard_map/add | solution.py:91
  118.3 6.4 %all-to-all-start.4 = ((f32[128,4,2048]{2,1,0:T(4,128)}), f32[128,4,2048]{2,1,0:T(4,128)}, u32[]{:S(2)}, u32[]{:S(2)}) async-start(f32[128,4,2048]{2,1,0:T(4,128)} %copy.22), calls=%async_computation.4 | async-start | bytes 8388608 | tf_op jit(solution)/shard_map/all_to_all | solution.py:101
  124.7 1.1 fusion.3
  125.8 6.7 %convolution_convert_fusion = bf16[256,2048]{1,0:T(8,128)(2,1)} fusion(bf16[256,2048]{1,0:T(8,128)(2,1)S(1)} %fusion.3, bf16[2048,2048]{1,0:T(8,128)(2,1)} %param.6), kind=kOutput, calls=%fused_computation.11 | convolution fusion | flops 2148007936 | bytes 10485760 | tf_op jit(solution)/shard_map/dot_general | solution.py:98
  132.5 45.4 %all-to-all-done.4 = f32[128,4,2048]{2,1,0:T(4,128)} async-done(((f32[128,4,2048]{2,1,0:T(4,128)}), f32[128,4,2048]{2,1,0:T(4,128)}, u32[]{:S(2)}, u32[]{:S(2)}) %all-to-all-start.4) | async-done | bytes 4194336 | tf_op jit(solution)/shard_map/all_to_all | solution.py:101
  177.9 5.3 %reshape.88 = f32[512,2048]{1,0:T(8,128)} reshape(f32[128,4,2048]{2,1,0:T(4,128)} %all-to-all-done.4) | data formatting | bytes 8388608 | tf_op jit(solution)/shard_map/reshape | solution.py:102
  (8 shorter events, 0.1 us)
Async XLA Ops:
  10.6 26.1 %copy-start = (f32[8,2048]{1,0:T(8,128)S(1)}, f32[8,2048]{1,0:T(8,128)}, u32[]{:S(2)}) copy-start(f32[8,2048]{1,0:T(8,128)} %param.7) | copy-start | bytes 196612
  56.1 2.4 %copy-start.2 = (bf16[256,2048]{1,0:T(8,128)(2,1)S(1)}, bf16[256,2048]{1,0:T(8,128)(2,1)}, u32[]{:S(2)}) copy-start(bf16[256,2048]{1,0:T(8,128)(2,1)} %param.5) | copy-start | bytes 3145732
  89.0 5.4 %copy-start.1 = (s32[256,1]{0,1:T(1,128)S(1)}, s32[256,1]{0,1:T(1,128)}, u32[]{:S(2)}) copy-start(s32[256,1]{0,1:T(1,128)} %param.9) | copy-start | bytes 3076
  90.2 17.2 %all-to-all-start.3 = ((f32[16,8,2048]{2,1,0:T(8,128)}), f32[16,8,2048]{2,1,0:T(8,128)S(1)}, u32[]{:S(2)}, u32[]{:S(2)}) async-start(f32[16,8,2048]{2,1,0:T(8,128)} %broadcast_in_dim.25), calls=%async_computation.3 | async-start | bytes 2097152 | tf_op jit(solution)/shard_map/all_to_all | solution.py:21
  118.3 59.6 %all-to-all-start.4 = ((f32[128,4,2048]{2,1,0:T(4,128)}), f32[128,4,2048]{2,1,0:T(4,128)}, u32[]{:S(2)}, u32[]{:S(2)}) async-start(f32[128,4,2048]{2,1,0:T(4,128)} %copy.22), calls=%async_computation.4 | async-start | bytes 8388608 | tf_op jit(solution)/shard_map/all_to_all | solution.py:101

commit v5 on v4

--- a/solution.py
+++ b/solution.py
@@ -7,6 +7,21 @@
 
 
 step_size = 0.25
+
+
+def bf16_pieces(value):
+    high = lax.reduce_precision(value, exponent_bits=8, mantissa_bits=7)
+    rest = value - high
+    middle = lax.reduce_precision(rest, exponent_bits=8, mantissa_bits=7)
+    low = rest - middle
+    return jnp.concatenate(
+        [high.astype(jnp.bfloat16), middle.astype(jnp.bfloat16), low.astype(jnp.bfloat16)], axis=0
+    )
+
+
+def one_hot_pick(selector, table_pieces):
+    stacked = jnp.concatenate([selector.astype(jnp.bfloat16)] * 3, axis=-1)
+    return jnp.einsum("...k,kh->...h", stacked, table_pieces, preferred_element_type=jnp.float32)
 
 
 def unit_sum(partial, unit_count):
@@ -85,16 +100,9 @@
             )
         parent_gap = (county_hist - child_total) / tract_count[:, None]
         region_gap = unit_gather(parent_gap, unit_count)
-        estimate = stepped + jnp.dot(
-            member, region_gap, precision=lax.Precision.HIGHEST, preferred_element_type=jnp.float32
-        )
-    grouped = slot_stepped + jnp.einsum(
-        "osc,ch->osh",
-        slot_member,
-        region_gap,
-        precision=lax.Precision.HIGHEST,
-        preferred_element_type=jnp.float32,
-    )
+        gap_pieces = bf16_pieces(region_gap)
+        estimate = stepped + one_hot_pick(member, gap_pieces)
+    grouped = slot_stepped + one_hot_pick(slot_member, gap_pieces)
     released = jnp.dot(
         estimate.astype(jnp.bfloat16), strategy, preferred_element_type=jnp.float32
     ).astype(jnp.bfloat16)

time: 184 us -> 187 us (1.016)
  blocking collectives: 63.2 us -> 44.9 us
  waiting for transfers between devices: 49.1 us -> 66.3 us
  starting transfers between devices: 10.2 us -> 13.8 us
    all_to_all x1 -> x0, blocking collectives: 19.2 us -> none  [unit_gather(): arrived = lax.all_to_all(spread, 'unit', 0, 0, tiled=True)]
    all_to_all x1 -> x2, waiting for transfers between devices: 3.74 us -> 21 us  [unit_gather(): arrived = lax.all_to_all(spread, 'unit', 0, 0, tiled=True)]
    all_to_all x1 -> x2, starting transfers between devices: 3.84 us -> 7.49 us  [unit_gather(): arrived = lax.all_to_all(spread, 'unit', 0, 0, tiled=True)]
    dot_general x3 -> x2, matrix products: 9.69 us -> 7.13 us  [one_hot_pick(): jnp.einsum('...k,kh->...h', stacked, table_pieces, preferred_element_type...]
  transfers between devices with their start and end apart: 2 -> 3, of which waited for: 2 -> 3; matrix products, arithmetic and copies ran while one was open for 9% -> 9% of each run, Pallas kernels for 0% -> 0%
where the time goes in v5:
time: 187 us; the launch traced here: 186 us
  waiting for transfers between devices  66.3 us (35%)
  blocking collectives  44.9 us (24%)
  matrix products  34.7 us (19%)
  local copies, waits for them, and re-layouts  22.6 us (12%)
  starting transfers between devices  13.8 us (7%)
  other arithmetic  3.24 us (2%)
    all_to_all x1, waiting for transfers between devices, local(): lax.all_to_all(grouped, ('region', 'unit'), split_axis=0, concat_axis=0,...  45.4 us
    all_to_all x2, blocking collectives, unit_sum(): arrived = lax.all_to_all(grouped, 'unit', 0, 0, tiled=True)  44.9 us
    all_to_all x2, waiting for transfers between devices, unit_gather(): arrived = lax.all_to_all(spread, 'unit', 0, 0, tiled=True)  21 us
    dot_general x2, matrix products, local(): lax.dot_general(misfit, strategy, (((1,), (1,)), ((), ())), preferred_ele...  17.8 us
    dot_general x1, matrix products, local(): jnp.dot(estimate.astype(jnp.bfloat16), strategy, preferred_element_type=j...  7.87 us
    all_to_all x2, starting transfers between devices, unit_gather(): arrived = lax.all_to_all(spread, 'unit', 0, 0, tiled=True)  7.49 us
    dot_general x2, matrix products, one_hot_pick(): jnp.einsum('...k,kh->...h', stacked, table_pieces, preferred_element_type...  7.13 us
    all_to_all x1, starting transfers between devices, local(): lax.all_to_all(grouped, ('region', 'unit'), split_axis=0, concat_axis=0,...  6.33 us
  transfers between devices with their start and end apart: 3, of which 3 were waited for; matrix products, arithmetic and copies ran while one was open for 9% of the time, Pallas kernels for 0%

profile of v5, /device:TPU:6, one launch (start us, length us, event | category | flops | bytes accessed | tf_op | source)
XLA Modules:
  0.0 186.4 jit_solution(13577385721778344817)
XLA Ops:
  0.6 0.8 copy.18
  1.4 0.2 fusion.23
  1.7 0.9 fusion.25
  2.6 0.7 broadcast_add_fusion.2
  3.3 0.1 convert_reduce_fusion
  3.4 6.1 %fusion = f32[256,2048]{1,0:T(8,128)S(1)} fusion(bf16[2048,2048]{1,0:T(8,128)(2,1)} %param.6, bf16[256,2048]{1,0:T(8,128)(2,1)} %param.5), kind=kOutput, calls=%fused_computation.6 | convolution fusion | flops 2149056512 | bytes 11534336 | tf_op jit(solution)/shard_map/dot_general | solution.py:76
  9.5 0.9 fusion.27
  10.4 0.1 broadcast_in_dim.23
  10.5 0.1 maximum_bitcast_fusion
  10.6 0.0 copy-start.1
  10.6 25.9 %all_to_all.25 = f32[16,8,2176]{2,1,0:T(8,128)S(1)} all-to-all(f32[16,8,2176]{2,1,0:T(8,128)S(1)} %maximum_bitcast_fusion), channel_id=1, replica_groups=mesh['region'=8,'unit'=16] {'unit'}, dimensions={0} | all-to-all | bytes 2228224 | tf_op jit(solution)/shard_map/all_to_all | solution.py:30
  36.5 0.1 reduce_sum.48
  36.6 0.1 slice_reduce_fusion
  36.7 0.0 copy-done.1
  36.7 0.1 fusion.28
  36.8 1.1 broadcast_in_dim.24
  37.9 3.7 %all-to-all-start.1 = ((f32[16,8,2048]{2,1,0:T(8,128)}), f32[16,8,2048]{2,1,0:T(8,128)S(1)}, u32[]{:S(2)}, u32[]{:S(2)}) async-start(f32[16,8,2048]{2,1,0:T(8,128)} %broadcast_in_dim.24), calls=%async_computation.1 | async-start | bytes 2097152 | tf_op jit(solution)/shard_map/all_to_all | solution.py:36
  41.5 0.1 convert_convert_fusion.1
  41.7 15.9 %all-to-all-done.1 = f32[16,8,2048]{2,1,0:T(8,128)S(1)} async-done(((f32[16,8,2048]{2,1,0:T(8,128)}), f32[16,8,2048]{2,1,0:T(8,128)S(1)}, u32[]{:S(2)}, u32[]{:S(2)}) %all-to-all-start.1) | async-done | bytes 1048608 | tf_op jit(solution)/shard_map/all_to_all | solution.py:36
  57.6 0.3 reduce-precision_convert_fusion.3
  57.8 2.1 %convolution_add_fusion.1 = f32[256,2048]{1,0:T(8,128)} fusion(f32[256,2048]{1,0:T(8,128)S(1)} %fusion, bf16[128,2048]{1,0:T(8,128)(2,1)S(1)} %get-tuple-element.8, bf16[128,2048]{1,0:T(8,128)(2,1)S(1)} %get-tuple-element.9, bf16[128,2048]{1,0:T(8,128)(2,1)S(1)} %get-tuple-element.7, bf16[256,128]{1,0:T(8,128)(2,1)S(1)} %convert_convert_fusion.1), kind=kOutput, calls=%fused_computation.4 | convolution fusion | flops 408485888 | bytes 5832704 | tf_op jit(solution)/shard_map/...k,kh->...h/dot_general | solution.py:24
  59.9 11.8 %fusion.1 = f32[256,2048]{1,0:T(8,128)S(1)} fusion(f32[256,2048]{1,0:T(8,128)} %convolution_add_fusion.1, bf16[2048,2048]{1,0:T(8,128)(2,1)} %param.6, bf16[256,2048]{1,0:T(8,128)(2,1)} %param.5), kind=kOutput, calls=%fused_computation.7 | convolution fusion | flops 4298113024 | bytes 13631488 | tf_op jit(solution)/shard_map/dot_general | solution.py:76
  71.7 0.0 copy-start
  71.7 0.9 convolution_bitcast_fusion
  72.6 19.0 %all_to_all.26 = f32[16,8,2048]{2,1,0:T(8,128)S(1)} all-to-all(f32[16,8,2048]{2,1,0:T(8,128)S(1)} %convolution_bitcast_fusion), channel_id=1, replica_groups=mesh['region'=8,'unit'=16] {'unit'}, dimensions={0} | all-to-all | bytes 2097152 | tf_op jit(solution)/shard_map/all_to_all | solution.py:30
  91.7 0.0 copy-start.2
  91.7 0.1 reduce_sum.49
  91.7 0.1 subtract_divide_fusion
  91.8 1.1 broadcast_in_dim.25
  92.9 3.8 %all-to-all-start.3 = ((f32[16,8,2048]{2,1,0:T(8,128)}), f32[16,8,2048]{2,1,0:T(8,128)S(1)}, u32[]{:S(2)}, u32[]{:S(2)}) async-start(f32[16,8,2048]{2,1,0:T(8,128)} %broadcast_in_dim.25), calls=%async_computation.3 | async-start | bytes 2097152 | tf_op jit(solution)/shard_map/all_to_all | solution.py:36
  96.7 0.1 select_reduce_fusion
  96.9 0.1 sub.55
  97.0 0.1 copy.20
  97.1 0.0 copy-done.2
  97.1 0.1 convert_convert_fusion
  97.2 0.0 copy-done
  97.2 4.1 %scatter_custom_fusion = f32[512,2048]{1,0:T(8,128)} fusion(s32[256]{0:T(256)S(1)} %bitcast.52, f32[256,2048]{1,0:T(8,128)S(1)} %fusion.1, f32[]{:T(128)} %constant.10.clone.1), kind=kCustom, calls=%fused_computation.13 | custom fusion | bytes 4194308 | tf_op jit(solution)/shard_map/scatter | solution.py:98
  101.3 5.2 %reshape.73 = f32[128,4,2048]{2,1,0:T(4,128)} reshape(f32[512,2048]{1,0:T(8,128)} %scatter_custom_fusion) | data formatting | bytes 8388608 | tf_op jit(solution)/shard_map/reshape | solution.py:99
  106.5 5.1 %all-to-all-done.3 = f32[16,8,2048]{2,1,0:T(8,128)S(1)} async-done(((f32[16,8,2048]{2,1,0:T(8,128)}), f32[16,8,2048]{2,1,0:T(8,128)S(1)}, u32[]{:S(2)}, u32[]{:S(2)}) %all-to-all-start.3) | async-done | bytes 1048608 | tf_op jit(solution)/shard_map/all_to_all | solution.py:36
  111.5 0.3 reduce-precision_convert_fusion.1
  111.8 5.1 %copy_add_fusion = f32[128,4,2048]{2,0,1:T(8,128)S(1)} fusion(f32[128,4,2048]{2,1,0:T(4,128)} %reshape.73, bf16[128,2048]{1,0:T(8,128)(2,1)S(1)} %get-tuple-element.5, bf16[128,2048]{1,0:T(8,128)(2,1)S(1)} %get-tuple-element.6, bf16[128,2048]{1,0:T(8,128)(2,1)S(1)} %get-tuple-element.4, bf16[128,4,128]{2,0,1:T(8,128)(2,1)S(1)} %convert_convert_fusion), kind=kOutput, calls=%fused_computation.1 | convolution fusion | flops 812253184 | bytes 10092544 | tf_op jit(solution)/shard_map/...k,kh->...h/dot_general | solution.py:24
  116.9 4.7 %copy.22 = f32[128,4,2048]{2,1,0:T(4,128)} copy(f32[128,4,2048]{2,0,1:T(8,128)S(1)} %copy_add_fusion) | data formatting | bytes 8388608 | tf_op jit(solution)/shard_map/add | solution.py:105
  121.6 6.3 %all-to-all-start.4 = ((f32[128,4,2048]{2,1,0:T(4,128)}), f32[128,4,2048]{2,1,0:T(4,128)}, u32[]{:S(2)}, u32[]{:S(2)}) async-start(f32[128,4,2048]{2,1,0:T(4,128)} %copy.22), calls=%async_computation.4 | async-start | bytes 8388608 | tf_op jit(solution)/shard_map/all_to_all | solution.py:109
  127.9 7.9 %convolution_convert_fusion = bf16[256,2048]{1,0:T(8,128)(2,1)} fusion(bf16[2048,2048]{1,0:T(8,128)(2,1)} %param.6, f32[256,2048]{1,0:T(8,128)} %copy-done, bf16[128,2048]{1,0:T(8,128)(2,1)S(1)} %get-tuple-element.5, bf16[128,2048]{1,0:T(8,128)(2,1)S(1)} %get-tuple-element.6, bf16[128,2048]{1,0:T(8,128)(2,1)S(1)} %get-tuple-element.4, ...), kind=kOutput, calls=%fused_computation.11 | convolution fusion | flops 2557018112 | bytes 13172736 | tf_op jit(solution)/shard_map/dot_general | solution.py:106
  135.8 45.4 %all-to-all-done.4 = f32[128,4,2048]{2,1,0:T(4,128)} async-done(((f32[128,4,2048]{2,1,0:T(4,128)}), f32[128,4,2048]{2,1,0:T(4,128)}, u32[]{:S(2)}, u32[]{:S(2)}) %all-to-all-start.4) | async-done | bytes 4194336 | tf_op jit(solution)/shard_map/all_to_all | solution.py:109
  181.2 5.3 %reshape.74 = f32[512,2048]{1,0:T(8,128)} reshape(f32[128,4,2048]{2,1,0:T(4,128)} %all-to-all-done.4) | data formatting | bytes 8388608 | tf_op jit(solution)/shard_map/reshape | solution.py:110
  (8 shorter events, 0.1 us)
Async XLA Ops:
  10.6 26.1 %copy-start.1 = (f32[8,2048]{1,0:T(8,128)S(1)}, f32[8,2048]{1,0:T(8,128)}, u32[]{:S(2)}) copy-start(f32[8,2048]{1,0:T(8,128)} %param.7) | copy-start | bytes 196612
  37.9 19.7 %all-to-all-start.1 = ((f32[16,8,2048]{2,1,0:T(8,128)}), f32[16,8,2048]{2,1,0:T(8,128)S(1)}, u32[]{:S(2)}, u32[]{:S(2)}) async-start(f32[16,8,2048]{2,1,0:T(8,128)} %broadcast_in_dim.24), calls=%async_computation.1 | async-start | bytes 2097152 | tf_op jit(solution)/shard_map/all_to_all | solution.py:36
  71.7 25.6 %copy-start = (f32[256,2048]{1,0:T(8,128)}, f32[256,2048]{1,0:T(8,128)S(1)}, u32[]{:S(2)}) copy-start(f32[256,2048]{1,0:T(8,128)S(1)} %fusion.1) | copy-start | bytes 6291460
  91.7 5.4 %copy-start.2 = (s32[256,1]{0,1:T(1,128)S(1)}, s32[256,1]{0,1:T(1,128)}, u32[]{:S(2)}) copy-start(s32[256,1]{0,1:T(1,128)} %param.9) | copy-start | bytes 3076
  92.9 18.7 %all-to-all-start.3 = ((f32[16,8,2048]{2,1,0:T(8,128)}), f32[16,8,2048]{2,1,0:T(8,128)S(1)}, u32[]{:S(2)}, u32[]{:S(2)}) async-start(f32[16,8,2048]{2,1,0:T(8,128)} %broadcast_in_dim.25), calls=%async_computation.3 | async-start | bytes 2097152 | tf_op jit(solution)/shard_map/all_to_all | solution.py:36
  121.6 59.6 %all-to-all-start.4 = ((f32[128,4,2048]{2,1,0:T(4,128)}), f32[128,4,2048]{2,1,0:T(4,128)}, u32[]{:S(2)}, u32[]{:S(2)}) async-start(f32[128,4,2048]{2,1,0:T(4,128)} %copy.22), calls=%async_computation.4 | async-start | bytes 8388608 | tf_op jit(solution)/shard_map/all_to_all | solution.py:109

commit v6 on v5

--- a/solution.py
+++ b/solution.py
@@ -63,8 +63,9 @@
     slot_member = (
         slot_county[:, None] == jnp.arange(county_region, dtype=jnp.int32)[None, :]
     ).astype(jnp.float32).reshape(devices, capacity, county_region)
+    tally = jnp.broadcast_to(county_tally[:, None], (county_region, tally_lanes))
+    tract_count = unit_sum(tally, unit_count)[:, 0]
     estimate = jnp.zeros((tract_rows, width), jnp.float32)
-    tract_count = None
     for iteration in range(ITERS):
         if iteration == 0:
             misfit = -noisy
@@ -84,13 +85,7 @@
             precision=lax.Precision.HIGHEST,
             preferred_element_type=jnp.float32,
         )
-        if tract_count is None:
-            tally = jnp.broadcast_to(county_tally[:, None], (county_region, tally_lanes))
-            summed = unit_sum(jnp.concatenate([partial_value, tally], axis=1), unit_count)
-            child_total = summed[:, :width]
-            tract_count = summed[:, width]
-        else:
-            child_total = unit_sum(partial_value, unit_count)
+        child_total = unit_sum(partial_value, unit_count)
         if iteration == ITERS - 1:
             slot_stepped = (
                 jnp.zeros((devices * capacity, width), jnp.float32)

time: 187 us -> 195 us (1.043)
  blocking collectives: 44.9 us -> 19.4 us
  waiting for transfers between devices: 66.3 us -> 82.5 us
  starting transfers between devices: 13.8 us -> 29.3 us
    all_to_all x2 -> x1, blocking collectives: 44.9 us -> 19.4 us  [unit_sum(): arrived = lax.all_to_all(grouped, 'unit', 0, 0, tiled=True)]
    all_to_all x0 -> x2, waiting for transfers between devices: none -> 16.8 us  [unit_sum(): arrived = lax.all_to_all(grouped, 'unit', 0, 0, tiled=True)]
    all_to_all x0 -> x2, starting transfers between devices: none -> 15.4 us  [unit_sum(): arrived = lax.all_to_all(grouped, 'unit', 0, 0, tiled=True)]
  transfers between devices with their start and end apart: 3 -> 5, of which waited for: 3 -> 4; matrix products, arithmetic and copies ran while one was open for 9% -> 13% of each run, Pallas kernels for 0% -> 0%
where the time goes in v6:
time: 195 us; the launch traced here: 194 us
  waiting for transfers between devices  82.5 us (42%)
  matrix products  35.7 us (18%)
  starting transfers between devices  29.3 us (15%)
  local copies, waits for them, and re-layouts  23.3 us (12%)
  blocking collectives  19.4 us (10%)
  other arithmetic  3.17 us (2%)
    all_to_all x1, waiting for transfers between devices, local(): lax.all_to_all(grouped, ('region', 'unit'), split_axis=0, concat_axis=0,...  45.4 us
    all_to_all x2, waiting for transfers between devices, unit_gather(): arrived = lax.all_to_all(spread, 'unit', 0, 0, tiled=True)  20.4 us
    all_to_all x1, blocking collectives, unit_sum(): arrived = lax.all_to_all(grouped, 'unit', 0, 0, tiled=True)  19.4 us
    dot_general x2, matrix products, local(): lax.dot_general(misfit, strategy, (((1,), (1,)), ((), ())), preferred_ele...  17.8 us
    all_to_all x2, waiting for transfers between devices, unit_sum(): arrived = lax.all_to_all(grouped, 'unit', 0, 0, tiled=True)  16.8 us
    all_to_all x2, starting transfers between devices, unit_sum(): arrived = lax.all_to_all(grouped, 'unit', 0, 0, tiled=True)  15.4 us
    dot_general x1, matrix products, local(): jnp.dot(estimate.astype(jnp.bfloat16), strategy, preferred_element_type=j...  7.87 us
    all_to_all x2, starting transfers between devices, unit_gather(): arrived = lax.all_to_all(spread, 'unit', 0, 0, tiled=True)  7.49 us
  transfers between devices with their start and end apart: 5, of which 4 were waited for; matrix products, arithmetic and copies ran while one was open for 13% of the time, Pallas kernels for 0%

profile of v6, /device:TPU:6, one launch (start us, length us, event | category | flops | bytes accessed | tf_op | source)
XLA Modules:
  0.0 194.2 jit_solution(8334938608759356546)
XLA Ops:
  0.6 0.8 copy.23
  1.4 0.2 fusion.23
  1.7 0.9 fusion.25
  2.6 0.7 broadcast_add_fusion.2
  3.3 0.1 convert_reduce_fusion
  3.4 0.1 broadcast_in_dim.25
  3.5 0.7 broadcast_in_dim.26
  4.2 8.0 %all-to-all-start.1 = ((f32[16,8,128]{2,1,0:T(8,128)}), f32[16,8,128]{2,1,0:T(8,128)S(1)}, u32[]{:S(2)}, u32[]{:S(2)}) async-start(f32[16,8,128]{2,1,0:T(8,128)} %broadcast_in_dim.26), calls=%async_computation.1 | async-start | bytes 131072 | tf_op jit(solution)/shard_map/all_to_all | solution.py:30
  12.3 6.1 %fusion = f32[256,2048]{1,0:T(8,128)S(1)} fusion(bf16[2048,2048]{1,0:T(8,128)(2,1)} %param.6, bf16[256,2048]{1,0:T(8,128)(2,1)} %param.5), kind=kOutput, calls=%fused_computation.6 | convolution fusion | flops 2149056512 | bytes 11534336 | tf_op jit(solution)/shard_map/dot_general | solution.py:77
  18.4 1.9 convolution_bitcast_fusion.1
  20.3 0.0 copy-start.1
  20.3 0.0 all-to-all-done.1
  20.3 7.4 %all-to-all-start = ((f32[16,8,2048]{2,1,0:T(8,128)}), f32[16,8,2048]{2,1,0:T(8,128)S(1)}, u32[]{:S(2)}, u32[]{:S(2)}) async-start(f32[16,8,2048]{2,1,0:T(8,128)} %convolution_bitcast_fusion.1), calls=%async_computation | async-start | bytes 2097152 | tf_op jit(solution)/shard_map/all_to_all | solution.py:30
  27.7 0.1 slice_reduce_fusion
  27.8 16.8 %all-to-all-done = f32[16,8,2048]{2,1,0:T(8,128)S(1)} async-done(((f32[16,8,2048]{2,1,0:T(8,128)}), f32[16,8,2048]{2,1,0:T(8,128)S(1)}, u32[]{:S(2)}, u32[]{:S(2)}) %all-to-all-start) | async-done | bytes 1048608 | tf_op jit(solution)/shard_map/all_to_all | solution.py:30
  44.5 0.1 reduce_sum.56
  44.6 0.0 copy-done.1
  44.6 0.1 subtract_divide_fusion.1
  44.7 1.1 broadcast_in_dim.27
  45.8 3.7 %all-to-all-start.2 = ((f32[16,8,2048]{2,1,0:T(8,128)}), f32[16,8,2048]{2,1,0:T(8,128)S(1)}, u32[]{:S(2)}, u32[]{:S(2)}) async-start(f32[16,8,2048]{2,1,0:T(8,128)} %broadcast_in_dim.27), calls=%async_computation.2 | async-start | bytes 2097152 | tf_op jit(solution)/shard_map/all_to_all | solution.py:36
  49.4 0.1 convert_convert_fusion.1
  49.5 15.3 %all-to-all-done.2 = f32[16,8,2048]{2,1,0:T(8,128)S(1)} async-done(((f32[16,8,2048]{2,1,0:T(8,128)}), f32[16,8,2048]{2,1,0:T(8,128)S(1)}, u32[]{:S(2)}, u32[]{:S(2)}) %all-to-all-start.2) | async-done | bytes 1048608 | tf_op jit(solution)/shard_map/all_to_all | solution.py:36
  64.8 0.3 reduce-precision_convert_fusion.3
  65.1 2.1 %convolution_add_fusion.1 = f32[256,2048]{1,0:T(8,128)} fusion(f32[256,2048]{1,0:T(8,128)S(1)} %fusion, bf16[128,2048]{1,0:T(8,128)(2,1)S(1)} %get-tuple-element.8, bf16[128,2048]{1,0:T(8,128)(2,1)S(1)} %get-tuple-element.9, bf16[128,2048]{1,0:T(8,128)(2,1)S(1)} %get-tuple-element.7, bf16[256,128]{1,0:T(8,128)(2,1)S(1)} %convert_convert_fusion.1), kind=kOutput, calls=%fused_computation.4 | convolution fusion | flops 408485888 | bytes 5832704 | tf_op jit(solution)/shard_map/...k,kh->...h/dot_general | solution.py:24
  67.1 11.8 %fusion.1 = f32[256,2048]{1,0:T(8,128)S(1)} fusion(f32[256,2048]{1,0:T(8,128)} %convolution_add_fusion.1, bf16[2048,2048]{1,0:T(8,128)(2,1)} %param.6, bf16[256,2048]{1,0:T(8,128)(2,1)} %param.5), kind=kOutput, calls=%fused_computation.7 | convolution fusion | flops 4298113024 | bytes 13631488 | tf_op jit(solution)/shard_map/dot_general | solution.py:77
  78.9 0.0 copy-start
  78.9 0.9 convolution_bitcast_fusion
  79.9 19.4 %all_to_all.30 = f32[16,8,2048]{2,1,0:T(8,128)S(1)} all-to-all(f32[16,8,2048]{2,1,0:T(8,128)S(1)} %convolution_bitcast_fusion), channel_id=1, replica_groups=mesh['region'=8,'unit'=16] {'unit'}, dimensions={0} | all-to-all | bytes 2097152 | tf_op jit(solution)/shard_map/all_to_all | solution.py:30
  99.2 0.0 copy-start.2
  99.2 0.1 reduce_sum.59
  99.3 0.1 subtract_divide_fusion
  99.4 1.1 broadcast_in_dim.28
  100.4 3.8 %all-to-all-start.4 = ((f32[16,8,2048]{2,1,0:T(8,128)}), f32[16,8,2048]{2,1,0:T(8,128)S(1)}, u32[]{:S(2)}, u32[]{:S(2)}) async-start(f32[16,8,2048]{2,1,0:T(8,128)} %broadcast_in_dim.28), calls=%async_computation.4 | async-start | bytes 2097152 | tf_op jit(solution)/shard_map/all_to_all | solution.py:36
  104.3 0.1 select_reduce_fusion
  104.5 0.1 sub.55
  104.6 0.1 copy.25
  104.6 0.0 copy-done.2
  104.6 0.1 convert_convert_fusion
  104.8 0.0 copy-done
  104.8 4.1 %scatter_custom_fusion = f32[512,2048]{1,0:T(8,128)} fusion(s32[256]{0:T(256)S(1)} %bitcast.52, f32[256,2048]{1,0:T(8,128)S(1)} %fusion.1, f32[]{:T(128)} %constant.10.clone.1), kind=kCustom, calls=%fused_computation.14 | custom fusion | bytes 4194308 | tf_op jit(solution)/shard_map/scatter | solution.py:93
  108.9 5.2 %reshape.79 = f32[128,4,2048]{2,1,0:T(4,128)} reshape(f32[512,2048]{1,0:T(8,128)} %scatter_custom_fusion) | data formatting | bytes 8388608 | tf_op jit(solution)/shard_map/reshape | solution.py:94
  114.1 5.1 %all-to-all-done.4 = f32[16,8,2048]{2,1,0:T(8,128)S(1)} async-done(((f32[16,8,2048]{2,1,0:T(8,128)}), f32[16,8,2048]{2,1,0:T(8,128)S(1)}, u32[]{:S(2)}, u32[]{:S(2)}) %all-to-all-start.4) | async-done | bytes 1048608 | tf_op jit(solution)/shard_map/all_to_all | solution.py:36
  119.2 0.3 reduce-precision_convert_fusion.1
  119.4 5.1 %copy_add_fusion = f32[128,4,2048]{2,0,1:T(8,128)S(1)} fusion(f32[128,4,2048]{2,1,0:T(4,128)} %reshape.79, bf16[128,2048]{1,0:T(8,128)(2,1)S(1)} %get-tuple-element.5, bf16[128,2048]{1,0:T(8,128)(2,1)S(1)} %get-tuple-element.6, bf16[128,2048]{1,0:T(8,128)(2,1)S(1)} %get-tuple-element.4, bf16[128,4,128]{2,0,1:T(8,128)(2,1)S(1)} %convert_convert_fusion), kind=kOutput, calls=%fused_computation.1 | convolution fusion | flops 812253184 | bytes 10092544 | tf_op jit(solution)/shard_map/...k,kh->...h/dot_general | solution.py:24
  124.5 4.7 %copy.27 = f32[128,4,2048]{2,1,0:T(4,128)} copy(f32[128,4,2048]{2,0,1:T(8,128)S(1)} %copy_add_fusion) | data formatting | bytes 8388608 | tf_op jit(solution)/shard_map/add | solution.py:100
  129.2 6.4 %all-to-all-start.5 = ((f32[128,4,2048]{2,1,0:T(4,128)}), f32[128,4,2048]{2,1,0:T(4,128)}, u32[]{:S(2)}, u32[]{:S(2)}) async-start(f32[128,4,2048]{2,1,0:T(4,128)} %copy.27), calls=%async_computation.5 | async-start | bytes 8388608 | tf_op jit(solution)/shard_map/all_to_all | solution.py:104
  135.7 7.9 %convolution_convert_fusion = bf16[256,2048]{1,0:T(8,128)(2,1)} fusion(bf16[2048,2048]{1,0:T(8,128)(2,1)} %param.6, f32[256,2048]{1,0:T(8,128)} %copy-done, bf16[128,2048]{1,0:T(8,128)(2,1)S(1)} %get-tuple-element.5, bf16[128,2048]{1,0:T(8,128)(2,1)S(1)} %get-tuple-element.6, bf16[128,2048]{1,0:T(8,128)(2,1)S(1)} %get-tuple-element.4, ...), kind=kOutput, calls=%fused_computation.11 | convolution fusion | flops 2557018112 | bytes 13172736 | tf_op jit(solution)/shard_map/dot_general | solution.py:101
  143.5 45.4 %all-to-all-done.5 = f32[128,4,2048]{2,1,0:T(4,128)} async-done(((f32[128,4,2048]{2,1,0:T(4,128)}), f32[128,4,2048]{2,1,0:T(4,128)}, u32[]{:S(2)}, u32[]{:S(2)}) %all-to-all-start.5) | async-done | bytes 4194336 | tf_op jit(solution)/shard_map/all_to_all | solution.py:104
  188.9 5.3 %reshape.80 = f32[512,2048]{1,0:T(8,128)} reshape(f32[128,4,2048]{2,1,0:T(4,128)} %all-to-all-done.5) | data formatting | bytes 8388608 | tf_op jit(solution)/shard_map/reshape | solution.py:105
  (9 shorter events, 0.1 us)
Async XLA Ops:
  4.2 16.1 %all-to-all-start.1 = ((f32[16,8,128]{2,1,0:T(8,128)}), f32[16,8,128]{2,1,0:T(8,128)S(1)}, u32[]{:S(2)}, u32[]{:S(2)}) async-start(f32[16,8,128]{2,1,0:T(8,128)} %broadcast_in_dim.26), calls=%async_computation.1 | async-start | bytes 131072 | tf_op jit(solution)/shard_map/all_to_all | solution.py:30
  20.3 24.3 %copy-start.1 = (f32[8,2048]{1,0:T(8,128)S(1)}, f32[8,2048]{1,0:T(8,128)}, u32[]{:S(2)}) copy-start(f32[8,2048]{1,0:T(8,128)} %param.7) | copy-start | bytes 196612
  20.3 24.3 %all-to-all-start = ((f32[16,8,2048]{2,1,0:T(8,128)}), f32[16,8,2048]{2,1,0:T(8,128)S(1)}, u32[]{:S(2)}, u32[]{:S(2)}) async-start(f32[16,8,2048]{2,1,0:T(8,128)} %convolution_bitcast_fusion.1), calls=%async_computation | async-start | bytes 2097152 | tf_op jit(solution)/shard_map/all_to_all | solution.py:30
  45.8 19.0 %all-to-all-start.2 = ((f32[16,8,2048]{2,1,0:T(8,128)}), f32[16,8,2048]{2,1,0:T(8,128)S(1)}, u32[]{:S(2)}, u32[]{:S(2)}) async-start(f32[16,8,2048]{2,1,0:T(8,128)} %broadcast_in_dim.27), calls=%async_computation.2 | async-start | bytes 2097152 | tf_op jit(solution)/shard_map/all_to_all | solution.py:36
  78.9 25.9 %copy-start = (f32[256,2048]{1,0:T(8,128)}, f32[256,2048]{1,0:T(8,128)S(1)}, u32[]{:S(2)}) copy-start(f32[256,2048]{1,0:T(8,128)S(1)} %fusion.1) | copy-start | bytes 6291460
  99.2 5.4 %copy-start.2 = (s32[256,1]{0,1:T(1,128)S(1)}, s32[256,1]{0,1:T(1,128)}, u32[]{:S(2)}) copy-start(s32[256,1]{0,1:T(1,128)} %param.9) | copy-start | bytes 3076
  100.4 18.7 %all-to-all-start.4 = ((f32[16,8,2048]{2,1,0:T(8,128)}), f32[16,8,2048]{2,1,0:T(8,128)S(1)}, u32[]{:S(2)}, u32[]{:S(2)}) async-start(f32[16,8,2048]{2,1,0:T(8,128)} %broadcast_in_dim.28), calls=%async_computation.4 | async-start | bytes 2097152 | tf_op jit(solution)/shard_map/all_to_all | solution.py:36
  129.2 59.7 %all-to-all-start.5 = ((f32[128,4,2048]{2,1,0:T(4,128)}), f32[128,4,2048]{2,1,0:T(4,128)}, u32[]{:S(2)}, u32[]{:S(2)}) async-start(f32[128,4,2048]{2,1,0:T(4,128)} %copy.27), calls=%async_computation.5 | async-start | bytes 8388608 | tf_op jit(solution)/shard_map/all_to_all | solution.py:104

commit v7 on v5

--- a/solution.py
+++ b/solution.py
@@ -51,18 +51,6 @@
     )
     county_tally = jnp.sum(member, axis=0)
     tally_lanes = 128
-    owners = tract_owner[:, 0]
-    owner_hits = (owners[:, None] == jnp.arange(devices, dtype=jnp.int32)[None, :]).astype(
-        jnp.int32
-    )
-    slot_index = jnp.sum((jnp.cumsum(owner_hits, axis=0) - owner_hits) * owner_hits, axis=1)
-    capacity = 2 * tract_rows // devices
-    target = owners * capacity + slot_index
-    slot_hits = target[None, :] == jnp.arange(devices * capacity, dtype=jnp.int32)[:, None]
-    slot_county = jnp.sum(jnp.where(slot_hits, local_id[None, :] + 1, 0), axis=1) - 1
-    slot_member = (
-        slot_county[:, None] == jnp.arange(county_region, dtype=jnp.int32)[None, :]
-    ).astype(jnp.float32).reshape(devices, capacity, county_region)
     estimate = jnp.zeros((tract_rows, width), jnp.float32)
     tract_count = None
     for iteration in range(ITERS):
@@ -92,6 +80,23 @@
         else:
             child_total = unit_sum(partial_value, unit_count)
         if iteration == ITERS - 1:
+            late_owner, child_total = lax.optimization_barrier((tract_owner, child_total))
+            owners = late_owner[:, 0]
+            owner_hits = (
+                owners[:, None] == jnp.arange(devices, dtype=jnp.int32)[None, :]
+            ).astype(jnp.int32)
+            slot_index = jnp.sum(
+                (jnp.cumsum(owner_hits, axis=0) - owner_hits) * owner_hits, axis=1
+            )
+            capacity = 2 * tract_rows // devices
+            target = owners * capacity + slot_index
+            slot_hits = (
+                target[None, :] == jnp.arange(devices * capacity, dtype=jnp.int32)[:, None]
+            )
+            slot_county = jnp.sum(jnp.where(slot_hits, local_id[None, :] + 1, 0), axis=1) - 1
+            slot_member = (
+                slot_county[:, None] == jnp.arange(county_region, dtype=jnp.int32)[None, :]
+            ).astype(jnp.float32).reshape(devices, capacity, county_region)
             slot_stepped = (
                 jnp.zeros((devices * capacity, width), jnp.float32)
                 .at[target]

time: 187 us -> 186 us (level)
  transfers between devices with their start and end apart: 3 -> 3, of which waited for: 3 -> 3; matrix products, arithmetic and copies ran while one was open for 9% -> 10% of each run, Pallas kernels for 0% -> 0%
where the time goes in v7:
time: 186 us; the launch traced here: 185 us
  waiting for transfers between devices  66.1 us (36%)
  blocking collectives  44.9 us (24%)
  matrix products  34.7 us (19%)
  local copies, waits for them, and re-layouts  21.9 us (12%)
  starting transfers between devices  13.9 us (7%)
  other arithmetic  2.54 us (1%)
    all_to_all x1, waiting for transfers between devices, local(): lax.all_to_all(grouped, ('region', 'unit'), split_axis=0, concat_axis=0,...  45.4 us
    all_to_all x2, blocking collectives, unit_sum(): arrived = lax.all_to_all(grouped, 'unit', 0, 0, tiled=True)  44.9 us
    all_to_all x2, waiting for transfers between devices, unit_gather(): arrived = lax.all_to_all(spread, 'unit', 0, 0, tiled=True)  20.8 us
    dot_general x2, matrix products, local(): lax.dot_general(misfit, strategy, (((1,), (1,)), ((), ())), preferred_ele...  17.8 us
    dot_general x1, matrix products, local(): jnp.dot(estimate.astype(jnp.bfloat16), strategy, preferred_element_type=j...  7.87 us
    all_to_all x2, starting transfers between devices, unit_gather(): arrived = lax.all_to_all(spread, 'unit', 0, 0, tiled=True)  7.49 us
    dot_general x2, matrix products, one_hot_pick(): jnp.einsum('...k,kh->...h', stacked, table_pieces, preferred_element_type...  7.13 us
    all_to_all x1, starting transfers between devices, local(): lax.all_to_all(grouped, ('region', 'unit'), split_axis=0, concat_axis=0,...  6.44 us
  transfers between devices with their start and end apart: 3, of which 3 were waited for; matrix products, arithmetic and copies ran while one was open for 10% of the time, Pallas kernels for 0%

profile of v7, /device:TPU:6, one launch (start us, length us, event | category | flops | bytes accessed | tf_op | source)
XLA Modules:
  0.0 185.0 jit_solution(9675358051058000651)
XLA Ops:
  0.6 0.7 broadcast_add_fusion.2
  1.3 0.1 convert_reduce_fusion
  1.4 6.1 %fusion = f32[256,2048]{1,0:T(8,128)S(1)} fusion(bf16[2048,2048]{1,0:T(8,128)(2,1)} %param.6, bf16[256,2048]{1,0:T(8,128)(2,1)} %param.5), kind=kOutput, calls=%fused_computation.6 | convolution fusion | flops 2149056512 | bytes 11534336 | tf_op jit(solution)/shard_map/dot_general | solution.py:64
  7.5 0.9 fusion.27
  8.5 0.1 broadcast_in_dim.19
  8.5 0.1 maximum_bitcast_fusion
  8.6 0.0 copy-start.1
  8.7 25.9 %all_to_all.25 = f32[16,8,2176]{2,1,0:T(8,128)S(1)} all-to-all(f32[16,8,2176]{2,1,0:T(8,128)S(1)} %maximum_bitcast_fusion), channel_id=1, replica_groups=mesh['region'=8,'unit'=16] {'unit'}, dimensions={0} | all-to-all | bytes 2228224 | tf_op jit(solution)/shard_map/all_to_all | solution.py:30
  34.6 0.1 reduce_sum.48
  34.6 0.1 slice_reduce_fusion
  34.7 0.0 copy-done.1
  34.7 0.1 fusion.28
  34.8 1.1 broadcast_in_dim.24
  35.9 3.7 %all-to-all-start.1 = ((f32[16,8,2048]{2,1,0:T(8,128)}), f32[16,8,2048]{2,1,0:T(8,128)S(1)}, u32[]{:S(2)}, u32[]{:S(2)}) async-start(f32[16,8,2048]{2,1,0:T(8,128)} %broadcast_in_dim.24), calls=%async_computation.1 | async-start | bytes 2097152 | tf_op jit(solution)/shard_map/all_to_all | solution.py:36
  39.6 0.1 convert_convert_fusion.1
  39.7 15.9 %all-to-all-done.1 = f32[16,8,2048]{2,1,0:T(8,128)S(1)} async-done(((f32[16,8,2048]{2,1,0:T(8,128)}), f32[16,8,2048]{2,1,0:T(8,128)S(1)}, u32[]{:S(2)}, u32[]{:S(2)}) %all-to-all-start.1) | async-done | bytes 1048608 | tf_op jit(solution)/shard_map/all_to_all | solution.py:36
  55.6 0.3 reduce-precision_convert_fusion.3
  55.9 2.1 %convolution_add_fusion.1 = f32[256,2048]{1,0:T(8,128)} fusion(f32[256,2048]{1,0:T(8,128)S(1)} %fusion, bf16[128,2048]{1,0:T(8,128)(2,1)S(1)} %get-tuple-element.12, bf16[128,2048]{1,0:T(8,128)(2,1)S(1)} %get-tuple-element.13, bf16[128,2048]{1,0:T(8,128)(2,1)S(1)} %get-tuple-element.11, bf16[256,128]{1,0:T(8,128)(2,1)S(1)} %convert_convert_fusion.1), kind=kOutput, calls=%fused_computation.4 | convolution fusion | flops 408485888 | bytes 5832704 | tf_op jit(solution)/shard_map/...k,kh->...h/dot_general | solution.py:24
  57.9 11.8 %fusion.1 = f32[256,2048]{1,0:T(8,128)S(1)} fusion(f32[256,2048]{1,0:T(8,128)} %convolution_add_fusion.1, bf16[2048,2048]{1,0:T(8,128)(2,1)} %param.6, bf16[256,2048]{1,0:T(8,128)(2,1)} %param.5), kind=kOutput, calls=%fused_computation.7 | convolution fusion | flops 4298113024 | bytes 13631488 | tf_op jit(solution)/shard_map/dot_general | solution.py:64
  69.7 0.0 copy-start
  69.7 0.9 convolution_bitcast_fusion
  70.6 0.0 copy-start.2
  70.7 19.0 %all_to_all.26 = f32[16,8,2048]{2,1,0:T(8,128)S(1)} all-to-all(f32[16,8,2048]{2,1,0:T(8,128)S(1)} %convolution_bitcast_fusion), channel_id=1, replica_groups=mesh['region'=8,'unit'=16] {'unit'}, dimensions={0} | all-to-all | bytes 2097152 | tf_op jit(solution)/shard_map/all_to_all | solution.py:30
  89.7 0.1 reduce_sum.49
  89.7 0.1 subtract_divide_fusion
  89.8 0.0 copy-done.2
  89.8 0.1 copy.18
  89.9 0.2 fusion.23
  90.3 1.1 broadcast_in_dim.25
  91.3 3.8 %all-to-all-start.3 = ((f32[16,8,2048]{2,1,0:T(8,128)}), f32[16,8,2048]{2,1,0:T(8,128)S(1)}, u32[]{:S(2)}, u32[]{:S(2)}) async-start(f32[16,8,2048]{2,1,0:T(8,128)} %broadcast_in_dim.25), calls=%async_computation.3 | async-start | bytes 2097152 | tf_op jit(solution)/shard_map/all_to_all | solution.py:36
  95.2 0.2 fusion.25
  95.4 0.2 select_reduce_fusion
  95.5 0.1 sub.55
  95.6 0.1 copy.20
  95.7 0.0 copy-done
  95.7 4.1 %scatter_custom_fusion = f32[512,2048]{1,0:T(8,128)} fusion(s32[256]{0:T(256)S(1)} %bitcast.52, f32[256,2048]{1,0:T(8,128)S(1)} %fusion.1, f32[]{:T(128)} %constant.10.clone.1), kind=kCustom, calls=%fused_computation.13 | custom fusion | bytes 4194308 | tf_op jit(solution)/shard_map/scatter | solution.py:103
  99.8 5.2 %reshape.73 = f32[128,4,2048]{2,1,0:T(4,128)} reshape(f32[512,2048]{1,0:T(8,128)} %scatter_custom_fusion) | data formatting | bytes 8388608 | tf_op jit(solution)/shard_map/reshape | solution.py:104
  105.0 0.1 convert_convert_fusion
  105.1 4.9 %all-to-all-done.3 = f32[16,8,2048]{2,1,0:T(8,128)S(1)} async-done(((f32[16,8,2048]{2,1,0:T(8,128)}), f32[16,8,2048]{2,1,0:T(8,128)S(1)}, u32[]{:S(2)}, u32[]{:S(2)}) %all-to-all-start.3) | async-done | bytes 1048608 | tf_op jit(solution)/shard_map/all_to_all | solution.py:36
  110.0 0.3 reduce-precision_convert_fusion.1
  110.3 5.1 %copy_add_fusion = f32[128,4,2048]{2,0,1:T(8,128)S(1)} fusion(f32[128,4,2048]{2,1,0:T(4,128)} %reshape.73, bf16[128,2048]{1,0:T(8,128)(2,1)S(1)} %get-tuple-element.9, bf16[128,2048]{1,0:T(8,128)(2,1)S(1)} %get-tuple-element.10, bf16[128,2048]{1,0:T(8,128)(2,1)S(1)} %get-tuple-element.8, bf16[128,4,128]{2,0,1:T(8,128)(2,1)S(1)} %convert_convert_fusion), kind=kOutput, calls=%fused_computation.1 | convolution fusion | flops 812253184 | bytes 10092544 | tf_op jit(solution)/shard_map/...k,kh->...h/dot_general | solution.py:24
  115.3 4.7 %copy.22 = f32[128,4,2048]{2,1,0:T(4,128)} copy(f32[128,4,2048]{2,0,1:T(8,128)S(1)} %copy_add_fusion) | data formatting | bytes 8388608 | tf_op jit(solution)/shard_map/add | solution.py:110
  120.0 6.4 %all-to-all-start.4 = ((f32[128,4,2048]{2,1,0:T(4,128)}), f32[128,4,2048]{2,1,0:T(4,128)}, u32[]{:S(2)}, u32[]{:S(2)}) async-start(f32[128,4,2048]{2,1,0:T(4,128)} %copy.22), calls=%async_computation.4 | async-start | bytes 8388608 | tf_op jit(solution)/shard_map/all_to_all | solution.py:114
  126.5 7.9 %convolution_convert_fusion = bf16[256,2048]{1,0:T(8,128)(2,1)} fusion(bf16[2048,2048]{1,0:T(8,128)(2,1)} %param.6, f32[256,2048]{1,0:T(8,128)} %copy-done, bf16[128,2048]{1,0:T(8,128)(2,1)S(1)} %get-tuple-element.9, bf16[128,2048]{1,0:T(8,128)(2,1)S(1)} %get-tuple-element.10, bf16[128,2048]{1,0:T(8,128)(2,1)S(1)} %get-tuple-element.8, ...), kind=kOutput, calls=%fused_computation.11 | convolution fusion | flops 2557018112 | bytes 13172736 | tf_op jit(solution)/shard_map/dot_general | solution.py:111
  134.4 45.4 %all-to-all-done.4 = f32[128,4,2048]{2,1,0:T(4,128)} async-done(((f32[128,4,2048]{2,1,0:T(4,128)}), f32[128,4,2048]{2,1,0:T(4,128)}, u32[]{:S(2)}, u32[]{:S(2)}) %all-to-all-start.4) | async-done | bytes 4194336 | tf_op jit(solution)/shard_map/all_to_all | solution.py:114
  179.7 5.3 %reshape.74 = f32[512,2048]{1,0:T(8,128)} reshape(f32[128,4,2048]{2,1,0:T(4,128)} %all-to-all-done.4) | data formatting | bytes 8388608 | tf_op jit(solution)/shard_map/reshape | solution.py:115
  (9 shorter events, 0.1 us)
Async XLA Ops:
  8.6 26.1 %copy-start.1 = (f32[8,2048]{1,0:T(8,128)S(1)}, f32[8,2048]{1,0:T(8,128)}, u32[]{:S(2)}) copy-start(f32[8,2048]{1,0:T(8,128)} %param.7) | copy-start | bytes 196612
  35.9 19.7 %all-to-all-start.1 = ((f32[16,8,2048]{2,1,0:T(8,128)}), f32[16,8,2048]{2,1,0:T(8,128)S(1)}, u32[]{:S(2)}, u32[]{:S(2)}) async-start(f32[16,8,2048]{2,1,0:T(8,128)} %broadcast_in_dim.24), calls=%async_computation.1 | async-start | bytes 2097152 | tf_op jit(solution)/shard_map/all_to_all | solution.py:36
  69.7 26.0 %copy-start = (f32[256,2048]{1,0:T(8,128)}, f32[256,2048]{1,0:T(8,128)S(1)}, u32[]{:S(2)}) copy-start(f32[256,2048]{1,0:T(8,128)S(1)} %fusion.1) | copy-start | bytes 6291460
  70.6 19.2 %copy-start.2 = (s32[256,1]{0,1:T(1,128)S(1)}, s32[256,1]{0,1:T(1,128)}, u32[]{:S(2)}) copy-start(s32[256,1]{0,1:T(1,128)} %param.9) | copy-start | bytes 3076
  91.3 18.7 %all-to-all-start.3 = ((f32[16,8,2048]{2,1,0:T(8,128)}), f32[16,8,2048]{2,1,0:T(8,128)S(1)}, u32[]{:S(2)}, u32[]{:S(2)}) async-start(f32[16,8,2048]{2,1,0:T(8,128)} %broadcast_in_dim.25), calls=%async_computation.3 | async-start | bytes 2097152 | tf_op jit(solution)/shard_map/all_to_all | solution.py:36
  120.0 59.7 %all-to-all-start.4 = ((f32[128,4,2048]{2,1,0:T(4,128)}), f32[128,4,2048]{2,1,0:T(4,128)}, u32[]{:S(2)}, u32[]{:S(2)}) async-start(f32[128,4,2048]{2,1,0:T(4,128)} %copy.22), calls=%async_computation.4 | async-start | bytes 8388608 | tf_op jit(solution)/shard_map/all_to_all | solution.py:114

commit v8 on v7

--- a/solution.py
+++ b/solution.py
@@ -7,21 +7,6 @@
 
 
 step_size = 0.25
-
-
-def bf16_pieces(value):
-    high = lax.reduce_precision(value, exponent_bits=8, mantissa_bits=7)
-    rest = value - high
-    middle = lax.reduce_precision(rest, exponent_bits=8, mantissa_bits=7)
-    low = rest - middle
-    return jnp.concatenate(
-        [high.astype(jnp.bfloat16), middle.astype(jnp.bfloat16), low.astype(jnp.bfloat16)], axis=0
-    )
-
-
-def one_hot_pick(selector, table_pieces):
-    stacked = jnp.concatenate([selector.astype(jnp.bfloat16)] * 3, axis=-1)
-    return jnp.einsum("...k,kh->...h", stacked, table_pieces, preferred_element_type=jnp.float32)
 
 
 def unit_sum(partial, unit_count):
@@ -105,9 +90,16 @@
             )
         parent_gap = (county_hist - child_total) / tract_count[:, None]
         region_gap = unit_gather(parent_gap, unit_count)
-        gap_pieces = bf16_pieces(region_gap)
-        estimate = stepped + one_hot_pick(member, gap_pieces)
-    grouped = slot_stepped + one_hot_pick(slot_member, gap_pieces)
+        estimate = stepped + jnp.dot(
+            member, region_gap, precision=lax.Precision.HIGHEST, preferred_element_type=jnp.float32
+        )
+    grouped = slot_stepped + jnp.einsum(
+        "osc,ch->osh",
+        slot_member,
+        region_gap,
+        precision=lax.Precision.HIGHEST,
+        preferred_element_type=jnp.float32,
+    )
     released = jnp.dot(
         estimate.astype(jnp.bfloat16), strategy, preferred_element_type=jnp.float32
     ).astype(jnp.bfloat16)

time: 186 us -> 182 us (0.978)
  blocking collectives: 44.9 us -> 63.2 us
  waiting for transfers between devices: 66.1 us -> 48.9 us
  starting transfers between devices: 13.9 us -> 10.2 us
    all_to_all x0 -> x1, blocking collectives: none -> 19.2 us  [unit_gather(): arrived = lax.all_to_all(spread, 'unit', 0, 0, tiled=True)]
    all_to_all x2 -> x1, waiting for transfers between devices: 20.8 us -> 3.49 us  [unit_gather(): arrived = lax.all_to_all(spread, 'unit', 0, 0, tiled=True)]
    all_to_all x2 -> x1, starting transfers between devices: 7.49 us -> 3.84 us  [unit_gather(): arrived = lax.all_to_all(spread, 'unit', 0, 0, tiled=True)]
    dot_general x2 -> x3, matrix products: 7.13 us -> 9.69 us  [the longest x1 6.26 us: local(): jnp.einsum('osc,ch->osh', slot_member, region_gap, precision=lax.Precisio...]
  transfers between devices with their start and end apart: 3 -> 2, of which waited for: 3 -> 2; matrix products, arithmetic and copies ran while one was open for 10% -> 10% of each run, Pallas kernels for 0% -> 0%
where the time goes in v8:
time: 182 us
  blocking collectives  63.2 us (35%)
  waiting for transfers between devices  48.9 us (27%)
  matrix products  35.8 us (20%)
  local copies, waits for them, and re-layouts  20.9 us (11%)
  starting transfers between devices  10.2 us (6%)
    all_to_all x1, waiting for transfers between devices, local(): lax.all_to_all(grouped, ('region', 'unit'), split_axis=0, concat_axis=0,...  45.4 us
    all_to_all x2, blocking collectives, unit_sum(): arrived = lax.all_to_all(grouped, 'unit', 0, 0, tiled=True)  43.9 us
    all_to_all x1, blocking collectives, unit_gather(): arrived = lax.all_to_all(spread, 'unit', 0, 0, tiled=True)  19.2 us
    dot_general x2, matrix products, local(): lax.dot_general(misfit, strategy, (((1,), (1,)), ((), ())), preferred_ele...  17.6 us
    dot_general x1, matrix products, local(): jnp.dot(estimate.astype(jnp.bfloat16), strategy, preferred_element_type=j...  6.71 us
    all_to_all x1, starting transfers between devices, local(): lax.all_to_all(grouped, ('region', 'unit'), split_axis=0, concat_axis=0,...  6.37 us
    dot_general x1, matrix products, local(): jnp.einsum('osc,ch->osh', slot_member, region_gap, precision=lax.Precisio...  6.26 us
    reshape x1, local copies, waits for them, and re-layouts, local(): relaid = arrived.reshape(devices * capacity, width)  5.27 us
  transfers between devices with their start and end apart: 2, of which 2 were waited for; matrix products, arithmetic and copies ran while one was open for 10% of the time, Pallas kernels for 0%

profile of v8, /device:TPU:6, one launch (start us, length us, event | category | flops | bytes accessed | tf_op | source)
XLA Modules:
  0.0 181.6 jit_solution(2815768364366212899)
XLA Ops:
  0.6 0.7 broadcast_add_fusion.2
  1.3 0.1 convert_reduce_fusion
  1.4 6.1 %fusion = f32[256,2048]{1,0:T(8,128)S(1)} fusion(bf16[2048,2048]{1,0:T(8,128)(2,1)} %param.6, bf16[256,2048]{1,0:T(8,128)(2,1)} %param.5), kind=kOutput, calls=%fused_computation.6 | convolution fusion | flops 2149056512 | bytes 11534336 | tf_op jit(solution)/shard_map/dot_general | solution.py:49
  7.5 0.9 fusion.20
  8.5 0.1 broadcast_in_dim.19
  8.5 0.1 maximum_bitcast_fusion
  8.6 0.0 copy-start
  8.7 25.9 %all_to_all.25 = f32[16,8,2176]{2,1,0:T(8,128)S(1)} all-to-all(f32[16,8,2176]{2,1,0:T(8,128)S(1)} %maximum_bitcast_fusion), channel_id=1, replica_groups=mesh['region'=8,'unit'=16] {'unit'}, dimensions={0} | all-to-all | bytes 2228224 | tf_op jit(solution)/shard_map/all_to_all | solution.py:15
  34.6 0.1 reduce_sum.48
  34.6 0.1 slice_reduce_fusion
  34.7 0.0 copy-done
  34.7 0.1 fusion.21
  34.8 0.1 broadcast_in_dim.24
  34.9 19.2 %all_to_all.26 = f32[16,8,2048]{2,1,0:T(8,128)S(1)} all-to-all(f32[16,8,2048]{2,1,0:T(8,128)S(1)} %broadcast_in_dim.24), channel_id=1, replica_groups=mesh['region'=8,'unit'=16] {'unit'}, dimensions={0} | all-to-all | bytes 2097152 | tf_op jit(solution)/shard_map/all_to_all | solution.py:21
  54.2 0.0 copy-start.2
  54.2 2.4 %convolution_add_fusion.1 = f32[256,2048]{1,0:T(8,128)} fusion(f32[256,2048]{1,0:T(8,128)S(1)} %fusion, f32[16,8,2048]{2,1,0:T(8,128)S(1)} %all_to_all.26, s32[256]{0:T(256)S(1)} %get-tuple-element.7), kind=kOutput, calls=%fused_computation.5 | convolution fusion | flops 805863424 | bytes 5243904 | tf_op jit(solution)/shard_map/dot_general | solution.py:93
  56.5 0.0 copy-done.2
  56.5 11.5 %fusion.1 = f32[256,2048]{1,0:T(8,128)S(1)} fusion(f32[256,2048]{1,0:T(8,128)} %convolution_add_fusion.1, bf16[2048,2048]{1,0:T(8,128)(2,1)} %param.6, bf16[256,2048]{1,0:T(8,128)(2,1)S(1)} %copy-done.2), kind=kOutput, calls=%fused_computation.7 | convolution fusion | flops 4298113024 | bytes 13631488 | tf_op jit(solution)/shard_map/dot_general | solution.py:49
  68.0 0.9 convolution_bitcast_fusion
  69.0 0.0 copy-start.1
  69.0 18.0 %all_to_all.27 = f32[16,8,2048]{2,1,0:T(8,128)S(1)} all-to-all(f32[16,8,2048]{2,1,0:T(8,128)S(1)} %convolution_bitcast_fusion), channel_id=1, replica_groups=mesh['region'=8,'unit'=16] {'unit'}, dimensions={0} | all-to-all | bytes 2097152 | tf_op jit(solution)/shard_map/all_to_all | solution.py:15
  87.0 0.1 reduce_sum.49
  87.0 0.1 subtract_divide_fusion
  87.1 0.0 copy-done.1
  87.1 0.1 copy.18
  87.2 0.2 fusion.15
  87.5 1.1 broadcast_in_dim.25
  88.6 3.8 %all-to-all-start.3 = ((f32[16,8,2048]{2,1,0:T(8,128)}), f32[16,8,2048]{2,1,0:T(8,128)S(1)}, u32[]{:S(2)}, u32[]{:S(2)}) async-start(f32[16,8,2048]{2,1,0:T(8,128)} %broadcast_in_dim.25), calls=%async_computation.3 | async-start | bytes 2097152 | tf_op jit(solution)/shard_map/all_to_all | solution.py:21
  92.5 0.2 fusion.17
  92.7 0.2 select_reduce_fusion
  92.8 0.1 sub.39
  92.9 0.1 copy.20
  93.0 4.1 %scatter_custom_fusion = f32[512,2048]{1,0:T(8,128)} fusion(s32[256]{0:T(256)S(1)} %bitcast.49, f32[256,2048]{1,0:T(8,128)S(1)} %fusion.1, f32[]{:T(128)} %constant.10.clone.1), kind=kCustom, calls=%fused_computation.13 | custom fusion | bytes 4194308 | tf_op jit(solution)/shard_map/scatter | solution.py:88
  97.1 5.2 %reshape.87 = f32[128,4,2048]{2,1,0:T(4,128)} reshape(f32[512,2048]{1,0:T(8,128)} %scatter_custom_fusion) | data formatting | bytes 8388608 | tf_op jit(solution)/shard_map/reshape | solution.py:89
  102.3 3.5 %all-to-all-done.3 = f32[16,8,2048]{2,1,0:T(8,128)S(1)} async-done(((f32[16,8,2048]{2,1,0:T(8,128)}), f32[16,8,2048]{2,1,0:T(8,128)S(1)}, u32[]{:S(2)}, u32[]{:S(2)}) %all-to-all-start.3) | async-done | bytes 1048608 | tf_op jit(solution)/shard_map/all_to_all | solution.py:21
  105.8 6.3 %copy_add_fusion = f32[128,4,2048]{2,0,1:T(8,128)S(1)} fusion(f32[128,4,2048]{2,1,0:T(4,128)} %reshape.87, f32[16,8,2048]{2,1,0:T(8,128)S(1)} %all-to-all-done.3, s32[128,4]{0,1:T(4,128)S(1)} %copy.20), kind=kOutput, calls=%fused_computation.1 | convolution fusion | flops 1611726848 | bytes 9439232 | tf_op jit(solution)/shard_map/osc,ch->osh/dot_general | solution.py:96
  112.0 4.7 %copy.22 = f32[128,4,2048]{2,1,0:T(4,128)} copy(f32[128,4,2048]{2,0,1:T(8,128)S(1)} %copy_add_fusion) | data formatting | bytes 8388608 | tf_op jit(solution)/shard_map/add | solution.py:96
  116.7 6.4 %all-to-all-start.4 = ((f32[128,4,2048]{2,1,0:T(4,128)}), f32[128,4,2048]{2,1,0:T(4,128)}, u32[]{:S(2)}, u32[]{:S(2)}) async-start(f32[128,4,2048]{2,1,0:T(4,128)} %copy.22), calls=%async_computation.4 | async-start | bytes 8388608 | tf_op jit(solution)/shard_map/all_to_all | solution.py:106
  123.1 1.1 fusion.3
  124.2 6.7 %convolution_convert_fusion = bf16[256,2048]{1,0:T(8,128)(2,1)} fusion(bf16[256,2048]{1,0:T(8,128)(2,1)S(1)} %fusion.3, bf16[2048,2048]{1,0:T(8,128)(2,1)} %param.6), kind=kOutput, calls=%fused_computation.11 | convolution fusion | flops 2148007936 | bytes 10485760 | tf_op jit(solution)/shard_map/dot_general | solution.py:103
  130.9 45.4 %all-to-all-done.4 = f32[128,4,2048]{2,1,0:T(4,128)} async-done(((f32[128,4,2048]{2,1,0:T(4,128)}), f32[128,4,2048]{2,1,0:T(4,128)}, u32[]{:S(2)}, u32[]{:S(2)}) %all-to-all-start.4) | async-done | bytes 4194336 | tf_op jit(solution)/shard_map/all_to_all | solution.py:106
  176.3 5.3 %reshape.88 = f32[512,2048]{1,0:T(8,128)} reshape(f32[128,4,2048]{2,1,0:T(4,128)} %all-to-all-done.4) | data formatting | bytes 8388608 | tf_op jit(solution)/shard_map/reshape | solution.py:107
  (9 shorter events, 0.1 us)
Async XLA Ops:
  8.6 26.1 %copy-start = (f32[8,2048]{1,0:T(8,128)S(1)}, f32[8,2048]{1,0:T(8,128)}, u32[]{:S(2)}) copy-start(f32[8,2048]{1,0:T(8,128)} %param.7) | copy-start | bytes 196612
  54.2 2.4 %copy-start.2 = (bf16[256,2048]{1,0:T(8,128)(2,1)S(1)}, bf16[256,2048]{1,0:T(8,128)(2,1)}, u32[]{:S(2)}) copy-start(bf16[256,2048]{1,0:T(8,128)(2,1)} %param.5) | copy-start | bytes 3145732
  69.0 18.2 %copy-start.1 = (s32[256,1]{0,1:T(1,128)S(1)}, s32[256,1]{0,1:T(1,128)}, u32[]{:S(2)}) copy-start(s32[256,1]{0,1:T(1,128)} %param.9) | copy-start | bytes 3076
  88.6 17.2 %all-to-all-start.3 = ((f32[16,8,2048]{2,1,0:T(8,128)}), f32[16,8,2048]{2,1,0:T(8,128)S(1)}, u32[]{:S(2)}, u32[]{:S(2)}) async-start(f32[16,8,2048]{2,1,0:T(8,128)} %broadcast_in_dim.25), calls=%async_computation.3 | async-start | bytes 2097152 | tf_op jit(solution)/shard_map/all_to_all | solution.py:21
  116.7 59.6 %all-to-all-start.4 = ((f32[128,4,2048]{2,1,0:T(4,128)}), f32[128,4,2048]{2,1,0:T(4,128)}, u32[]{:S(2)}, u32[]{:S(2)}) async-start(f32[128,4,2048]{2,1,0:T(4,128)} %copy.22), calls=%async_computation.4 | async-start | bytes 8388608 | tf_op jit(solution)/shard_map/all_to_all | solution.py:106

commit v9 on v7

--- a/solution.py
+++ b/solution.py
@@ -105,9 +105,10 @@
             )
         parent_gap = (county_hist - child_total) / tract_count[:, None]
         region_gap = unit_gather(parent_gap, unit_count)
-        gap_pieces = bf16_pieces(region_gap)
-        estimate = stepped + one_hot_pick(member, gap_pieces)
-    grouped = slot_stepped + one_hot_pick(slot_member, gap_pieces)
+        estimate = stepped + jnp.dot(
+            member, region_gap, precision=lax.Precision.HIGHEST, preferred_element_type=jnp.float32
+        )
+    grouped = slot_stepped + one_hot_pick(slot_member, bf16_pieces(region_gap))
     released = jnp.dot(
         estimate.astype(jnp.bfloat16), strategy, preferred_element_type=jnp.float32
     ).astype(jnp.bfloat16)

time: 186 us -> 182 us (0.978)
  blocking collectives: 44.9 us -> 63.2 us
  waiting for transfers between devices: 66.1 us -> 48.8 us
  starting transfers between devices: 13.9 us -> 10.3 us
    all_to_all x0 -> x1, blocking collectives: none -> 19.2 us  [unit_gather(): arrived = lax.all_to_all(spread, 'unit', 0, 0, tiled=True)]
    all_to_all x2 -> x1, waiting for transfers between devices: 20.8 us -> 3.4 us  [unit_gather(): arrived = lax.all_to_all(spread, 'unit', 0, 0, tiled=True)]
    all_to_all x2 -> x1, starting transfers between devices: 7.49 us -> 3.84 us  [unit_gather(): arrived = lax.all_to_all(spread, 'unit', 0, 0, tiled=True)]
    dot_general x0 -> x2, matrix products: none -> 3.43 us  [local(): jnp.dot(member, region_gap, precision=lax.Precision.HIGHEST, preferred_el...]
    dot_general x2 -> x1, matrix products: 7.13 us -> 5.1 us  [one_hot_pick(): jnp.einsum('...k,kh->...h', stacked, table_pieces, preferred_element_type...]
  transfers between devices with their start and end apart: 3 -> 2, of which waited for: 3 -> 2; matrix products, arithmetic and copies ran while one was open for 10% -> 10% of each run, Pallas kernels for 0% -> 0%
where the time goes in v9:
time: 182 us; the launch traced here: 181 us
  blocking collectives  63.2 us (35%)
  waiting for transfers between devices  48.8 us (27%)
  matrix products  34.7 us (19%)
  local copies, waits for them, and re-layouts  20.9 us (11%)
  starting transfers between devices  10.3 us (6%)
  other arithmetic  2.17 us (1%)
    all_to_all x1, waiting for transfers between devices, local(): lax.all_to_all(grouped, ('region', 'unit'), split_axis=0, concat_axis=0,...  45.4 us
    all_to_all x2, blocking collectives, unit_sum(): arrived = lax.all_to_all(grouped, 'unit', 0, 0, tiled=True)  43.9 us
    all_to_all x1, blocking collectives, unit_gather(): arrived = lax.all_to_all(spread, 'unit', 0, 0, tiled=True)  19.2 us
    dot_general x2, matrix products, local(): lax.dot_general(misfit, strategy, (((1,), (1,)), ((), ())), preferred_ele...  17.6 us
    dot_general x1, matrix products, local(): jnp.dot(estimate.astype(jnp.bfloat16), strategy, preferred_element_type=j...  6.71 us
    all_to_all x1, starting transfers between devices, local(): lax.all_to_all(grouped, ('region', 'unit'), split_axis=0, concat_axis=0,...  6.47 us
    reshape x1, local copies, waits for them, and re-layouts, local(): relaid = arrived.reshape(devices * capacity, width)  5.27 us
    reshape x1, local copies, waits for them, and re-layouts, local(): slot_stepped = jnp.zeros((devices * capacity, width), jnp.float32).at[tar...  5.17 us
  transfers between devices with their start and end apart: 2, of which 2 were waited for; matrix products, arithmetic and copies ran while one was open for 10% of the time, Pallas kernels for 0%

profile of v9, /device:TPU:6, one launch (start us, length us, event | category | flops | bytes accessed | tf_op | source)
XLA Modules:
  0.0 180.9 jit_solution(17245170242829954243)
XLA Ops:
  0.6 0.7 broadcast_add_fusion.2
  1.3 0.1 convert_reduce_fusion
  1.4 6.1 %fusion = f32[256,2048]{1,0:T(8,128)S(1)} fusion(bf16[2048,2048]{1,0:T(8,128)(2,1)} %param.6, bf16[256,2048]{1,0:T(8,128)(2,1)} %param.5), kind=kOutput, calls=%fused_computation.6 | convolution fusion | flops 2149056512 | bytes 11534336 | tf_op jit(solution)/shard_map/dot_general | solution.py:64
  7.5 0.9 fusion.26
  8.5 0.1 broadcast_in_dim.19
  8.5 0.1 maximum_bitcast_fusion.2
  8.6 0.0 copy-start
  8.7 25.9 %all_to_all.25 = f32[16,8,2176]{2,1,0:T(8,128)S(1)} all-to-all(f32[16,8,2176]{2,1,0:T(8,128)S(1)} %maximum_bitcast_fusion.2), channel_id=1, replica_groups=mesh['region'=8,'unit'=16] {'unit'}, dimensions={0} | all-to-all | bytes 2228224 | tf_op jit(solution)/shard_map/all_to_all | solution.py:30
  34.6 0.1 reduce_sum.48
  34.6 0.1 slice_reduce_fusion
  34.7 0.0 copy-done
  34.7 0.1 fusion.27
  34.8 0.1 broadcast_in_dim.24
  34.9 19.2 %all_to_all.26 = f32[16,8,2048]{2,1,0:T(8,128)S(1)} all-to-all(f32[16,8,2048]{2,1,0:T(8,128)S(1)} %broadcast_in_dim.24), channel_id=1, replica_groups=mesh['region'=8,'unit'=16] {'unit'}, dimensions={0} | all-to-all | bytes 2097152 | tf_op jit(solution)/shard_map/all_to_all | solution.py:36
  54.2 0.0 copy-start.2
  54.2 2.4 %convolution_add_fusion.1 = f32[256,2048]{1,0:T(8,128)} fusion(f32[256,2048]{1,0:T(8,128)S(1)} %fusion, f32[16,8,2048]{2,1,0:T(8,128)S(1)} %all_to_all.26, s32[256]{0:T(256)S(1)} %get-tuple-element.7), kind=kOutput, calls=%fused_computation.5 | convolution fusion | flops 805863424 | bytes 5243904 | tf_op jit(solution)/shard_map/dot_general | solution.py:108
  56.5 0.0 copy-done.2
  56.5 11.5 %fusion.1 = f32[256,2048]{1,0:T(8,128)S(1)} fusion(f32[256,2048]{1,0:T(8,128)} %convolution_add_fusion.1, bf16[2048,2048]{1,0:T(8,128)(2,1)} %param.6, bf16[256,2048]{1,0:T(8,128)(2,1)S(1)} %copy-done.2), kind=kOutput, calls=%fused_computation.7 | convolution fusion | flops 4298113024 | bytes 13631488 | tf_op jit(solution)/shard_map/dot_general | solution.py:64
  68.0 0.9 convolution_bitcast_fusion
  69.0 0.0 copy-start.1
  69.0 18.0 %all_to_all.27 = f32[16,8,2048]{2,1,0:T(8,128)S(1)} all-to-all(f32[16,8,2048]{2,1,0:T(8,128)S(1)} %convolution_bitcast_fusion), channel_id=1, replica_groups=mesh['region'=8,'unit'=16] {'unit'}, dimensions={0} | all-to-all | bytes 2097152 | tf_op jit(solution)/shard_map/all_to_all | solution.py:30
  87.0 0.1 reduce_sum.49
  87.0 0.1 subtract_divide_fusion
  87.1 0.0 copy-done.1
  87.1 0.1 copy.18
  87.2 0.2 fusion.22
  87.5 1.1 broadcast_in_dim.25
  88.6 3.8 %all-to-all-start.3 = ((f32[16,8,2048]{2,1,0:T(8,128)}), f32[16,8,2048]{2,1,0:T(8,128)S(1)}, u32[]{:S(2)}, u32[]{:S(2)}) async-start(f32[16,8,2048]{2,1,0:T(8,128)} %broadcast_in_dim.25), calls=%async_computation.3 | async-start | bytes 2097152 | tf_op jit(solution)/shard_map/all_to_all | solution.py:36
  92.5 0.2 fusion.24
  92.7 0.2 select_reduce_fusion
  92.8 0.1 sub.45
  92.9 0.1 copy.20
  93.0 4.1 %scatter_custom_fusion = f32[512,2048]{1,0:T(8,128)} fusion(s32[256]{0:T(256)S(1)} %bitcast.51, f32[256,2048]{1,0:T(8,128)S(1)} %fusion.1, f32[]{:T(128)} %constant.10.clone.1), kind=kCustom, calls=%fused_computation.13 | custom fusion | bytes 4194308 | tf_op jit(solution)/shard_map/scatter | solution.py:103
  97.1 5.2 %reshape.73 = f32[128,4,2048]{2,1,0:T(4,128)} reshape(f32[512,2048]{1,0:T(8,128)} %scatter_custom_fusion) | data formatting | bytes 8388608 | tf_op jit(solution)/shard_map/reshape | solution.py:104
  102.3 0.1 convert_convert_fusion
  102.4 3.4 %all-to-all-done.3 = f32[16,8,2048]{2,1,0:T(8,128)S(1)} async-done(((f32[16,8,2048]{2,1,0:T(8,128)}), f32[16,8,2048]{2,1,0:T(8,128)S(1)}, u32[]{:S(2)}, u32[]{:S(2)}) %all-to-all-start.3) | async-done | bytes 1048608 | tf_op jit(solution)/shard_map/all_to_all | solution.py:36
  105.8 0.3 reduce-precision_convert_fusion.1
  106.1 5.1 %copy_add_fusion = f32[128,4,2048]{2,0,1:T(8,128)S(1)} fusion(f32[128,4,2048]{2,1,0:T(4,128)} %reshape.73, bf16[128,2048]{1,0:T(8,128)(2,1)S(1)} %get-tuple-element.9, bf16[128,2048]{1,0:T(8,128)(2,1)S(1)} %get-tuple-element.10, bf16[128,2048]{1,0:T(8,128)(2,1)S(1)} %get-tuple-element.8, bf16[128,4,128]{2,0,1:T(8,128)(2,1)S(1)} %convert_convert_fusion), kind=kOutput, calls=%fused_computation.1 | convolution fusion | flops 812253184 | bytes 10092544 | tf_op jit(solution)/shard_map/...k,kh->...h/dot_general | solution.py:24
  111.2 4.7 %copy.22 = f32[128,4,2048]{2,1,0:T(4,128)} copy(f32[128,4,2048]{2,0,1:T(8,128)S(1)} %copy_add_fusion) | data formatting | bytes 8388608 | tf_op jit(solution)/shard_map/add | solution.py:111
  115.9 6.5 %all-to-all-start.4 = ((f32[128,4,2048]{2,1,0:T(4,128)}), f32[128,4,2048]{2,1,0:T(4,128)}, u32[]{:S(2)}, u32[]{:S(2)}) async-start(f32[128,4,2048]{2,1,0:T(4,128)} %copy.22), calls=%async_computation.4 | async-start | bytes 8388608 | tf_op jit(solution)/shard_map/all_to_all | solution.py:115
  122.4 1.1 fusion.3
  123.5 6.7 %convolution_convert_fusion = bf16[256,2048]{1,0:T(8,128)(2,1)} fusion(bf16[256,2048]{1,0:T(8,128)(2,1)S(1)} %fusion.3, bf16[2048,2048]{1,0:T(8,128)(2,1)} %param.6), kind=kOutput, calls=%fused_computation.11 | convolution fusion | flops 2148007936 | bytes 10485760 | tf_op jit(solution)/shard_map/dot_general | solution.py:112
  130.2 45.4 %all-to-all-done.4 = f32[128,4,2048]{2,1,0:T(4,128)} async-done(((f32[128,4,2048]{2,1,0:T(4,128)}), f32[128,4,2048]{2,1,0:T(4,128)}, u32[]{:S(2)}, u32[]{:S(2)}) %all-to-all-start.4) | async-done | bytes 4194336 | tf_op jit(solution)/shard_map/all_to_all | solution.py:115
  175.6 5.3 %reshape.74 = f32[512,2048]{1,0:T(8,128)} reshape(f32[128,4,2048]{2,1,0:T(4,128)} %all-to-all-done.4) | data formatting | bytes 8388608 | tf_op jit(solution)/shard_map/reshape | solution.py:116
  (9 shorter events, 0.1 us)
Async XLA Ops:
  8.6 26.1 %copy-start = (f32[8,2048]{1,0:T(8,128)S(1)}, f32[8,2048]{1,0:T(8,128)}, u32[]{:S(2)}) copy-start(f32[8,2048]{1,0:T(8,128)} %param.7) | copy-start | bytes 196612
  54.2 2.4 %copy-start.2 = (bf16[256,2048]{1,0:T(8,128)(2,1)S(1)}, bf16[256,2048]{1,0:T(8,128)(2,1)}, u32[]{:S(2)}) copy-start(bf16[256,2048]{1,0:T(8,128)(2,1)} %param.5) | copy-start | bytes 3145732
  69.0 18.2 %copy-start.1 = (s32[256,1]{0,1:T(1,128)S(1)}, s32[256,1]{0,1:T(1,128)}, u32[]{:S(2)}) copy-start(s32[256,1]{0,1:T(1,128)} %param.9) | copy-start | bytes 3076
  88.6 17.2 %all-to-all-start.3 = ((f32[16,8,2048]{2,1,0:T(8,128)}), f32[16,8,2048]{2,1,0:T(8,128)S(1)}, u32[]{:S(2)}, u32[]{:S(2)}) async-start(f32[16,8,2048]{2,1,0:T(8,128)} %broadcast_in_dim.25), calls=%async_computation.3 | async-start | bytes 2097152 | tf_op jit(solution)/shard_map/all_to_all | solution.py:36
  115.9 59.7 %all-to-all-start.4 = ((f32[128,4,2048]{2,1,0:T(4,128)}), f32[128,4,2048]{2,1,0:T(4,128)}, u32[]{:S(2)}, u32[]{:S(2)}) async-start(f32[128,4,2048]{2,1,0:T(4,128)} %copy.22), calls=%async_computation.4 | async-start | bytes 8388608 | tf_op jit(solution)/shard_map/all_to_all | solution.py:115

commit v10 on v9

--- a/solution.py
+++ b/solution.py
@@ -94,21 +94,29 @@
                 target[None, :] == jnp.arange(devices * capacity, dtype=jnp.int32)[:, None]
             )
             slot_county = jnp.sum(jnp.where(slot_hits, local_id[None, :] + 1, 0), axis=1) - 1
-            slot_member = (
-                slot_county[:, None] == jnp.arange(county_region, dtype=jnp.int32)[None, :]
-            ).astype(jnp.float32).reshape(devices, capacity, county_region)
+            half = width // 2
+            row_county = jnp.repeat(slot_county, 2)
+            row_half = jnp.tile(jnp.arange(2, dtype=jnp.int32), devices * capacity)
+            k = jnp.arange(2 * 3 * county_region, dtype=jnp.int32)[None, :]
+            row_pick = (
+                (k // (3 * county_region) == row_half[:, None])
+                & (k % county_region == row_county[:, None])
+            ).astype(jnp.bfloat16)
             slot_stepped = (
                 jnp.zeros((devices * capacity, width), jnp.float32)
                 .at[target]
                 .set(stepped)
-                .reshape(devices, capacity, width)
+                .reshape(devices, 2 * capacity, half)
             )
         parent_gap = (county_hist - child_total) / tract_count[:, None]
         region_gap = unit_gather(parent_gap, unit_count)
         estimate = stepped + jnp.dot(
             member, region_gap, precision=lax.Precision.HIGHEST, preferred_element_type=jnp.float32
         )
-    grouped = slot_stepped + one_hot_pick(slot_member, bf16_pieces(region_gap))
+    gap_pieces = bf16_pieces(region_gap)
+    halves = jnp.concatenate([gap_pieces[:, :half], gap_pieces[:, half:]], axis=0)
+    picked = jnp.dot(row_pick, halves, preferred_element_type=jnp.float32)
+    grouped = slot_stepped + picked.reshape(devices, 2 * capacity, half)
     released = jnp.dot(
         estimate.astype(jnp.bfloat16), strategy, preferred_element_type=jnp.float32
     ).astype(jnp.bfloat16)

time: 182 us -> 181 us (level)
  blocking collectives: 63.2 us -> 45.1 us
  waiting for transfers between devices: 48.8 us -> 65.7 us
  starting transfers between devices: 10.3 us -> 13.9 us
  local copies, waits for them, and re-layouts: 20.9 us -> 18.2 us
    all_to_all x2 -> x1, blocking collectives: 43.9 us -> 25.9 us  [unit_sum(): arrived = lax.all_to_all(grouped, 'unit', 0, 0, tiled=True)]
    all_to_all x0 -> x1, waiting for transfers between devices: none -> 14.8 us  [unit_sum(): arrived = lax.all_to_all(grouped, 'unit', 0, 0, tiled=True)]
    add x1 -> x0, local copies, waits for them, and re-layouts: 4.71 us -> none  [local(): grouped = slot_stepped + one_hot_pick(slot_member, bf16_pieces(region_gap))]
    all_to_all x0 -> x1, starting transfers between devices: none -> 3.66 us  [unit_sum(): arrived = lax.all_to_all(grouped, 'unit', 0, 0, tiled=True)]
    all_to_all x1, waiting for transfers between devices: 3.4 us -> 5.47 us  [unit_gather(): arrived = lax.all_to_all(spread, 'unit', 0, 0, tiled=True)]
    unnamed x7 -> x9, local copies, waits for them, and re-layouts: 0.02 us -> 1.89 us
  transfers between devices with their start and end apart: 2 -> 3, of which waited for: 2 -> 3; matrix products, arithmetic and copies ran while one was open for 10% -> 10% of each run, Pallas kernels for 0% -> 0%
where the time goes in v10:
time: 181 us
  waiting for transfers between devices  65.7 us (36%)
  blocking collectives  45.1 us (25%)
  matrix products  34.5 us (19%)
  local copies, waits for them, and re-layouts  18.2 us (10%)
  starting transfers between devices  13.9 us (8%)
  other arithmetic  2.21 us (1%)
    all_to_all x1, waiting for transfers between devices, local(): lax.all_to_all(grouped, ('region', 'unit'), split_axis=0, concat_axis=0,...  45.4 us
    all_to_all x1, blocking collectives, unit_sum(): arrived = lax.all_to_all(grouped, 'unit', 0, 0, tiled=True)  25.9 us
    all_to_all x1, blocking collectives, unit_gather(): arrived = lax.all_to_all(spread, 'unit', 0, 0, tiled=True)  19.2 us
    dot_general x2, matrix products, local(): lax.dot_general(misfit, strategy, (((1,), (1,)), ((), ())), preferred_ele...  17.6 us
    all_to_all x1, waiting for transfers between devices, unit_sum(): arrived = lax.all_to_all(grouped, 'unit', 0, 0, tiled=True)  14.8 us
    dot_general x1, matrix products, local(): jnp.dot(estimate.astype(jnp.bfloat16), strategy, preferred_element_type=j...  6.71 us
    all_to_all x1, starting transfers between devices, local(): lax.all_to_all(grouped, ('region', 'unit'), split_axis=0, concat_axis=0,...  6.45 us
    all_to_all x1, waiting for transfers between devices, unit_gather(): arrived = lax.all_to_all(spread, 'unit', 0, 0, tiled=True)  5.47 us
  transfers between devices with their start and end apart: 3, of which 3 were waited for; matrix products, arithmetic and copies ran while one was open for 10% of the time, Pallas kernels for 0%

profile of v10, /device:TPU:6, one launch (start us, length us, event | category | flops | bytes accessed | tf_op | source)
XLA Modules:
  0.0 180.6 jit_solution(17367675789830549770)
XLA Ops:
  0.6 0.7 broadcast_add_fusion.2
  1.3 0.1 convert_reduce_fusion
  1.4 6.1 %fusion.4 = f32[256,2048]{1,0:T(8,128)S(1)} fusion(bf16[2048,2048]{1,0:T(8,128)(2,1)} %param.6, bf16[256,2048]{1,0:T(8,128)(2,1)} %param.5), kind=kOutput, calls=%fused_computation.10 | convolution fusion | flops 2149056512 | bytes 11534336 | tf_op jit(solution)/shard_map/dot_general | solution.py:64
  7.5 0.9 fusion.30
  8.5 0.1 broadcast_in_dim.25
  8.5 0.1 maximum_bitcast_fusion
  8.6 0.0 copy-start.1
  8.7 25.9 %all_to_all.25 = f32[16,8,2176]{2,1,0:T(8,128)S(1)} all-to-all(f32[16,8,2176]{2,1,0:T(8,128)S(1)} %maximum_bitcast_fusion), channel_id=1, replica_groups=mesh['region'=8,'unit'=16] {'unit'}, dimensions={0} | all-to-all | bytes 2228224 | tf_op jit(solution)/shard_map/all_to_all | solution.py:30
  34.6 0.1 reduce_sum.48
  34.6 0.1 slice_reduce_fusion
  34.7 0.0 copy-done.1
  34.7 0.1 fusion.31
  34.8 0.1 broadcast_in_dim.26
  34.9 19.2 %all_to_all.26 = f32[16,8,2048]{2,1,0:T(8,128)S(1)} all-to-all(f32[16,8,2048]{2,1,0:T(8,128)S(1)} %broadcast_in_dim.26), channel_id=1, replica_groups=mesh['region'=8,'unit'=16] {'unit'}, dimensions={0} | all-to-all | bytes 2097152 | tf_op jit(solution)/shard_map/all_to_all | solution.py:36
  54.2 0.0 copy-start.3
  54.2 2.4 %convolution_add_fusion.1 = f32[256,2048]{1,0:T(8,128)} fusion(f32[256,2048]{1,0:T(8,128)S(1)} %fusion.4, f32[16,8,2048]{2,1,0:T(8,128)S(1)} %all_to_all.26, s32[256]{0:T(256)S(1)} %get-tuple-element.7), kind=kOutput, calls=%fused_computation.9 | convolution fusion | flops 805863424 | bytes 5243904 | tf_op jit(solution)/shard_map/dot_general | solution.py:113
  56.5 0.0 copy-done.3
  56.5 11.5 %fusion.5 = f32[256,2048]{1,0:T(8,128)S(1)} fusion(f32[256,2048]{1,0:T(8,128)} %convolution_add_fusion.1, bf16[2048,2048]{1,0:T(8,128)(2,1)} %param.6, bf16[256,2048]{1,0:T(8,128)(2,1)S(1)} %copy-done.3), kind=kOutput, calls=%fused_computation.11 | convolution fusion | flops 4298113024 | bytes 13631488 | tf_op jit(solution)/shard_map/dot_general | solution.py:64
  68.0 1.9 %convolution_bitcast_fusion = f32[16,8,2048]{2,1,0:T(8,128)} fusion(f32[256,2048]{1,0:T(8,128)S(1)} %fusion.5, s32[256]{0:T(256)S(1)} %get-tuple-element.7), kind=kOutput, calls=%fused_computation.16 | convolution fusion | flops 805339136 | bytes 3146752 | tf_op jit(solution)/shard_map/dot_general | solution.py:68
  69.9 3.7 %all-to-all-start.2 = ((f32[16,8,2048]{2,1,0:T(8,128)}), f32[16,8,2048]{2,1,0:T(8,128)S(1)}, u32[]{:S(2)}, u32[]{:S(2)}) async-start(f32[16,8,2048]{2,1,0:T(8,128)} %convolution_bitcast_fusion), calls=%async_computation.2 | async-start | bytes 2097152 | tf_op jit(solution)/shard_map/all_to_all | solution.py:30
  73.6 0.2 eq.95
  73.8 0.0 copy-start.2
  73.8 14.8 %all-to-all-done.2 = f32[16,8,2048]{2,1,0:T(8,128)S(1)} async-done(((f32[16,8,2048]{2,1,0:T(8,128)}), f32[16,8,2048]{2,1,0:T(8,128)S(1)}, u32[]{:S(2)}, u32[]{:S(2)}) %all-to-all-start.2) | async-done | bytes 1048608 | tf_op jit(solution)/shard_map/all_to_all | solution.py:30
  88.6 0.1 reduce_sum.49
  88.7 0.1 subtract_divide_fusion
  88.8 1.1 broadcast_in_dim.27
  89.9 3.8 %all-to-all-start.3 = ((f32[16,8,2048]{2,1,0:T(8,128)}), f32[16,8,2048]{2,1,0:T(8,128)S(1)}, u32[]{:S(2)}, u32[]{:S(2)}) async-start(f32[16,8,2048]{2,1,0:T(8,128)} %broadcast_in_dim.27), calls=%async_computation.3 | async-start | bytes 2097152 | tf_op jit(solution)/shard_map/all_to_all | solution.py:36
  93.7 0.0 copy-done.2
  93.7 0.1 copy.10
  93.8 0.2 fusion.26
  94.1 0.2 fusion.28
  94.3 4.1 %scatter_custom_fusion = f32[512,2048]{1,0:T(8,128)} fusion(s32[256]{0:T(256)S(1)} %bitcast.49, f32[256,2048]{1,0:T(8,128)S(1)} %fusion.5, f32[]{:T(128)} %constant.22.clone.1), kind=kCustom, calls=%fused_computation.17 | custom fusion | bytes 4194308 | tf_op jit(solution)/shard_map/scatter | solution.py:108
  98.4 4.9 %reshape.101 = f32[128,8,1024]{2,1,0:T(8,128)} reshape(f32[512,2048]{1,0:T(8,128)} %scatter_custom_fusion) | data formatting | bytes 8388608 | tf_op jit(solution)/shard_map/reshape | solution.py:109
  103.3 0.2 select_reduce_fusion
  103.5 0.1 broadcast_in_dim.54
  103.6 0.2 eq.102
  103.8 5.5 %all-to-all-done.3 = f32[16,8,2048]{2,1,0:T(8,128)S(1)} async-done(((f32[16,8,2048]{2,1,0:T(8,128)}), f32[16,8,2048]{2,1,0:T(8,128)S(1)}, u32[]{:S(2)}, u32[]{:S(2)}) %all-to-all-start.3) | async-done | bytes 1048608 | tf_op jit(solution)/shard_map/all_to_all | solution.py:36
  109.3 0.3 reduce-precision_convert_fusion.1
  109.5 0.0 copy-start
  109.5 0.2 pad_maximum_fusion
  109.7 0.1 fusion.44
  109.9 1.9 %copy-done = f32[128,8,1024]{2,1,0:T(8,128)S(1)} copy-done((f32[128,8,1024]{2,1,0:T(8,128)S(1)}, f32[128,8,1024]{2,1,0:T(8,128)}, u32[]{:S(2)}) %copy-start) | copy-done | bytes 4194328
  111.7 3.9 %bitcast_add_fusion = f32[128,8,1024]{2,1,0:T(8,128)} fusion(f32[128,8,1024]{2,1,0:T(8,128)S(1)} %copy-done, bf16[384,1024]{1,0:T(8,128)(2,1)S(1)} %get-tuple-element.9, bf16[384,1024]{1,0:T(8,128)(2,1)S(1)} %get-tuple-element.8, s32[768]{0:T(1024)S(1)} %get-tuple-element.13, s32[768]{0:T(1024)S(1)} %get-tuple-element.14, s32[1024]{0:T(1024)S(1)} %eq.102, ...), kind=kOutput, calls=%fused_computation.1 | convolution fusion | flops 1617166336 | bytes 9975808 | tf_op jit(solution)/shard_map/dot_general | solution.py:118
  115.7 6.5 %all-to-all-start.4 = ((f32[128,8,1024]{2,1,0:T(8,128)}), f32[128,8,1024]{2,1,0:T(8,128)}, u32[]{:S(2)}, u32[]{:S(2)}) async-start(f32[128,8,1024]{2,1,0:T(8,128)} %bitcast_add_fusion), calls=%async_computation.4 | async-start | bytes 8388608 | tf_op jit(solution)/shard_map/all_to_all | solution.py:123
  122.1 1.1 fusion.7
  123.2 6.7 %convolution_convert_fusion = bf16[256,2048]{1,0:T(8,128)(2,1)} fusion(bf16[256,2048]{1,0:T(8,128)(2,1)S(1)} %fusion.7, bf16[2048,2048]{1,0:T(8,128)(2,1)} %param.6), kind=kOutput, calls=%fused_computation.15 | convolution fusion | flops 2148007936 | bytes 10485760 | tf_op jit(solution)/shard_map/dot_general | solution.py:120
  129.9 45.4 %all-to-all-done.4 = f32[128,8,1024]{2,1,0:T(8,128)} async-done(((f32[128,8,1024]{2,1,0:T(8,128)}), f32[128,8,1024]{2,1,0:T(8,128)}, u32[]{:S(2)}, u32[]{:S(2)}) %all-to-all-start.4) | async-done | bytes 4194336 | tf_op jit(solution)/shard_map/all_to_all | solution.py:123
  175.3 5.2 %reshape.103 = f32[512,2048]{1,0:T(8,128)} reshape(f32[128,8,1024]{2,1,0:T(8,128)} %all-to-all-done.4) | data formatting | bytes 8388608 | tf_op jit(solution)/shard_map/reshape | solution.py:124
  (11 shorter events, 0.1 us)
Async XLA Ops:
  8.6 26.1 %copy-start.1 = (f32[8,2048]{1,0:T(8,128)S(1)}, f32[8,2048]{1,0:T(8,128)}, u32[]{:S(2)}) copy-start(f32[8,2048]{1,0:T(8,128)} %param.7) | copy-start | bytes 196612
  54.2 2.4 %copy-start.3 = (bf16[256,2048]{1,0:T(8,128)(2,1)S(1)}, bf16[256,2048]{1,0:T(8,128)(2,1)}, u32[]{:S(2)}) copy-start(bf16[256,2048]{1,0:T(8,128)(2,1)} %param.5) | copy-start | bytes 3145732
  69.9 18.7 %all-to-all-start.2 = ((f32[16,8,2048]{2,1,0:T(8,128)}), f32[16,8,2048]{2,1,0:T(8,128)S(1)}, u32[]{:S(2)}, u32[]{:S(2)}) async-start(f32[16,8,2048]{2,1,0:T(8,128)} %convolution_bitcast_fusion), calls=%async_computation.2 | async-start | bytes 2097152 | tf_op jit(solution)/shard_map/all_to_all | solution.py:30
  73.8 19.9 %copy-start.2 = (s32[256,1]{0,1:T(1,128)S(1)}, s32[256,1]{0,1:T(1,128)}, u32[]{:S(2)}) copy-start(s32[256,1]{0,1:T(1,128)} %param.9) | copy-start | bytes 3076
  89.9 19.4 %all-to-all-start.3 = ((f32[16,8,2048]{2,1,0:T(8,128)}), f32[16,8,2048]{2,1,0:T(8,128)S(1)}, u32[]{:S(2)}, u32[]{:S(2)}) async-start(f32[16,8,2048]{2,1,0:T(8,128)} %broadcast_in_dim.27), calls=%async_computation.3 | async-start | bytes 2097152 | tf_op jit(solution)/shard_map/all_to_all | solution.py:36
  109.5 2.2 %copy-start = (f32[128,8,1024]{2,1,0:T(8,128)S(1)}, f32[128,8,1024]{2,1,0:T(8,128)}, u32[]{:S(2)}) copy-start(f32[128,8,1024]{2,1,0:T(8,128)} %reshape.101) | copy-start | bytes 12582916
  115.7 59.7 %all-to-all-start.4 = ((f32[128,8,1024]{2,1,0:T(8,128)}), f32[128,8,1024]{2,1,0:T(8,128)}, u32[]{:S(2)}, u32[]{:S(2)}) async-start(f32[128,8,1024]{2,1,0:T(8,128)} %bitcast_add_fusion), calls=%async_computation.4 | async-start | bytes 8388608 | tf_op jit(solution)/shard_map/all_to_all | solution.py:123

commit v11 on v10

--- a/solution.py
+++ b/solution.py
@@ -102,10 +102,11 @@
                 (k // (3 * county_region) == row_half[:, None])
                 & (k % county_region == row_county[:, None])
             ).astype(jnp.bfloat16)
+            half_target = (2 * target[:, None] + jnp.arange(2, dtype=jnp.int32)[None, :]).reshape(-1)
             slot_stepped = (
-                jnp.zeros((devices * capacity, width), jnp.float32)
-                .at[target]
-                .set(stepped)
+                jnp.zeros((2 * devices * capacity, half), jnp.float32)
+                .at[half_target]
+                .set(stepped.reshape(2 * tract_rows, half))
                 .reshape(devices, 2 * capacity, half)
             )
         parent_gap = (county_hist - child_total) / tract_count[:, None]

time: 181 us -> 182 us (level)
  waiting for transfers between devices: 65.7 us -> 68.1 us
    all_to_all x1, waiting for transfers between devices: 5.47 us -> 9.3 us  [unit_gather(): arrived = lax.all_to_all(spread, 'unit', 0, 0, tiled=True)]
    reshape x1, local copies, waits for them, and re-layouts: 4.92 us -> 1.53 us  [local(): stepped.reshape(2 * tract_rows, half)]
  transfers between devices with their start and end apart: 3 -> 3, of which waited for: 3 -> 3; matrix products, arithmetic and copies ran while one was open for 10% -> 9% of each run, Pallas kernels for 0% -> 0%
where the time goes in v11:
time: 182 us; the launch traced here: 181 us
  waiting for transfers between devices  68.1 us (37%)
  blocking collectives  45.1 us (25%)
  matrix products  34.5 us (19%)
  local copies, waits for them, and re-layouts  16.4 us (9%)
  starting transfers between devices  14 us (8%)
  other arithmetic  2.31 us (1%)
    all_to_all x1, waiting for transfers between devices, local(): lax.all_to_all(grouped, ('region', 'unit'), split_axis=0, concat_axis=0,...  45.4 us
    all_to_all x1, blocking collectives, unit_sum(): arrived = lax.all_to_all(grouped, 'unit', 0, 0, tiled=True)  25.9 us
    all_to_all x1, blocking collectives, unit_gather(): arrived = lax.all_to_all(spread, 'unit', 0, 0, tiled=True)  19.2 us
    dot_general x2, matrix products, local(): lax.dot_general(misfit, strategy, (((1,), (1,)), ((), ())), preferred_ele...  17.6 us
    all_to_all x1, waiting for transfers between devices, unit_sum(): arrived = lax.all_to_all(grouped, 'unit', 0, 0, tiled=True)  13.3 us
    all_to_all x1, waiting for transfers between devices, unit_gather(): arrived = lax.all_to_all(spread, 'unit', 0, 0, tiled=True)  9.3 us
    dot_general x1, matrix products, local(): jnp.dot(estimate.astype(jnp.bfloat16), strategy, preferred_element_type=j...  6.71 us
    all_to_all x1, starting transfers between devices, local(): lax.all_to_all(grouped, ('region', 'unit'), split_axis=0, concat_axis=0,...  6.46 us
  transfers between devices with their start and end apart: 3, of which 3 were waited for; matrix products, arithmetic and copies ran while one was open for 9% of the time, Pallas kernels for 0%

profile of v11, /device:TPU:6, one launch (start us, length us, event | category | flops | bytes accessed | tf_op | source)
XLA Modules:
  0.0 181.2 jit_solution(3991588972151314758)
XLA Ops:
  0.6 0.7 broadcast_add_fusion.2
  1.3 0.1 convert_reduce_fusion
  1.4 6.1 %fusion.4 = f32[256,2048]{1,0:T(8,128)S(1)} fusion(bf16[2048,2048]{1,0:T(8,128)(2,1)} %param.6, bf16[256,2048]{1,0:T(8,128)(2,1)} %param.5), kind=kOutput, calls=%fused_computation.10 | convolution fusion | flops 2149056512 | bytes 11534336 | tf_op jit(solution)/shard_map/dot_general | solution.py:64
  7.5 0.9 fusion.30
  8.5 0.1 broadcast_in_dim.25
  8.5 0.1 maximum_bitcast_fusion
  8.6 0.0 copy-start.1
  8.7 25.9 %all_to_all.25 = f32[16,8,2176]{2,1,0:T(8,128)S(1)} all-to-all(f32[16,8,2176]{2,1,0:T(8,128)S(1)} %maximum_bitcast_fusion), channel_id=1, replica_groups=mesh['region'=8,'unit'=16] {'unit'}, dimensions={0} | all-to-all | bytes 2228224 | tf_op jit(solution)/shard_map/all_to_all | solution.py:30
  34.6 0.1 reduce_sum.48
  34.6 0.1 slice_reduce_fusion
  34.7 0.0 copy-done.1
  34.7 0.1 fusion.31
  34.8 0.1 broadcast_in_dim.26
  34.9 19.2 %all_to_all.26 = f32[16,8,2048]{2,1,0:T(8,128)S(1)} all-to-all(f32[16,8,2048]{2,1,0:T(8,128)S(1)} %broadcast_in_dim.26), channel_id=1, replica_groups=mesh['region'=8,'unit'=16] {'unit'}, dimensions={0} | all-to-all | bytes 2097152 | tf_op jit(solution)/shard_map/all_to_all | solution.py:36
  54.2 0.0 copy-start.3
  54.2 2.4 %convolution_add_fusion.1 = f32[256,2048]{1,0:T(8,128)} fusion(f32[256,2048]{1,0:T(8,128)S(1)} %fusion.4, f32[16,8,2048]{2,1,0:T(8,128)S(1)} %all_to_all.26, s32[256]{0:T(256)S(1)} %get-tuple-element.7), kind=kOutput, calls=%fused_computation.9 | convolution fusion | flops 805863424 | bytes 5243904 | tf_op jit(solution)/shard_map/dot_general | solution.py:114
  56.5 0.0 copy-done.3
  56.5 11.5 %fusion.5 = f32[256,2048]{1,0:T(8,128)S(1)} fusion(f32[256,2048]{1,0:T(8,128)} %convolution_add_fusion.1, bf16[2048,2048]{1,0:T(8,128)(2,1)} %param.6, bf16[256,2048]{1,0:T(8,128)(2,1)S(1)} %copy-done.3), kind=kOutput, calls=%fused_computation.11 | convolution fusion | flops 4298113024 | bytes 13631488 | tf_op jit(solution)/shard_map/dot_general | solution.py:64
  68.0 1.9 %convolution_bitcast_fusion = f32[16,8,2048]{2,1,0:T(8,128)} fusion(f32[256,2048]{1,0:T(8,128)S(1)} %fusion.5, s32[256]{0:T(256)S(1)} %get-tuple-element.7), kind=kOutput, calls=%fused_computation.16 | convolution fusion | flops 805339136 | bytes 3146752 | tf_op jit(solution)/shard_map/dot_general | solution.py:68
  69.9 3.7 %all-to-all-start.2 = ((f32[16,8,2048]{2,1,0:T(8,128)}), f32[16,8,2048]{2,1,0:T(8,128)S(1)}, u32[]{:S(2)}, u32[]{:S(2)}) async-start(f32[16,8,2048]{2,1,0:T(8,128)} %convolution_bitcast_fusion), calls=%async_computation.2 | async-start | bytes 2097152 | tf_op jit(solution)/shard_map/all_to_all | solution.py:30
  73.6 0.2 eq.95
  73.8 0.0 copy-start.2
  73.8 1.5 reshape.138
  75.3 13.3 %all-to-all-done.2 = f32[16,8,2048]{2,1,0:T(8,128)S(1)} async-done(((f32[16,8,2048]{2,1,0:T(8,128)}), f32[16,8,2048]{2,1,0:T(8,128)S(1)}, u32[]{:S(2)}, u32[]{:S(2)}) %all-to-all-start.2) | async-done | bytes 1048608 | tf_op jit(solution)/shard_map/all_to_all | solution.py:30
  88.6 0.1 reduce_sum.49
  88.7 0.1 subtract_divide_fusion
  88.8 0.0 copy-done.2
  88.8 0.1 copy.10
  88.9 0.2 fusion.26
  89.2 0.2 fusion.28
  89.4 1.1 broadcast_in_dim.27
  90.5 3.8 %all-to-all-start.3 = ((f32[16,8,2048]{2,1,0:T(8,128)}), f32[16,8,2048]{2,1,0:T(8,128)S(1)}, u32[]{:S(2)}, u32[]{:S(2)}) async-start(f32[16,8,2048]{2,1,0:T(8,128)} %broadcast_in_dim.27), calls=%async_computation.3 | async-start | bytes 2097152 | tf_op jit(solution)/shard_map/all_to_all | solution.py:36
  94.3 0.1 iota_add_fusion
  94.4 0.1 add.93
  94.6 0.1 select_reduce_fusion
  94.7 0.1 broadcast_in_dim.31
  94.9 0.2 eq.102
  95.1 5.5 %scatter_custom_fusion = f32[1024,1024]{1,0:T(8,128)} fusion(s32[512]{0:T(512)S(1)} %bitcast.52, f32[512,1024]{1,0:T(8,128)} %reshape.138, f32[]{:T(128)} %constant.22.clone.1), kind=kCustom, calls=%fused_computation.17 | custom fusion | bytes 4194816 | tf_op jit(solution)/shard_map/scatter | solution.py:109
  100.6 9.3 %all-to-all-done.3 = f32[16,8,2048]{2,1,0:T(8,128)S(1)} async-done(((f32[16,8,2048]{2,1,0:T(8,128)}), f32[16,8,2048]{2,1,0:T(8,128)S(1)}, u32[]{:S(2)}, u32[]{:S(2)}) %all-to-all-start.3) | async-done | bytes 1048608 | tf_op jit(solution)/shard_map/all_to_all | solution.py:36
  109.9 0.3 reduce-precision_convert_fusion.1
  110.1 0.0 copy-start
  110.2 0.2 pad_maximum_fusion
  110.3 0.1 fusion.44
  110.5 1.9 %copy-done = f32[1024,1024]{1,0:T(8,128)S(1)} copy-done((f32[1024,1024]{1,0:T(8,128)S(1)}, f32[1024,1024]{1,0:T(8,128)}, u32[]{:S(2)}) %copy-start) | copy-done | bytes 4194328
  112.3 3.9 %add_bitcast_fusion = f32[128,8,1024]{2,1,0:T(8,128)} fusion(f32[1024,1024]{1,0:T(8,128)S(1)} %copy-done, bf16[384,1024]{1,0:T(8,128)(2,1)S(1)} %get-tuple-element.9, bf16[384,1024]{1,0:T(8,128)(2,1)S(1)} %get-tuple-element.8, s32[768]{0:T(1024)S(1)} %get-tuple-element.13, s32[768]{0:T(1024)S(1)} %get-tuple-element.14, s32[1024]{0:T(1024)S(1)} %eq.102, ...), kind=kOutput, calls=%fused_computation.1 | convolution fusion | flops 1617166336 | bytes 9975808 | tf_op jit(solution)/shard_map/dot_general | solution.py:119
  116.3 6.5 %all-to-all-start.4 = ((f32[128,8,1024]{2,1,0:T(8,128)}), f32[128,8,1024]{2,1,0:T(8,128)}, u32[]{:S(2)}, u32[]{:S(2)}) async-start(f32[128,8,1024]{2,1,0:T(8,128)} %add_bitcast_fusion), calls=%async_computation.4 | async-start | bytes 8388608 | tf_op jit(solution)/shard_map/all_to_all | solution.py:124
  122.7 1.1 fusion.7
  123.8 6.7 %convolution_convert_fusion = bf16[256,2048]{1,0:T(8,128)(2,1)} fusion(bf16[256,2048]{1,0:T(8,128)(2,1)S(1)} %fusion.7, bf16[2048,2048]{1,0:T(8,128)(2,1)} %param.6), kind=kOutput, calls=%fused_computation.15 | convolution fusion | flops 2148007936 | bytes 10485760 | tf_op jit(solution)/shard_map/dot_general | solution.py:121
  130.5 45.4 %all-to-all-done.4 = f32[128,8,1024]{2,1,0:T(8,128)} async-done(((f32[128,8,1024]{2,1,0:T(8,128)}), f32[128,8,1024]{2,1,0:T(8,128)}, u32[]{:S(2)}, u32[]{:S(2)}) %all-to-all-start.4) | async-done | bytes 4194336 | tf_op jit(solution)/shard_map/all_to_all | solution.py:124
  176.0 5.2 %reshape.133 = f32[512,2048]{1,0:T(8,128)} reshape(f32[128,8,1024]{2,1,0:T(8,128)} %all-to-all-done.4) | data formatting | bytes 8388608 | tf_op jit(solution)/shard_map/reshape | solution.py:125
  (12 shorter events, 0.1 us)
Async XLA Ops:
  8.6 26.1 %copy-start.1 = (f32[8,2048]{1,0:T(8,128)S(1)}, f32[8,2048]{1,0:T(8,128)}, u32[]{:S(2)}) copy-start(f32[8,2048]{1,0:T(8,128)} %param.7) | copy-start | bytes 196612
  54.2 2.4 %copy-start.3 = (bf16[256,2048]{1,0:T(8,128)(2,1)S(1)}, bf16[256,2048]{1,0:T(8,128)(2,1)}, u32[]{:S(2)}) copy-start(bf16[256,2048]{1,0:T(8,128)(2,1)} %param.5) | copy-start | bytes 3145732
  69.9 18.7 %all-to-all-start.2 = ((f32[16,8,2048]{2,1,0:T(8,128)}), f32[16,8,2048]{2,1,0:T(8,128)S(1)}, u32[]{:S(2)}, u32[]{:S(2)}) async-start(f32[16,8,2048]{2,1,0:T(8,128)} %convolution_bitcast_fusion), calls=%async_computation.2 | async-start | bytes 2097152 | tf_op jit(solution)/shard_map/all_to_all | solution.py:30
  73.8 15.0 %copy-start.2 = (s32[256,1]{0,1:T(1,128)S(1)}, s32[256,1]{0,1:T(1,128)}, u32[]{:S(2)}) copy-start(s32[256,1]{0,1:T(1,128)} %param.9) | copy-start | bytes 3076
  90.5 19.4 %all-to-all-start.3 = ((f32[16,8,2048]{2,1,0:T(8,128)}), f32[16,8,2048]{2,1,0:T(8,128)S(1)}, u32[]{:S(2)}, u32[]{:S(2)}) async-start(f32[16,8,2048]{2,1,0:T(8,128)} %broadcast_in_dim.27), calls=%async_computation.3 | async-start | bytes 2097152 | tf_op jit(solution)/shard_map/all_to_all | solution.py:36
  110.1 2.2 %copy-start = (f32[1024,1024]{1,0:T(8,128)S(1)}, f32[1024,1024]{1,0:T(8,128)}, u32[]{:S(2)}) copy-start(f32[1024,1024]{1,0:T(8,128)} %scatter_custom_fusion) | copy-start | bytes 12582916
  116.3 59.7 %all-to-all-start.4 = ((f32[128,8,1024]{2,1,0:T(8,128)}), f32[128,8,1024]{2,1,0:T(8,128)}, u32[]{:S(2)}, u32[]{:S(2)}) async-start(f32[128,8,1024]{2,1,0:T(8,128)} %add_bitcast_fusion), calls=%async_computation.4 | async-start | bytes 8388608 | tf_op jit(solution)/shard_map/all_to_all | solution.py:124

commit v12 on v11

--- a/solution.py
+++ b/solution.py
@@ -80,7 +80,9 @@
         else:
             child_total = unit_sum(partial_value, unit_count)
         if iteration == ITERS - 1:
-            late_owner, child_total = lax.optimization_barrier((tract_owner, child_total))
+            late_owner, late_stepped, child_total = lax.optimization_barrier(
+                (tract_owner, stepped, child_total)
+            )
             owners = late_owner[:, 0]
             owner_hits = (
                 owners[:, None] == jnp.arange(devices, dtype=jnp.int32)[None, :]
@@ -96,17 +98,17 @@
             slot_county = jnp.sum(jnp.where(slot_hits, local_id[None, :] + 1, 0), axis=1) - 1
             half = width // 2
             row_county = jnp.repeat(slot_county, 2)
-            row_half = jnp.tile(jnp.arange(2, dtype=jnp.int32), devices * capacity)
-            k = jnp.arange(2 * 3 * county_region, dtype=jnp.int32)[None, :]
+            pick_shape = (2 * devices * capacity, 2 * 3 * county_region)
+            row = lax.broadcasted_iota(jnp.int32, pick_shape, 0)
+            k = lax.broadcasted_iota(jnp.int32, pick_shape, 1)
             row_pick = (
-                (k // (3 * county_region) == row_half[:, None])
-                & (k % county_region == row_county[:, None])
+                (k // (3 * county_region) == row % 2) & (k % county_region == row_county[:, None])
             ).astype(jnp.bfloat16)
             half_target = (2 * target[:, None] + jnp.arange(2, dtype=jnp.int32)[None, :]).reshape(-1)
             slot_stepped = (
                 jnp.zeros((2 * devices * capacity, half), jnp.float32)
                 .at[half_target]
-                .set(stepped.reshape(2 * tract_rows, half))
+                .set(late_stepped.reshape(2 * tract_rows, half))
                 .reshape(devices, 2 * capacity, half)
             )
         parent_gap = (county_hist - child_total) / tract_count[:, None]

time: 182 us -> 182 us (level)
  no operation moved by 1% of the time
where the time goes in v12:
time: 182 us
  waiting for transfers between devices  68.2 us (37%)
  blocking collectives  45.1 us (25%)
  matrix products  34.7 us (19%)
  local copies, waits for them, and re-layouts  16.2 us (9%)
  starting transfers between devices  14.1 us (8%)
  other arithmetic  2.33 us (1%)
    all_to_all x1, waiting for transfers between devices, local(): lax.all_to_all(grouped, ('region', 'unit'), split_axis=0, concat_axis=0,...  45.4 us
    all_to_all x1, blocking collectives, unit_sum(): arrived = lax.all_to_all(grouped, 'unit', 0, 0, tiled=True)  25.9 us
    all_to_all x1, blocking collectives, unit_gather(): arrived = lax.all_to_all(spread, 'unit', 0, 0, tiled=True)  19.2 us
    dot_general x2, matrix products, local(): lax.dot_general(misfit, strategy, (((1,), (1,)), ((), ())), preferred_ele...  17.6 us
    all_to_all x1, waiting for transfers between devices, unit_sum(): arrived = lax.all_to_all(grouped, 'unit', 0, 0, tiled=True)  15 us
    all_to_all x1, waiting for transfers between devices, unit_gather(): arrived = lax.all_to_all(spread, 'unit', 0, 0, tiled=True)  7.78 us
    dot_general x1, matrix products, local(): jnp.dot(estimate.astype(jnp.bfloat16), strategy, preferred_element_type=j...  6.71 us
    all_to_all x1, starting transfers between devices, local(): lax.all_to_all(grouped, ('region', 'unit'), split_axis=0, concat_axis=0,...  6.45 us
  transfers between devices with their start and end apart: 3, of which 3 were waited for; matrix products, arithmetic and copies ran while one was open for 9% of the time, Pallas kernels for 0%

profile of v12, /device:TPU:6, one launch (start us, length us, event | category | flops | bytes accessed | tf_op | source)
XLA Modules:
  0.0 181.6 jit_solution(10811832306145426141)
XLA Ops:
  0.6 0.7 broadcast_add_fusion.3
  1.3 0.1 convert_reduce_fusion
  1.4 6.1 %fusion.3 = f32[256,2048]{1,0:T(8,128)S(1)} fusion(bf16[2048,2048]{1,0:T(8,128)(2,1)} %param.6, bf16[256,2048]{1,0:T(8,128)(2,1)} %param.5), kind=kOutput, calls=%fused_computation.10 | convolution fusion | flops 2149056512 | bytes 11534336 | tf_op jit(solution)/shard_map/dot_general | solution.py:64
  7.5 0.9 fusion.35
  8.5 0.1 broadcast_in_dim.25
  8.5 0.1 maximum_bitcast_fusion
  8.6 0.0 copy-start.1
  8.7 25.9 %all_to_all.25 = f32[16,8,2176]{2,1,0:T(8,128)S(1)} all-to-all(f32[16,8,2176]{2,1,0:T(8,128)S(1)} %maximum_bitcast_fusion), channel_id=1, replica_groups=mesh['region'=8,'unit'=16] {'unit'}, dimensions={0} | all-to-all | bytes 2228224 | tf_op jit(solution)/shard_map/all_to_all | solution.py:30
  34.6 0.1 reduce_sum.48
  34.6 0.1 slice_reduce_fusion
  34.7 0.0 copy-done.1
  34.7 0.1 fusion.36
  34.8 0.1 broadcast_in_dim.26
  34.9 19.2 %all_to_all.26 = f32[16,8,2048]{2,1,0:T(8,128)S(1)} all-to-all(f32[16,8,2048]{2,1,0:T(8,128)S(1)} %broadcast_in_dim.26), channel_id=1, replica_groups=mesh['region'=8,'unit'=16] {'unit'}, dimensions={0} | all-to-all | bytes 2097152 | tf_op jit(solution)/shard_map/all_to_all | solution.py:36
  54.2 0.0 copy-start.3
  54.2 2.4 %convolution_add_fusion.1 = f32[256,2048]{1,0:T(8,128)} fusion(f32[256,2048]{1,0:T(8,128)S(1)} %fusion.3, f32[16,8,2048]{2,1,0:T(8,128)S(1)} %all_to_all.26, s32[256]{0:T(256)S(1)} %get-tuple-element.9), kind=kOutput, calls=%fused_computation.9 | convolution fusion | flops 805863424 | bytes 5243904 | tf_op jit(solution)/shard_map/dot_general | solution.py:116
  56.5 0.0 copy-done.3
  56.5 11.5 %fusion.4 = f32[256,2048]{1,0:T(8,128)S(1)} fusion(f32[256,2048]{1,0:T(8,128)} %convolution_add_fusion.1, bf16[2048,2048]{1,0:T(8,128)(2,1)} %param.6, bf16[256,2048]{1,0:T(8,128)(2,1)S(1)} %copy-done.3), kind=kOutput, calls=%fused_computation.11 | convolution fusion | flops 4298113024 | bytes 13631488 | tf_op jit(solution)/shard_map/dot_general | solution.py:64
  68.0 1.9 %convolution_bitcast_fusion = f32[16,8,2048]{2,1,0:T(8,128)} fusion(f32[256,2048]{1,0:T(8,128)S(1)} %fusion.4, s32[256]{0:T(256)S(1)} %get-tuple-element.9), kind=kOutput, calls=%fused_computation.16 | convolution fusion | flops 805339136 | bytes 3146752 | tf_op jit(solution)/shard_map/dot_general | solution.py:68
  69.9 0.0 copy-start.2
  69.9 3.8 %all-to-all-start.2 = ((f32[16,8,2048]{2,1,0:T(8,128)}), f32[16,8,2048]{2,1,0:T(8,128)S(1)}, u32[]{:S(2)}, u32[]{:S(2)}) async-start(f32[16,8,2048]{2,1,0:T(8,128)} %convolution_bitcast_fusion), calls=%async_computation.2 | async-start | bytes 2097152 | tf_op jit(solution)/shard_map/all_to_all | solution.py:30
  73.8 15.0 %all-to-all-done.2 = f32[16,8,2048]{2,1,0:T(8,128)S(1)} async-done(((f32[16,8,2048]{2,1,0:T(8,128)}), f32[16,8,2048]{2,1,0:T(8,128)S(1)}, u32[]{:S(2)}, u32[]{:S(2)}) %all-to-all-start.2) | async-done | bytes 1048608 | tf_op jit(solution)/shard_map/all_to_all | solution.py:30
  88.8 0.1 reduce_sum.49
  88.8 0.1 subtract_divide_fusion
  88.9 0.0 copy-done.2
  88.9 0.1 copy.10
  89.0 0.2 fusion.31
  89.3 0.2 fusion.33
  89.5 1.1 broadcast_in_dim.27
  90.6 3.8 %all-to-all-start.3 = ((f32[16,8,2048]{2,1,0:T(8,128)}), f32[16,8,2048]{2,1,0:T(8,128)S(1)}, u32[]{:S(2)}, u32[]{:S(2)}) async-start(f32[16,8,2048]{2,1,0:T(8,128)} %broadcast_in_dim.27), calls=%async_computation.3 | async-start | bytes 2097152 | tf_op jit(solution)/shard_map/all_to_all | solution.py:36
  94.5 0.1 iota_add_fusion
  94.6 0.1 add.90
  94.7 0.1 select_reduce_fusion
  94.9 0.1 broadcast_in_dim.31
  95.0 0.2 eq.82
  95.2 1.5 reshape.99
  96.7 5.5 %scatter_custom_fusion = f32[1024,1024]{1,0:T(8,128)} fusion(s32[512]{0:T(512)S(1)} %bitcast.52, f32[512,1024]{1,0:T(8,128)} %reshape.99, f32[]{:T(128)} %constant.50.clone.1), kind=kCustom, calls=%fused_computation.17 | custom fusion | bytes 4194816 | tf_op jit(solution)/shard_map/scatter | solution.py:111
  102.2 7.8 %all-to-all-done.3 = f32[16,8,2048]{2,1,0:T(8,128)S(1)} async-done(((f32[16,8,2048]{2,1,0:T(8,128)}), f32[16,8,2048]{2,1,0:T(8,128)S(1)}, u32[]{:S(2)}, u32[]{:S(2)}) %all-to-all-start.3) | async-done | bytes 1048608 | tf_op jit(solution)/shard_map/all_to_all | solution.py:36
  110.0 0.3 reduce-precision_convert_fusion.1
  110.3 0.0 copy-start
  110.3 0.2 pad_maximum_fusion
  110.5 0.1 fusion.54
  110.6 1.9 %copy-done = f32[1024,1024]{1,0:T(8,128)S(1)} copy-done((f32[1024,1024]{1,0:T(8,128)S(1)}, f32[1024,1024]{1,0:T(8,128)}, u32[]{:S(2)}) %copy-start) | copy-done | bytes 4194328
  112.5 4.2 %add_bitcast_fusion = f32[128,8,1024]{2,1,0:T(8,128)} fusion(f32[1024,1024]{1,0:T(8,128)S(1)} %copy-done, bf16[384,1024]{1,0:T(8,128)(2,1)S(1)} %get-tuple-element.11, bf16[384,1024]{1,0:T(8,128)(2,1)S(1)} %get-tuple-element.10, s32[1024]{0:T(1024)S(1)} %eq.82, s32[768]{0:T(1024)S(1)} %get-tuple-element.16, s32[768]{0:T(1024)S(1)} %get-tuple-element.17, ...), kind=kOutput, calls=%fused_computation.1 | convolution fusion | flops 1619525632 | bytes 9988608 | tf_op jit(solution)/shard_map/dot_general | solution.py:121
  116.7 6.5 %all-to-all-start.4 = ((f32[128,8,1024]{2,1,0:T(8,128)}), f32[128,8,1024]{2,1,0:T(8,128)}, u32[]{:S(2)}, u32[]{:S(2)}) async-start(f32[128,8,1024]{2,1,0:T(8,128)} %add_bitcast_fusion), calls=%async_computation.4 | async-start | bytes 8388608 | tf_op jit(solution)/shard_map/all_to_all | solution.py:126
  123.1 1.1 fusion.6
  124.2 6.7 %convolution_convert_fusion = bf16[256,2048]{1,0:T(8,128)(2,1)} fusion(bf16[256,2048]{1,0:T(8,128)(2,1)S(1)} %fusion.6, bf16[2048,2048]{1,0:T(8,128)(2,1)} %param.6), kind=kOutput, calls=%fused_computation.15 | convolution fusion | flops 2148007936 | bytes 10485760 | tf_op jit(solution)/shard_map/dot_general | solution.py:123
  130.9 45.4 %all-to-all-done.4 = f32[128,8,1024]{2,1,0:T(8,128)} async-done(((f32[128,8,1024]{2,1,0:T(8,128)}), f32[128,8,1024]{2,1,0:T(8,128)}, u32[]{:S(2)}, u32[]{:S(2)}) %all-to-all-start.4) | async-done | bytes 4194336 | tf_op jit(solution)/shard_map/all_to_all | solution.py:126
  176.4 5.2 %reshape.94 = f32[512,2048]{1,0:T(8,128)} reshape(f32[128,8,1024]{2,1,0:T(8,128)} %all-to-all-done.4) | data formatting | bytes 8388608 | tf_op jit(solution)/shard_map/reshape | solution.py:127
  (15 shorter events, 0.1 us)
Async XLA Ops:
  8.6 26.1 %copy-start.1 = (f32[8,2048]{1,0:T(8,128)S(1)}, f32[8,2048]{1,0:T(8,128)}, u32[]{:S(2)}) copy-start(f32[8,2048]{1,0:T(8,128)} %param.7) | copy-start | bytes 196612
  54.2 2.4 %copy-start.3 = (bf16[256,2048]{1,0:T(8,128)(2,1)S(1)}, bf16[256,2048]{1,0:T(8,128)(2,1)}, u32[]{:S(2)}) copy-start(bf16[256,2048]{1,0:T(8,128)(2,1)} %param.5) | copy-start | bytes 3145732
  69.9 19.0 %copy-start.2 = (s32[256,1]{0,1:T(1,128)S(1)}, s32[256,1]{0,1:T(1,128)}, u32[]{:S(2)}) copy-start(s32[256,1]{0,1:T(1,128)} %param.9) | copy-start | bytes 3076
  69.9 18.9 %all-to-all-start.2 = ((f32[16,8,2048]{2,1,0:T(8,128)}), f32[16,8,2048]{2,1,0:T(8,128)S(1)}, u32[]{:S(2)}, u32[]{:S(2)}) async-start(f32[16,8,2048]{2,1,0:T(8,128)} %convolution_bitcast_fusion), calls=%async_computation.2 | async-start | bytes 2097152 | tf_op jit(solution)/shard_map/all_to_all | solution.py:30
  90.6 19.4 %all-to-all-start.3 = ((f32[16,8,2048]{2,1,0:T(8,128)}), f32[16,8,2048]{2,1,0:T(8,128)S(1)}, u32[]{:S(2)}, u32[]{:S(2)}) async-start(f32[16,8,2048]{2,1,0:T(8,128)} %broadcast_in_dim.27), calls=%async_computation.3 | async-start | bytes 2097152 | tf_op jit(solution)/shard_map/all_to_all | solution.py:36
  110.3 2.2 %copy-start = (f32[1024,1024]{1,0:T(8,128)S(1)}, f32[1024,1024]{1,0:T(8,128)}, u32[]{:S(2)}) copy-start(f32[1024,1024]{1,0:T(8,128)} %scatter_custom_fusion) | copy-start | bytes 12582916
  116.7 59.7 %all-to-all-start.4 = ((f32[128,8,1024]{2,1,0:T(8,128)}), f32[128,8,1024]{2,1,0:T(8,128)}, u32[]{:S(2)}, u32[]{:S(2)}) async-start(f32[128,8,1024]{2,1,0:T(8,128)} %add_bitcast_fusion), calls=%async_computation.4 | async-start | bytes 8388608 | tf_op jit(solution)/shard_map/all_to_all | solution.py:126

commit v13 on v9

--- a/solution.py
+++ b/solution.py
@@ -46,9 +46,10 @@
     county_region = county_hist.shape[0] * unit_count
     first_county = lax.axis_index("region") * county_region
     local_id = tract_county - first_county
-    member = (local_id[:, None] == jnp.arange(county_region, dtype=jnp.int32)[None, :]).astype(
-        jnp.float32
-    )
+    member_bf16 = (
+        local_id[:, None] == jnp.arange(county_region, dtype=jnp.int32)[None, :]
+    ).astype(jnp.bfloat16)
+    member = member_bf16.astype(jnp.float32)
     county_tally = jnp.sum(member, axis=0)
     tally_lanes = 128
     estimate = jnp.zeros((tract_rows, width), jnp.float32)
@@ -105,9 +106,19 @@
             )
         parent_gap = (county_hist - child_total) / tract_count[:, None]
         region_gap = unit_gather(parent_gap, unit_count)
-        estimate = stepped + jnp.dot(
-            member, region_gap, precision=lax.Precision.HIGHEST, preferred_element_type=jnp.float32
-        )
+        if iteration < ITERS - 1:
+            pieces = bf16_pieces(region_gap).reshape(3, county_region, width)
+            picks = [
+                jnp.dot(member_bf16, piece, preferred_element_type=jnp.float32) for piece in pieces
+            ]
+            estimate = stepped + ((picks[0] + picks[1]) + picks[2])
+        else:
+            estimate = stepped + jnp.dot(
+                member,
+                region_gap,
+                precision=lax.Precision.HIGHEST,
+                preferred_element_type=jnp.float32,
+            )
     grouped = slot_stepped + one_hot_pick(slot_member, bf16_pieces(region_gap))
     released = jnp.dot(
         estimate.astype(jnp.bfloat16), strategy, preferred_element_type=jnp.float32

time: 182 us -> 182 us (level)
    dot_general x0 -> x3, matrix products: none -> 2.83 us  [local(): jnp.dot(member_bf16, piece, preferred_element_type=jnp.float32)]
    dot_general x2 -> x1, matrix products: 3.43 us -> 1.07 us  [local(): jnp.dot(member, region_gap, precision=lax.Precision.HIGHEST, preferred_el...]
where the time goes in v13:
time: 182 us; the launch traced here: 181 us
  blocking collectives  63.2 us (35%)
  waiting for transfers between devices  48.8 us (27%)
  matrix products  35.1 us (19%)
  local copies, waits for them, and re-layouts  20.9 us (11%)
  starting transfers between devices  10.3 us (6%)
  other arithmetic  2.17 us (1%)
    all_to_all x1, waiting for transfers between devices, local(): lax.all_to_all(grouped, ('region', 'unit'), split_axis=0, concat_axis=0,...  45.4 us
    all_to_all x2, blocking collectives, unit_sum(): arrived = lax.all_to_all(grouped, 'unit', 0, 0, tiled=True)  43.9 us
    all_to_all x1, blocking collectives, unit_gather(): arrived = lax.all_to_all(spread, 'unit', 0, 0, tiled=True)  19.2 us
    dot_general x2, matrix products, local(): lax.dot_general(misfit, strategy, (((1,), (1,)), ((), ())), preferred_ele...  17.6 us
    dot_general x1, matrix products, local(): jnp.dot(estimate.astype(jnp.bfloat16), strategy, preferred_element_type=j...  6.72 us
    all_to_all x1, starting transfers between devices, local(): lax.all_to_all(grouped, ('region', 'unit'), split_axis=0, concat_axis=0,...  6.46 us
    reshape x1, local copies, waits for them, and re-layouts, local(): relaid = arrived.reshape(devices * capacity, width)  5.27 us
    reshape x1, local copies, waits for them, and re-layouts, local(): slot_stepped = jnp.zeros((devices * capacity, width), jnp.float32).at[tar...  5.17 us
  transfers between devices with their start and end apart: 2, of which 2 were waited for; matrix products, arithmetic and copies ran while one was open for 10% of the time, Pallas kernels for 0%

profile of v13, /device:TPU:6, one launch (start us, length us, event | category | flops | bytes accessed | tf_op | source)
XLA Modules:
  0.0 181.3 jit_solution(7171060432697648040)
XLA Ops:
  0.6 0.7 broadcast_add_fusion.2
  1.3 0.1 convert_reduce_fusion
  1.4 6.1 %fusion.1 = f32[256,2048]{1,0:T(8,128)S(1)} fusion(bf16[2048,2048]{1,0:T(8,128)(2,1)} %param.6, bf16[256,2048]{1,0:T(8,128)(2,1)} %param.5), kind=kOutput, calls=%fused_computation.8 | convolution fusion | flops 2149056512 | bytes 11534336 | tf_op jit(solution)/shard_map/dot_general | solution.py:65
  7.5 0.9 fusion.30
  8.5 0.1 broadcast_in_dim.19
  8.5 0.1 maximum_bitcast_fusion.2
  8.6 0.0 copy-start
  8.7 25.9 %all_to_all.25 = f32[16,8,2176]{2,1,0:T(8,128)S(1)} all-to-all(f32[16,8,2176]{2,1,0:T(8,128)S(1)} %maximum_bitcast_fusion.2), channel_id=1, replica_groups=mesh['region'=8,'unit'=16] {'unit'}, dimensions={0} | all-to-all | bytes 2228224 | tf_op jit(solution)/shard_map/all_to_all | solution.py:30
  34.6 0.1 reduce_sum.48
  34.6 0.1 slice_reduce_fusion
  34.7 0.0 copy-done
  34.7 0.1 fusion.31
  34.8 0.1 broadcast_in_dim.24
  34.9 19.2 %all_to_all.26 = f32[16,8,2048]{2,1,0:T(8,128)S(1)} all-to-all(f32[16,8,2048]{2,1,0:T(8,128)S(1)} %broadcast_in_dim.24), channel_id=1, replica_groups=mesh['region'=8,'unit'=16] {'unit'}, dimensions={0} | all-to-all | bytes 2097152 | tf_op jit(solution)/shard_map/all_to_all | solution.py:36
  54.2 0.5 fusion.19
  54.6 0.5 convolution_add_fusion.2
  55.1 0.0 copy-start.2
  55.1 1.9 %fusion = f32[256,2048]{1,0:T(8,128)} fusion(f32[256,2048]{1,0:T(8,128)S(1)} %fusion.1, f32[256,2048]{1,0:T(8,128)S(1)} %convolution_add_fusion.2, f32[16,8,2048]{2,1,0:T(8,128)S(1)} %all_to_all.26, s32[256]{0:T(256)S(1)} %get-tuple-element.7), kind=kOutput, calls=%fused_computation.6 | convolution fusion | flops 136609792 | bytes 7341056 | tf_op jit(solution)/shard_map/dot_general | solution.py:112
  57.0 0.0 copy-done.2
  57.0 11.5 %fusion.2 = f32[256,2048]{1,0:T(8,128)S(1)} fusion(f32[256,2048]{1,0:T(8,128)} %fusion, bf16[2048,2048]{1,0:T(8,128)(2,1)} %param.6, bf16[256,2048]{1,0:T(8,128)(2,1)S(1)} %copy-done.2), kind=kOutput, calls=%fused_computation.9 | convolution fusion | flops 4298113024 | bytes 13631488 | tf_op jit(solution)/shard_map/dot_general | solution.py:65
  68.5 0.9 convolution_bitcast_fusion
  69.4 0.0 copy-start.1
  69.5 18.0 %all_to_all.27 = f32[16,8,2048]{2,1,0:T(8,128)S(1)} all-to-all(f32[16,8,2048]{2,1,0:T(8,128)S(1)} %convolution_bitcast_fusion), channel_id=1, replica_groups=mesh['region'=8,'unit'=16] {'unit'}, dimensions={0} | all-to-all | bytes 2097152 | tf_op jit(solution)/shard_map/all_to_all | solution.py:30
  87.5 0.1 reduce_sum.49
  87.5 0.1 subtract_divide_fusion
  87.6 0.0 copy-done.1
  87.6 0.1 copy.18
  87.7 0.2 fusion.25
  88.0 1.1 broadcast_in_dim.25
  89.1 3.8 %all-to-all-start.3 = ((f32[16,8,2048]{2,1,0:T(8,128)}), f32[16,8,2048]{2,1,0:T(8,128)S(1)}, u32[]{:S(2)}, u32[]{:S(2)}) async-start(f32[16,8,2048]{2,1,0:T(8,128)} %broadcast_in_dim.25), calls=%async_computation.3 | async-start | bytes 2097152 | tf_op jit(solution)/shard_map/all_to_all | solution.py:36
  93.0 0.2 fusion.27
  93.2 0.2 select_reduce_fusion
  93.3 0.1 sub.53
  93.4 0.1 copy.20
  93.5 4.1 %scatter_custom_fusion = f32[512,2048]{1,0:T(8,128)} fusion(s32[256]{0:T(256)S(1)} %bitcast.58, f32[256,2048]{1,0:T(8,128)S(1)} %fusion.2, f32[]{:T(128)} %constant.10.clone.1), kind=kCustom, calls=%fused_computation.15 | custom fusion | bytes 4194308 | tf_op jit(solution)/shard_map/scatter | solution.py:104
  97.6 5.2 %reshape.80 = f32[128,4,2048]{2,1,0:T(4,128)} reshape(f32[512,2048]{1,0:T(8,128)} %scatter_custom_fusion) | data formatting | bytes 8388608 | tf_op jit(solution)/shard_map/reshape | solution.py:105
  102.8 0.1 convert_convert_fusion
  102.9 3.4 %all-to-all-done.3 = f32[16,8,2048]{2,1,0:T(8,128)S(1)} async-done(((f32[16,8,2048]{2,1,0:T(8,128)}), f32[16,8,2048]{2,1,0:T(8,128)S(1)}, u32[]{:S(2)}, u32[]{:S(2)}) %all-to-all-start.3) | async-done | bytes 1048608 | tf_op jit(solution)/shard_map/all_to_all | solution.py:36
  106.3 0.3 reduce-precision_convert_fusion.1
  106.6 5.1 %copy_add_fusion = f32[128,4,2048]{2,0,1:T(8,128)S(1)} fusion(f32[128,4,2048]{2,1,0:T(4,128)} %reshape.80, bf16[128,2048]{1,0:T(8,128)(2,1)S(1)} %get-tuple-element.9, bf16[128,2048]{1,0:T(8,128)(2,1)S(1)} %get-tuple-element.10, bf16[128,2048]{1,0:T(8,128)(2,1)S(1)} %get-tuple-element.8, bf16[128,4,128]{2,0,1:T(8,128)(2,1)S(1)} %convert_convert_fusion), kind=kOutput, calls=%fused_computation.1 | convolution fusion | flops 812253184 | bytes 10092544 | tf_op jit(solution)/shard_map/...k,kh->...h/dot_general | solution.py:24
  111.7 4.7 %copy.22 = f32[128,4,2048]{2,1,0:T(4,128)} copy(f32[128,4,2048]{2,0,1:T(8,128)S(1)} %copy_add_fusion) | data formatting | bytes 8388608 | tf_op jit(solution)/shard_map/add | solution.py:122
  116.4 6.5 %all-to-all-start.4 = ((f32[128,4,2048]{2,1,0:T(4,128)}), f32[128,4,2048]{2,1,0:T(4,128)}, u32[]{:S(2)}, u32[]{:S(2)}) async-start(f32[128,4,2048]{2,1,0:T(4,128)} %copy.22), calls=%async_computation.4 | async-start | bytes 8388608 | tf_op jit(solution)/shard_map/all_to_all | solution.py:126
  122.9 1.1 fusion.4
  123.9 6.7 %convolution_convert_fusion = bf16[256,2048]{1,0:T(8,128)(2,1)} fusion(bf16[256,2048]{1,0:T(8,128)(2,1)S(1)} %fusion.4, bf16[2048,2048]{1,0:T(8,128)(2,1)} %param.6), kind=kOutput, calls=%fused_computation.13 | convolution fusion | flops 2148007936 | bytes 10485760 | tf_op jit(solution)/shard_map/dot_general | solution.py:123
  130.7 45.4 %all-to-all-done.4 = f32[128,4,2048]{2,1,0:T(4,128)} async-done(((f32[128,4,2048]{2,1,0:T(4,128)}), f32[128,4,2048]{2,1,0:T(4,128)}, u32[]{:S(2)}, u32[]{:S(2)}) %all-to-all-start.4) | async-done | bytes 4194336 | tf_op jit(solution)/shard_map/all_to_all | solution.py:126
  176.1 5.3 %reshape.81 = f32[512,2048]{1,0:T(8,128)} reshape(f32[128,4,2048]{2,1,0:T(4,128)} %all-to-all-done.4) | data formatting | bytes 8388608 | tf_op jit(solution)/shard_map/reshape | solution.py:127
  (9 shorter events, 0.1 us)
Async XLA Ops:
  8.6 26.1 %copy-start = (f32[8,2048]{1,0:T(8,128)S(1)}, f32[8,2048]{1,0:T(8,128)}, u32[]{:S(2)}) copy-start(f32[8,2048]{1,0:T(8,128)} %param.7) | copy-start | bytes 196612
  55.1 1.9 %copy-start.2 = (bf16[256,2048]{1,0:T(8,128)(2,1)S(1)}, bf16[256,2048]{1,0:T(8,128)(2,1)}, u32[]{:S(2)}) copy-start(bf16[256,2048]{1,0:T(8,128)(2,1)} %param.5) | copy-start | bytes 3145732
  69.4 18.2 %copy-start.1 = (s32[256,1]{0,1:T(1,128)S(1)}, s32[256,1]{0,1:T(1,128)}, u32[]{:S(2)}) copy-start(s32[256,1]{0,1:T(1,128)} %param.9) | copy-start | bytes 3076
  89.1 17.2 %all-to-all-start.3 = ((f32[16,8,2048]{2,1,0:T(8,128)}), f32[16,8,2048]{2,1,0:T(8,128)S(1)}, u32[]{:S(2)}, u32[]{:S(2)}) async-start(f32[16,8,2048]{2,1,0:T(8,128)} %broadcast_in_dim.25), calls=%async_computation.3 | async-start | bytes 2097152 | tf_op jit(solution)/shard_map/all_to_all | solution.py:36
  116.4 59.7 %all-to-all-start.4 = ((f32[128,4,2048]{2,1,0:T(4,128)}), f32[128,4,2048]{2,1,0:T(4,128)}, u32[]{:S(2)}, u32[]{:S(2)}) async-start(f32[128,4,2048]{2,1,0:T(4,128)} %copy.22), calls=%async_computation.4 | async-start | bytes 8388608 | tf_op jit(solution)/shard_map/all_to_all | solution.py:126

commit v14 on v10

--- a/solution.py
+++ b/solution.py
@@ -96,11 +96,12 @@
             slot_county = jnp.sum(jnp.where(slot_hits, local_id[None, :] + 1, 0), axis=1) - 1
             half = width // 2
             row_county = jnp.repeat(slot_county, 2)
-            row_half = jnp.tile(jnp.arange(2, dtype=jnp.int32), devices * capacity)
-            k = jnp.arange(2 * 3 * county_region, dtype=jnp.int32)[None, :]
+            pick_shape = (2 * devices * capacity, 2 * 3 * county_region)
+            after = jnp.minimum(owners[0], 0)
+            row = lax.broadcasted_iota(jnp.int32, pick_shape, 0) + after
+            k = lax.broadcasted_iota(jnp.int32, pick_shape, 1) + after
             row_pick = (
-                (k // (3 * county_region) == row_half[:, None])
-                & (k % county_region == row_county[:, None])
+                (k // (3 * county_region) == row % 2) & (k % county_region == row_county[:, None])
             ).astype(jnp.bfloat16)
             slot_stepped = (
                 jnp.zeros((devices * capacity, width), jnp.float32)

time: 181 us -> 179 us (0.989)
  waiting for transfers between devices: 65.7 us -> 47.5 us
  blocking collectives: 45.1 us -> 63.2 us
  starting transfers between devices: 13.9 us -> 11.6 us
    all_to_all x1 -> x2, blocking collectives: 25.9 us -> 43.9 us  [unit_sum(): arrived = lax.all_to_all(grouped, 'unit', 0, 0, tiled=True)]
    all_to_all x1 -> x0, waiting for transfers between devices: 14.8 us -> none  [unit_sum(): arrived = lax.all_to_all(grouped, 'unit', 0, 0, tiled=True)]
    all_to_all x1 -> x0, starting transfers between devices: 3.66 us -> none  [unit_sum(): arrived = lax.all_to_all(grouped, 'unit', 0, 0, tiled=True)]
    all_to_all x1, waiting for transfers between devices: 5.47 us -> 2.03 us  [unit_gather(): arrived = lax.all_to_all(spread, 'unit', 0, 0, tiled=True)]
  transfers between devices with their start and end apart: 3 -> 2, of which waited for: 3 -> 2; matrix products, arithmetic and copies ran while one was open for 10% -> 10% of each run, Pallas kernels for 0% -> 0%
where the time goes in v14:
time: 179 us; the launch traced here: 178 us
  blocking collectives  63.2 us (35%)
  waiting for transfers between devices  47.5 us (27%)
  matrix products  33.8 us (19%)
  local copies, waits for them, and re-layouts  18.5 us (10%)
  starting transfers between devices  11.6 us (6%)
  other arithmetic  2.25 us (1%)
    all_to_all x1, waiting for transfers between devices, local(): lax.all_to_all(grouped, ('region', 'unit'), split_axis=0, concat_axis=0,...  45.4 us
    all_to_all x2, blocking collectives, unit_sum(): arrived = lax.all_to_all(grouped, 'unit', 0, 0, tiled=True)  43.9 us
    all_to_all x1, blocking collectives, unit_gather(): arrived = lax.all_to_all(spread, 'unit', 0, 0, tiled=True)  19.2 us
    dot_general x2, matrix products, local(): lax.dot_general(misfit, strategy, (((1,), (1,)), ((), ())), preferred_ele...  17.6 us
    all_to_all x1, starting transfers between devices, local(): lax.all_to_all(grouped, ('region', 'unit'), split_axis=0, concat_axis=0,...  7.81 us
    dot_general x1, matrix products, local(): jnp.dot(estimate.astype(jnp.bfloat16), strategy, preferred_element_type=j...  6.71 us
    reshape x1, local copies, waits for them, and re-layouts, local(): relaid = arrived.reshape(devices * capacity, width)  5.22 us
    reshape x1, local copies, waits for them, and re-layouts, local(): slot_stepped = jnp.zeros((devices * capacity, width), jnp.float32).at[tar...  4.92 us
  transfers between devices with their start and end apart: 2, of which 2 were waited for; matrix products, arithmetic and copies ran while one was open for 10% of the time, Pallas kernels for 0%

profile of v14, /device:TPU:6, one launch (start us, length us, event | category | flops | bytes accessed | tf_op | source)
XLA Modules:
  0.0 178.3 jit_solution(11214746539798822950)
XLA Ops:
  0.6 0.7 broadcast_add_fusion.5
  1.3 0.1 convert_reduce_fusion
  1.4 6.1 %fusion.3 = f32[256,2048]{1,0:T(8,128)S(1)} fusion(bf16[2048,2048]{1,0:T(8,128)(2,1)} %param.6, bf16[256,2048]{1,0:T(8,128)(2,1)} %param.5), kind=kOutput, calls=%fused_computation.10 | convolution fusion | flops 2149056512 | bytes 11534336 | tf_op jit(solution)/shard_map/dot_general | solution.py:64
  7.5 0.9 fusion.35
  8.5 0.1 broadcast_in_dim.25
  8.5 0.1 maximum_bitcast_fusion
  8.6 0.0 copy-start.1
  8.7 25.9 %all_to_all.25 = f32[16,8,2176]{2,1,0:T(8,128)S(1)} all-to-all(f32[16,8,2176]{2,1,0:T(8,128)S(1)} %maximum_bitcast_fusion), channel_id=1, replica_groups=mesh['region'=8,'unit'=16] {'unit'}, dimensions={0} | all-to-all | bytes 2228224 | tf_op jit(solution)/shard_map/all_to_all | solution.py:30
  34.6 0.1 reduce_sum.48
  34.6 0.1 slice_reduce_fusion
  34.7 0.0 copy-done.1
  34.7 0.1 fusion.36
  34.8 0.1 broadcast_in_dim.26
  34.9 19.2 %all_to_all.26 = f32[16,8,2048]{2,1,0:T(8,128)S(1)} all-to-all(f32[16,8,2048]{2,1,0:T(8,128)S(1)} %broadcast_in_dim.26), channel_id=1, replica_groups=mesh['region'=8,'unit'=16] {'unit'}, dimensions={0} | all-to-all | bytes 2097152 | tf_op jit(solution)/shard_map/all_to_all | solution.py:36
  54.2 0.0 copy-start.3
  54.2 2.4 %convolution_add_fusion.1 = f32[256,2048]{1,0:T(8,128)} fusion(f32[256,2048]{1,0:T(8,128)S(1)} %fusion.3, f32[16,8,2048]{2,1,0:T(8,128)S(1)} %all_to_all.26, s32[256]{0:T(256)S(1)} %get-tuple-element.7), kind=kOutput, calls=%fused_computation.9 | convolution fusion | flops 805863424 | bytes 5243904 | tf_op jit(solution)/shard_map/dot_general | solution.py:114
  56.5 0.0 copy-done.3
  56.5 11.5 %fusion.4 = f32[256,2048]{1,0:T(8,128)S(1)} fusion(f32[256,2048]{1,0:T(8,128)} %convolution_add_fusion.1, bf16[2048,2048]{1,0:T(8,128)(2,1)} %param.6, bf16[256,2048]{1,0:T(8,128)(2,1)S(1)} %copy-done.3), kind=kOutput, calls=%fused_computation.11 | convolution fusion | flops 4298113024 | bytes 13631488 | tf_op jit(solution)/shard_map/dot_general | solution.py:64
  68.0 0.9 convolution_bitcast_fusion
  69.0 18.0 %all_to_all.27 = f32[16,8,2048]{2,1,0:T(8,128)S(1)} all-to-all(f32[16,8,2048]{2,1,0:T(8,128)S(1)} %convolution_bitcast_fusion), channel_id=1, replica_groups=mesh['region'=8,'unit'=16] {'unit'}, dimensions={0} | all-to-all | bytes 2097152 | tf_op jit(solution)/shard_map/all_to_all | solution.py:30
  87.0 0.0 copy-start.2
  87.0 0.1 reduce_sum.49
  87.0 0.1 subtract_divide_fusion
  87.1 1.1 broadcast_in_dim.27
  88.2 3.8 %all-to-all-start.3 = ((f32[16,8,2048]{2,1,0:T(8,128)}), f32[16,8,2048]{2,1,0:T(8,128)S(1)}, u32[]{:S(2)}, u32[]{:S(2)}) async-start(f32[16,8,2048]{2,1,0:T(8,128)} %broadcast_in_dim.27), calls=%async_computation.3 | async-start | bytes 2097152 | tf_op jit(solution)/shard_map/all_to_all | solution.py:36
  92.0 0.0 copy-done.2
  92.0 0.1 copy.10
  92.2 0.2 fusion.31
  92.5 0.2 fusion.33
  92.7 0.5 slice.26
  93.2 4.1 %scatter_custom_fusion = f32[512,2048]{1,0:T(8,128)} fusion(s32[256]{0:T(256)S(1)} %bitcast.50, f32[256,2048]{1,0:T(8,128)S(1)} %fusion.4, f32[]{:T(128)} %constant.48.clone.1), kind=kCustom, calls=%fused_computation.17 | custom fusion | bytes 4194308 | tf_op jit(solution)/shard_map/scatter | solution.py:109
  97.3 4.9 %reshape.66 = f32[128,8,1024]{2,1,0:T(8,128)} reshape(f32[512,2048]{1,0:T(8,128)} %scatter_custom_fusion) | data formatting | bytes 8388608 | tf_op jit(solution)/shard_map/reshape | solution.py:110
  102.2 0.1 select_reduce_fusion
  102.3 0.1 broadcast_in_dim.53
  102.5 0.2 eq.82
  103.3 2.0 %all-to-all-done.3 = f32[16,8,2048]{2,1,0:T(8,128)S(1)} async-done(((f32[16,8,2048]{2,1,0:T(8,128)}), f32[16,8,2048]{2,1,0:T(8,128)S(1)}, u32[]{:S(2)}, u32[]{:S(2)}) %all-to-all-start.3) | async-done | bytes 1048608 | tf_op jit(solution)/shard_map/all_to_all | solution.py:36
  105.4 0.3 reduce-precision_convert_fusion.1
  105.7 0.0 copy-start
  105.7 0.2 pad_maximum_fusion
  105.8 0.1 fusion.47
  106.0 1.9 %copy-done = f32[128,8,1024]{2,1,0:T(8,128)S(1)} copy-done((f32[128,8,1024]{2,1,0:T(8,128)S(1)}, f32[128,8,1024]{2,1,0:T(8,128)}, u32[]{:S(2)}) %copy-start) | copy-done | bytes 4194328
  107.8 4.2 %bitcast_add_fusion = f32[128,8,1024]{2,1,0:T(8,128)} fusion(f32[128,8,1024]{2,1,0:T(8,128)S(1)} %copy-done, bf16[384,1024]{1,0:T(8,128)(2,1)S(1)} %get-tuple-element.9, bf16[384,1024]{1,0:T(8,128)(2,1)S(1)} %get-tuple-element.8, s32[1024]{0:T(1024)S(1)} %eq.82, s32[768]{0:T(1024)S(1)} %get-tuple-element.13, s32[768]{0:T(1024)S(1)} %get-tuple-element.19, ...), kind=kOutput, calls=%fused_computation.1 | convolution fusion | flops 1619525632 | bytes 9988608 | tf_op jit(solution)/shard_map/dot_general | solution.py:119
  112.0 7.8 %all-to-all-start.4 = ((f32[128,8,1024]{2,1,0:T(8,128)}), f32[128,8,1024]{2,1,0:T(8,128)}, u32[]{:S(2)}, u32[]{:S(2)}) async-start(f32[128,8,1024]{2,1,0:T(8,128)} %bitcast_add_fusion), calls=%async_computation.4 | async-start | bytes 8388608 | tf_op jit(solution)/shard_map/all_to_all | solution.py:124
  119.9 1.1 fusion.6
  120.9 6.7 %convolution_convert_fusion = bf16[256,2048]{1,0:T(8,128)(2,1)} fusion(bf16[256,2048]{1,0:T(8,128)(2,1)S(1)} %fusion.6, bf16[2048,2048]{1,0:T(8,128)(2,1)} %param.6), kind=kOutput, calls=%fused_computation.15 | convolution fusion | flops 2148007936 | bytes 10485760 | tf_op jit(solution)/shard_map/dot_general | solution.py:121
  127.6 45.4 %all-to-all-done.4 = f32[128,8,1024]{2,1,0:T(8,128)} async-done(((f32[128,8,1024]{2,1,0:T(8,128)}), f32[128,8,1024]{2,1,0:T(8,128)}, u32[]{:S(2)}, u32[]{:S(2)}) %all-to-all-start.4) | async-done | bytes 4194336 | tf_op jit(solution)/shard_map/all_to_all | solution.py:124
  173.1 5.2 %reshape.68 = f32[512,2048]{1,0:T(8,128)} reshape(f32[128,8,1024]{2,1,0:T(8,128)} %all-to-all-done.4) | data formatting | bytes 8388608 | tf_op jit(solution)/shard_map/reshape | solution.py:125
  (14 shorter events, 0.2 us)
Async XLA Ops:
  8.6 26.1 %copy-start.1 = (f32[8,2048]{1,0:T(8,128)S(1)}, f32[8,2048]{1,0:T(8,128)}, u32[]{:S(2)}) copy-start(f32[8,2048]{1,0:T(8,128)} %param.7) | copy-start | bytes 196612
  54.2 2.4 %copy-start.3 = (bf16[256,2048]{1,0:T(8,128)(2,1)S(1)}, bf16[256,2048]{1,0:T(8,128)(2,1)}, u32[]{:S(2)}) copy-start(bf16[256,2048]{1,0:T(8,128)(2,1)} %param.5) | copy-start | bytes 3145732
  87.0 5.1 %copy-start.2 = (s32[256,1]{0,1:T(1,128)S(1)}, s32[256,1]{0,1:T(1,128)}, u32[]{:S(2)}) copy-start(s32[256,1]{0,1:T(1,128)} %param.9) | copy-start | bytes 3076
  88.2 17.2 %all-to-all-start.3 = ((f32[16,8,2048]{2,1,0:T(8,128)}), f32[16,8,2048]{2,1,0:T(8,128)S(1)}, u32[]{:S(2)}, u32[]{:S(2)}) async-start(f32[16,8,2048]{2,1,0:T(8,128)} %broadcast_in_dim.27), calls=%async_computation.3 | async-start | bytes 2097152 | tf_op jit(solution)/shard_map/all_to_all | solution.py:36
  105.7 2.2 %copy-start = (f32[128,8,1024]{2,1,0:T(8,128)S(1)}, f32[128,8,1024]{2,1,0:T(8,128)}, u32[]{:S(2)}) copy-start(f32[128,8,1024]{2,1,0:T(8,128)} %reshape.66) | copy-start | bytes 12582916
  112.0 61.1 %all-to-all-start.4 = ((f32[128,8,1024]{2,1,0:T(8,128)}), f32[128,8,1024]{2,1,0:T(8,128)}, u32[]{:S(2)}, u32[]{:S(2)}) async-start(f32[128,8,1024]{2,1,0:T(8,128)} %bitcast_add_fusion), calls=%async_computation.4 | async-start | bytes 8388608 | tf_op jit(solution)/shard_map/all_to_all | solution.py:124

commit v15 on v14

--- a/solution.py
+++ b/solution.py
@@ -114,8 +114,13 @@
         estimate = stepped + jnp.dot(
             member, region_gap, precision=lax.Precision.HIGHEST, preferred_element_type=jnp.float32
         )
-    gap_pieces = bf16_pieces(region_gap)
-    halves = jnp.concatenate([gap_pieces[:, :half], gap_pieces[:, half:]], axis=0)
+    high = lax.reduce_precision(region_gap, exponent_bits=8, mantissa_bits=7)
+    middle = lax.reduce_precision(region_gap - high, exponent_bits=8, mantissa_bits=7)
+    low = (region_gap - high) - middle
+    split = [part.astype(jnp.bfloat16) for part in (high, middle, low)]
+    halves = jnp.concatenate(
+        [part[:, :half] for part in split] + [part[:, half:] for part in split], axis=0
+    )
     picked = jnp.dot(row_pick, halves, preferred_element_type=jnp.float32)
     grouped = slot_stepped + picked.reshape(devices, 2 * capacity, half)
     released = jnp.dot(

time: 179 us -> 179 us (level)
  no operation moved by 1% of the time
where the time goes in v15:
time: 179 us; the launch traced here: 178 us
  blocking collectives  63.2 us (35%)
  waiting for transfers between devices  47.5 us (27%)
  matrix products  33.9 us (19%)
  local copies, waits for them, and re-layouts  18.4 us (10%)
  starting transfers between devices  11.6 us (6%)
  other arithmetic  2.09 us (1%)
    all_to_all x1, waiting for transfers between devices, local(): lax.all_to_all(grouped, ('region', 'unit'), split_axis=0, concat_axis=0,...  45.4 us
    all_to_all x2, blocking collectives, unit_sum(): arrived = lax.all_to_all(grouped, 'unit', 0, 0, tiled=True)  43.9 us
    all_to_all x1, blocking collectives, unit_gather(): arrived = lax.all_to_all(spread, 'unit', 0, 0, tiled=True)  19.2 us
    dot_general x2, matrix products, local(): lax.dot_general(misfit, strategy, (((1,), (1,)), ((), ())), preferred_ele...  17.8 us
    all_to_all x1, starting transfers between devices, local(): lax.all_to_all(grouped, ('region', 'unit'), split_axis=0, concat_axis=0,...  7.81 us
    dot_general x1, matrix products, local(): jnp.dot(estimate.astype(jnp.bfloat16), strategy, preferred_element_type=j...  6.71 us
    reshape x1, local copies, waits for them, and re-layouts, local(): relaid = arrived.reshape(devices * capacity, width)  5.22 us
    reshape x1, local copies, waits for them, and re-layouts, local(): slot_stepped = jnp.zeros((devices * capacity, width), jnp.float32).at[tar...  4.92 us
  transfers between devices with their start and end apart: 2, of which 2 were waited for; matrix products, arithmetic and copies ran while one was open for 10% of the time, Pallas kernels for 0%

profile of v15, /device:TPU:6, one launch (start us, length us, event | category | flops | bytes accessed | tf_op | source)
XLA Modules:
  0.0 178.2 jit_solution(17387971451153078979)
XLA Ops:
  0.6 0.7 broadcast_add_fusion.5
  1.3 0.1 convert_reduce_fusion
  1.4 6.1 %fusion.3 = f32[256,2048]{1,0:T(8,128)S(1)} fusion(bf16[2048,2048]{1,0:T(8,128)(2,1)} %param.6, bf16[256,2048]{1,0:T(8,128)(2,1)} %param.5), kind=kOutput, calls=%fused_computation.10 | convolution fusion | flops 2149056512 | bytes 11534336 | tf_op jit(solution)/shard_map/dot_general | solution.py:64
  7.5 0.9 fusion.32
  8.5 0.1 broadcast_in_dim.25
  8.5 0.1 maximum_bitcast_fusion
  8.6 0.0 copy-start.1
  8.7 25.9 %all_to_all.25 = f32[16,8,2176]{2,1,0:T(8,128)S(1)} all-to-all(f32[16,8,2176]{2,1,0:T(8,128)S(1)} %maximum_bitcast_fusion), channel_id=1, replica_groups=mesh['region'=8,'unit'=16] {'unit'}, dimensions={0} | all-to-all | bytes 2228224 | tf_op jit(solution)/shard_map/all_to_all | solution.py:30
  34.6 0.1 reduce_sum.48
  34.6 0.1 slice_reduce_fusion
  34.7 0.0 copy-done.1
  34.7 0.1 fusion.33
  34.8 0.1 broadcast_in_dim.26
  34.9 19.2 %all_to_all.26 = f32[16,8,2048]{2,1,0:T(8,128)S(1)} all-to-all(f32[16,8,2048]{2,1,0:T(8,128)S(1)} %broadcast_in_dim.26), channel_id=1, replica_groups=mesh['region'=8,'unit'=16] {'unit'}, dimensions={0} | all-to-all | bytes 2097152 | tf_op jit(solution)/shard_map/all_to_all | solution.py:36
  54.2 2.4 %convolution_add_fusion.1 = f32[256,2048]{1,0:T(8,128)} fusion(f32[256,2048]{1,0:T(8,128)S(1)} %fusion.3, f32[16,8,2048]{2,1,0:T(8,128)S(1)} %all_to_all.26, s32[256]{0:T(256)S(1)} %get-tuple-element.7), kind=kOutput, calls=%fused_computation.9 | convolution fusion | flops 805863424 | bytes 5243904 | tf_op jit(solution)/shard_map/dot_general | solution.py:114
  56.5 11.8 %fusion.4 = f32[256,2048]{1,0:T(8,128)S(1)} fusion(f32[256,2048]{1,0:T(8,128)} %convolution_add_fusion.1, bf16[2048,2048]{1,0:T(8,128)(2,1)} %param.6, bf16[256,2048]{1,0:T(8,128)(2,1)} %param.5), kind=kOutput, calls=%fused_computation.11 | convolution fusion | flops 4298113024 | bytes 13631488 | tf_op jit(solution)/shard_map/dot_general | solution.py:64
  68.3 0.9 convolution_bitcast_fusion
  69.2 18.0 %all_to_all.27 = f32[16,8,2048]{2,1,0:T(8,128)S(1)} all-to-all(f32[16,8,2048]{2,1,0:T(8,128)S(1)} %convolution_bitcast_fusion), channel_id=1, replica_groups=mesh['region'=8,'unit'=16] {'unit'}, dimensions={0} | all-to-all | bytes 2097152 | tf_op jit(solution)/shard_map/all_to_all | solution.py:30
  87.3 0.0 copy-start.2
  87.3 0.1 reduce_sum.49
  87.3 0.1 subtract_divide_fusion
  87.4 1.1 broadcast_in_dim.27
  88.5 3.8 %all-to-all-start.3 = ((f32[16,8,2048]{2,1,0:T(8,128)}), f32[16,8,2048]{2,1,0:T(8,128)S(1)}, u32[]{:S(2)}, u32[]{:S(2)}) async-start(f32[16,8,2048]{2,1,0:T(8,128)} %broadcast_in_dim.27), calls=%async_computation.3 | async-start | bytes 2097152 | tf_op jit(solution)/shard_map/all_to_all | solution.py:36
  92.3 0.0 copy-done.2
  92.3 0.1 copy.10
  92.4 0.2 fusion.28
  92.7 0.2 fusion.30
  93.0 0.5 slice.38
  93.5 4.1 %scatter_custom_fusion = f32[512,2048]{1,0:T(8,128)} fusion(s32[256]{0:T(256)S(1)} %bitcast.51, f32[256,2048]{1,0:T(8,128)S(1)} %fusion.4, f32[]{:T(128)} %constant.48.clone.1), kind=kCustom, calls=%fused_computation.17 | custom fusion | bytes 4194308 | tf_op jit(solution)/shard_map/scatter | solution.py:109
  97.5 4.9 %reshape.66 = f32[128,8,1024]{2,1,0:T(8,128)} reshape(f32[512,2048]{1,0:T(8,128)} %scatter_custom_fusion) | data formatting | bytes 8388608 | tf_op jit(solution)/shard_map/reshape | solution.py:110
  102.5 0.1 select_reduce_fusion
  102.6 0.1 broadcast_in_dim.53
  102.8 0.2 eq.82
  103.6 2.0 %all-to-all-done.3 = f32[16,8,2048]{2,1,0:T(8,128)S(1)} async-done(((f32[16,8,2048]{2,1,0:T(8,128)}), f32[16,8,2048]{2,1,0:T(8,128)S(1)}, u32[]{:S(2)}, u32[]{:S(2)}) %all-to-all-start.3) | async-done | bytes 1048608 | tf_op jit(solution)/shard_map/all_to_all | solution.py:36
  105.7 0.0 copy-start
  105.7 0.3 fusion.21
  106.1 1.7 copy-done
  107.9 4.0 %bitcast_add_fusion = f32[128,8,1024]{2,1,0:T(8,128)} fusion(f32[128,8,1024]{2,1,0:T(8,128)S(1)} %copy-done, bf16[768,1024]{1,0:T(8,128)(2,1)S(1)} %slice_dynamic-update-slice_fusion, s32[1024]{0:T(1024)S(1)} %eq.82, s32[768]{0:T(1024)S(1)} %get-tuple-element.11, s32[768]{0:T(1024)S(1)} %get-tuple-element.17, s32[1024]{0:T(1024)S(1)} %get-tuple-element.13, ...), kind=kOutput, calls=%fused_computation.1 | convolution fusion | flops 1616379904 | bytes 9988608 | tf_op jit(solution)/shard_map/dot_general | solution.py:124
  111.9 7.8 %all-to-all-start.4 = ((f32[128,8,1024]{2,1,0:T(8,128)}), f32[128,8,1024]{2,1,0:T(8,128)}, u32[]{:S(2)}, u32[]{:S(2)}) async-start(f32[128,8,1024]{2,1,0:T(8,128)} %bitcast_add_fusion), calls=%async_computation.4 | async-start | bytes 8388608 | tf_op jit(solution)/shard_map/all_to_all | solution.py:129
  119.7 1.1 fusion.6
  120.8 6.7 %convolution_convert_fusion = bf16[256,2048]{1,0:T(8,128)(2,1)} fusion(bf16[256,2048]{1,0:T(8,128)(2,1)S(1)} %fusion.6, bf16[2048,2048]{1,0:T(8,128)(2,1)} %param.6), kind=kOutput, calls=%fused_computation.15 | convolution fusion | flops 2148007936 | bytes 10485760 | tf_op jit(solution)/shard_map/dot_general | solution.py:126
  127.5 45.4 %all-to-all-done.4 = f32[128,8,1024]{2,1,0:T(8,128)} async-done(((f32[128,8,1024]{2,1,0:T(8,128)}), f32[128,8,1024]{2,1,0:T(8,128)}, u32[]{:S(2)}, u32[]{:S(2)}) %all-to-all-start.4) | async-done | bytes 4194336 | tf_op jit(solution)/shard_map/all_to_all | solution.py:129
  172.9 5.2 %reshape.68 = f32[512,2048]{1,0:T(8,128)} reshape(f32[128,8,1024]{2,1,0:T(8,128)} %all-to-all-done.4) | data formatting | bytes 8388608 | tf_op jit(solution)/shard_map/reshape | solution.py:130
  (20 shorter events, 0.3 us)
Async XLA Ops:
  8.6 26.1 %copy-start.1 = (f32[8,2048]{1,0:T(8,128)S(1)}, f32[8,2048]{1,0:T(8,128)}, u32[]{:S(2)}) copy-start(f32[8,2048]{1,0:T(8,128)} %param.7) | copy-start | bytes 196612
  87.3 5.1 %copy-start.2 = (s32[256,1]{0,1:T(1,128)S(1)}, s32[256,1]{0,1:T(1,128)}, u32[]{:S(2)}) copy-start(s32[256,1]{0,1:T(1,128)} %param.9) | copy-start | bytes 3076
  88.5 17.2 %all-to-all-start.3 = ((f32[16,8,2048]{2,1,0:T(8,128)}), f32[16,8,2048]{2,1,0:T(8,128)S(1)}, u32[]{:S(2)}, u32[]{:S(2)}) async-start(f32[16,8,2048]{2,1,0:T(8,128)} %broadcast_in_dim.27), calls=%async_computation.3 | async-start | bytes 2097152 | tf_op jit(solution)/shard_map/all_to_all | solution.py:36
  105.7 2.2 %copy-start = (f32[128,8,1024]{2,1,0:T(8,128)S(1)}, f32[128,8,1024]{2,1,0:T(8,128)}, u32[]{:S(2)}) copy-start(f32[128,8,1024]{2,1,0:T(8,128)} %reshape.66) | copy-start | bytes 12582916
  111.9 61.1 %all-to-all-start.4 = ((f32[128,8,1024]{2,1,0:T(8,128)}), f32[128,8,1024]{2,1,0:T(8,128)}, u32[]{:S(2)}, u32[]{:S(2)}) async-start(f32[128,8,1024]{2,1,0:T(8,128)} %bitcast_add_fusion), calls=%async_computation.4 | async-start | bytes 8388608 | tf_op jit(solution)/shard_map/all_to_all | solution.py:129
